TPU v7x, 256 devices: a whole 4x4x8 slice. The times are simulated.
256 devices in a mesh: req: 128 (over z, y, x), tensor: 2 (over core).
Axes of the slice: x: 4, y: 4, z: 8, core: 2. Of those that a mesh axis runs over, the one named last changes fastest.
Arguments:
- patches: bfloat16 [256, 256, 1280], P('req'), may hold values from -6 to 6
- grids: int32 [256, 2], replicated, may hold values from 2 to 16, as said below
- place: int32 [256], replicated, may hold values from 0 to 255, as said below
- text_tokens: bfloat16 [128, 384, 1280], P('req'), may hold values from -6 to 6
- encoder_attend_in: bfloat16 [1280, 3, 1280], P(None, None, 'tensor'), may hold values from -0.15625 to 0.15625
- encoder_attend_out: bfloat16 [1280, 1280], P('tensor'), may hold values from -0.15625 to 0.15625
- encoder_expand: bfloat16 [1280, 5120], P(None, 'tensor'), may hold values from -0.15625 to 0.15625
- encoder_contract: bfloat16 [5120, 1280], P('tensor'), may hold values from -0.078125 to 0.078125
- encoder_gain_first: float32 [1280], replicated, may hold values from 0.25 to 1.75
- encoder_gain_second: float32 [1280], replicated, may hold values from 0.25 to 1.75
- merge_weight: bfloat16 [5120, 1280], P(None, 'tensor'), may hold values from -0.078125 to 0.078125
- decoder_attend_in: bfloat16 [1280, 3, 1280], P(None, None, 'tensor'), may hold values from -0.15625 to 0.15625
- decoder_attend_out: bfloat16 [1280, 1280], P('tensor'), may hold values from -0.15625 to 0.15625
- decoder_expand: bfloat16 [1280, 5120], P(None, 'tensor'), may hold values from -0.15625 to 0.15625
- decoder_contract: bfloat16 [5120, 1280], P('tensor'), may hold values from -0.078125 to 0.078125
- decoder_gain_first: float32 [1280], replicated, may hold values from 0.25 to 1.75
- decoder_gain_second: float32 [1280], replicated, may hold values from 0.25 to 1.75
Outputs:
- decoded: bfloat16 [128, 512, 1280], P('req')
Inputs may be any that keep to these rules, and one draw needn't show every extreme that they name: `grids`: both entries are even; image 0 always has the full 16 x 16 grid. A permutation: image i's merged tokens go to request place[i] // 2, image slot place[i] % 2. The request index, taken bitwise exclusive-or with i // 2, depends on i % 2 only: it is 1 when i % 2 = 0 and 64 when i % 2 = 1.
All inputs are finite; a program needn't handle non-finite values.
Results may differ from a plain program's by a relative error of at most 0.015.
Values may be sent and summed in bfloat16 or wider, within the bound.
No kernel may reach another device: no remote copies, remote signals or barrier semaphores. Data moves between devices by JAX's collectives and lax.ppermute only.
A program may use at most 192 MiB of HBM per device.

v0:
```python
import functools

import jax
import jax.numpy as jnp
from jax import lax
from jax.experimental import pallas as pl
from jax.experimental.pallas import tpu as pltpu
from jax.sharding import PartitionSpec as P

HEAD_DIM = 80
GRID = 16
REQ_XOR = (1, 64)


def normalize(values, gain):
    center = values - jnp.mean(values, axis=-1, keepdims=True)
    spread = jnp.mean(center * center, axis=-1, keepdims=True)
    return center * lax.rsqrt(spread + 1e-06) * gain


def tensor_sum(partial):
    mine = partial.astype(jnp.bfloat16)
    other = lax.ppermute(mine, "tensor", [(0, 1), (1, 0)])
    return mine.astype(jnp.float32) + other.astype(jnp.float32)


def _feed_forward_kernel(rows_per_step, x_ref, w1_ref, w2_ref, o_ref, acc_ref):
    k = pl.program_id(0)

    @pl.when(k == 0)
    def _():
        acc_ref[...] = jnp.zeros_like(acc_ref)

    w1 = w1_ref[...]
    w2 = w2_ref[...]
    for r in range(x_ref.shape[0] // rows_per_step):
        rows = pl.ds(r * rows_per_step, rows_per_step)
        h = jnp.dot(x_ref[rows, :], w1, preferred_element_type=jnp.float32)
        g = (h * 0.5 * (1.0 + lax.erf(h * (2.0 ** -0.5)))).astype(jnp.bfloat16)
        acc_ref[rows, :] += jnp.dot(g, w2, preferred_element_type=jnp.float32)

    @pl.when(k == pl.num_programs(0) - 1)
    def _():
        o_ref[...] = acc_ref[...].astype(o_ref.dtype)


def feed_forward(x, expand, contract, hidden_step=512, rows_per_step=128):
    length, width = x.shape
    hidden = expand.shape[1]
    return pl.pallas_call(
        functools.partial(_feed_forward_kernel, rows_per_step),
        out_shape=jax.ShapeDtypeStruct((length, width), jnp.bfloat16),
        grid=(hidden // hidden_step,),
        in_specs=[
            pl.BlockSpec((length, width), lambda k: (0, 0)),
            pl.BlockSpec((width, hidden_step), lambda k: (0, k)),
            pl.BlockSpec((hidden_step, width), lambda k: (k, 0)),
        ],
        out_specs=pl.BlockSpec((length, width), lambda k: (0, 0)),
        scratch_shapes=[pltpu.VMEM((length, width), jnp.float32)],
        cost_estimate=pl.CostEstimate(
            flops=4 * length * width * hidden,
            transcendentals=length * hidden,
            bytes_accessed=2 * (2 * width * hidden + 2 * length * width),
        ),
    )(x, expand, contract)


def attend(normed, allowed, attend_in, attend_out):
    batch, length, width = normed.shape
    projected = jnp.einsum(
        "bld,dkf->blkf", normed, attend_in, preferred_element_type=jnp.float32
    ).astype(jnp.bfloat16)
    projected = projected.reshape(batch, length, 3, -1, HEAD_DIM)
    queries = projected[:, :, 0]
    key_rows = projected[:, :, 1]
    value_rows = projected[:, :, 2]
    scores = jnp.einsum(
        "bqhd,bkhd->bhqk", queries, key_rows, preferred_element_type=jnp.float32
    ) * HEAD_DIM ** (-0.5)
    scores = jnp.where(allowed[:, None], scores, jnp.float32(-1e30))
    probs = jax.nn.softmax(scores, axis=-1).astype(jnp.bfloat16)
    mixed = jnp.einsum(
        "bhqk,bkhd->bqhd", probs, value_rows, preferred_element_type=jnp.float32
    ).astype(jnp.bfloat16)
    return jnp.dot(mixed.reshape(batch, length, -1), attend_out, preferred_element_type=jnp.float32)


def layer(inputs, allowed, attend_in, attend_out, expand, contract, gain_first, gain_second):
    widened = inputs.astype(jnp.float32)
    first = lax.optimization_barrier(normalize(widened, gain_first).astype(jnp.bfloat16))
    attended = attend(first, allowed, attend_in, attend_out)
    residual = widened + tensor_sum(attended)
    second = normalize(residual, gain_second).astype(jnp.bfloat16)
    batch, length, width = second.shape
    partial_out = feed_forward(second.reshape(batch * length, width), expand, contract)
    return (residual + tensor_sum(partial_out.reshape(batch, length, width))).astype(jnp.bfloat16)


def on_device(
    req_count,
    patches,
    grids,
    place,
    text_tokens,
    encoder_attend_in,
    encoder_attend_out,
    encoder_expand,
    encoder_contract,
    encoder_gain_first,
    encoder_gain_second,
    merge_weight,
    decoder_attend_in,
    decoder_attend_out,
    decoder_expand,
    decoder_contract,
    decoder_gain_first,
    decoder_gain_second,
):
    device = lax.axis_index("req")
    core = lax.axis_index("tensor")
    images_here, cell_count, width = patches.shape
    side = GRID
    half = side // 2
    slot_count = half * half
    local_grids = lax.dynamic_slice_in_dim(grids, device * images_here, images_here, 0)
    cells = jnp.arange(cell_count)
    cell_valid = ((cells // side)[None, :] < local_grids[:, 0:1]) & (
        (cells % side)[None, :] < local_grids[:, 1:2]
    )
    image_allowed = jnp.broadcast_to(cell_valid[:, None, :], (images_here, cell_count, cell_count))
    encoded = layer(
        patches,
        image_allowed,
        encoder_attend_in,
        encoder_attend_out,
        encoder_expand,
        encoder_contract,
        encoder_gain_first,
        encoder_gain_second,
    )
    blocks = (
        encoded.reshape(images_here, half, 2, half, 2, width)
        .transpose(0, 1, 3, 2, 4, 5)
        .reshape(images_here * slot_count, 4 * width)
    )
    merged = jnp.dot(blocks, merge_weight, preferred_element_type=jnp.float32).astype(jnp.bfloat16)
    merged = merged.reshape(images_here, slot_count, -1)

    arrived = []
    for j in range(images_here):
        halves = []
        for flip in (0, 1):
            perm = [
                (r * 2 + t, (r ^ REQ_XOR[j]) * 2 + (t ^ flip))
                for r in range(req_count)
                for t in range(2)
            ]
            halves.append(lax.ppermute(merged[j], ("req", "tensor"), perm))
        same, other = halves
        low = jnp.where(core == 0, same, other)
        high = jnp.where(core == 0, other, same)
        arrived.append(jnp.concatenate([low, high], axis=-1))
    sources = [(device ^ REQ_XOR[j]) * images_here + j for j in range(images_here)]
    first_slot = place[sources[0]] % 2
    swap = first_slot != 0
    image_rows = jnp.where(
        swap,
        jnp.concatenate([arrived[1], arrived[0]], axis=0),
        jnp.concatenate([arrived[0], arrived[1]], axis=0),
    )
    grid_a = grids[sources[0]]
    grid_b = grids[sources[1]]
    slot_grids = jnp.where(swap, jnp.stack([grid_b, grid_a]), jnp.stack([grid_a, grid_b]))
    slots = jnp.arange(slot_count)
    merged_valid = ((2 * (slots // half))[None, :] < slot_grids[:, 0:1]) & (
        (2 * (slots % half))[None, :] < slot_grids[:, 1:2]
    )
    prompt = jnp.concatenate([image_rows, text_tokens[0]], axis=0)[None]
    text_count = text_tokens.shape[1]
    prompt_valid = jnp.concatenate(
        [merged_valid.reshape(-1), jnp.ones((text_count,), bool)], axis=0
    )
    length = prompt.shape[1]
    positions = jnp.arange(length)
    prompt_allowed = (prompt_valid[None, :] & (positions[None, :] <= positions[:, None]))[None]
    decoded = layer(
        prompt,
        prompt_allowed,
        decoder_attend_in,
        decoder_attend_out,
        decoder_expand,
        decoder_contract,
        decoder_gain_first,
        decoder_gain_second,
    )
    return jnp.where(prompt_valid[None, :, None], decoded, jnp.zeros_like(decoded))


def solution(mesh):
    placed = (
        P("req", None, None),
        P(),
        P(),
        P("req", None, None),
        P(None, None, "tensor"),
        P("tensor", None),
        P(None, "tensor"),
        P("tensor", None),
        P(),
        P(),
        P(None, "tensor"),
        P(None, None, "tensor"),
        P("tensor", None),
        P(None, "tensor"),
        P("tensor", None),
        P(),
        P(),
    )

    def body(*args):
        return on_device(mesh.shape["req"], *args)

    return jax.shard_map(
        body, mesh=mesh, in_specs=placed, out_specs=P("req", None, None), check_vma=False
    )
```

profile of v0, /device:TPU:1, one launch (start us, length us, event | category | flops | bytes accessed | tf_op | source)
XLA Modules:
  0.0 128.7 jit_solution(13694647071360350360)
XLA Ops:
  0.0 0.0 copy-start
  0.0 0.9 constant_dynamic-slice_fusion
  0.9 1.6 %convert_reduce_fusion.1 = f32[2,256]{1,0:T(2,128)S(1)} fusion(bf16[2,256,1280]{2,1,0:T(8,128)(2,1)} %param.17), kind=kLoop, calls=%fused_computation.20 | loop fusion | flops 1310208 | bytes 1312768 | tf_op jit(solution)/shard_map/reduce_sum | solution.py:16
  2.5 1.8 %fusion.18 = f32[2,256]{1,0:T(2,128)S(1)} fusion(bf16[2,256,1280]{2,1,0:T(8,128)(2,1)} %param.17, f32[2,256]{1,0:T(2,128)S(1)} %broadcast_multiply_fusion.3), kind=kLoop, calls=%fused_computation.32 | loop fusion | flops 2620928 | bytes 1314816 | tf_op jit(solution)/shard_map/reduce_sum | solution.py:17
  4.3 0.0 copy-done.2
  4.3 0.0 copy-done.9
  4.3 0.5 fusion.20
  4.8 6.5 %fusion.25 = bf16[2,256,3,640]{3,1,2,0:T(8,128)(2,1)} fusion(bf16[1280,3,640]{2,0,1:T(8,128)(2,1)} %param.21, bf16[2,256,1280]{2,1,0:T(8,128)(2,1)S(1)} %fusion.20), kind=kOutput, calls=%fused_computation.45 | convolution fusion | flops 2517565440 | bytes 8192000 | tf_op jit(solution)/shard_map/bld,dkf->blkf/dot_general | solution.py:71
  11.3 4.0 %copy.40 = bf16[2,256,3,640]{1,3,0,2:T(8,128)(2,1)} copy(bf16[2,256,3,640]{3,1,2,0:T(8,128)(2,1)} %fusion.25) | data formatting | bytes 3932160 | tf_op jit(solution)/shard_map/reshape | solution.py:74
  15.3 2.0 %fusion.38 = f32[2,8,256,256]{2,3,1,0:T(8,128)S(1)} fusion(bf16[2,256,3,8,80]{1,4,3,0,2:T(8,128)(2,1)} %bitcast.92), kind=kOutput, calls=%fused_computation.64 | convolution fusion | flops 167772160 | bytes 5505024 | tf_op jit(solution)/shard_map/bqhd,bkhd->bhqk/dot_general | solution.py:78
  17.3 0.1 compare_and_fusion
  17.4 1.5 %fusion.52 = (f32[2,8,256]{2,1,0:T(8,128)S(1)}, f32[2,8,256,256]{2,3,1,0:T(8,128)S(1)}) fusion(f32[2,8,256,256]{2,3,1,0:T(8,128)S(1)} %fusion.38, pred[2,256]{1,0:T(4,128)(4,1)S(1)} %compare_and_fusion), kind=kOutput, calls=%fused_computation.113 | output fusion | flops 6291711 | bytes 8405504 | tf_op jit(solution)/shard_map/sub | solution.py:82
  18.9 1.6 %fusion.29 = bf16[2,8,80,256]{3,2,1,0:T(8,128)(2,1)S(1)} fusion(f32[2,8,256,256]{2,3,1,0:T(8,128)S(1)} %get-tuple-element.18, f32[2,8,256]{2,1,0:T(8,128)S(1)} %get-tuple-element.17, bf16[2,256,3,8,80]{1,4,3,0,2:T(8,128)(2,1)} %bitcast.93), kind=kOutput, calls=%fused_computation.48 | convolution fusion | flops 170196992 | bytes 5521408 | tf_op jit(solution)/shard_map/bhqk,bkhd->bqhd/dot_general | solution.py:83
  20.5 0.0 copy-done
  20.5 1.2 convolution_convert_fusion.1
  21.8 3.3 %collective-permute-start = (bf16[2,256,1280]{2,1,0:T(8,128)(2,1)S(1)}, bf16[2,256,1280]{2,1,0:T(8,128)(2,1)S(1)}, u32[]{:S(2)}, u32[]{:S(2)}) collective-permute-start(bf16[2,256,1280]{2,1,0:T(8,128)(2,1)S(1)} %convolution_convert_fusion.1), channel_id=1, source_target_pairs={{0,1},{1,0},{2,3},{3,2},{4,5},{5,4},{6,7},{7,6},{8,9},{9,8},{10,11... | collective-permute-start | bytes 3932168 | tf_op jit(solution)/shard_map/ppermute | solution.py:23
  25.1 2.7 %collective-permute-done = bf16[2,256,1280]{2,1,0:T(8,128)(2,1)S(1)} collective-permute-done((bf16[2,256,1280]{2,1,0:T(8,128)(2,1)S(1)}, bf16[2,256,1280]{2,1,0:T(8,128)(2,1)S(1)}, u32[]{:S(2)}, u32[]{:S(2)}) %collective-permute-start) | collective-permute-done | bytes 1310752 | tf_op jit(solution)/shard_map/ppermute | solution.py:23
  27.8 0.6 fusion.49
  28.4 0.8 multiply_reduce_fusion.1
  29.2 1.8 %multiply_convert_fusion.1 = bf16[2,256,1280]{2,1,0:T(8,128)(2,1)} fusion(f32[1280]{0:T(1024)S(1)} %copy-done.10, f32[2,256]{1,0:T(2,128)S(1)} %add_rsqrt_fusion.2, f32[2,256]{1,0:T(2,128)S(1)} %broadcast_multiply_fusion.2, bf16[2,256,1280]{2,1,0:T(8,128)(2,1)S(1)} %collective-permute-done, bf16[2,256,1280]{2,1,0:T(8,128)(2,1)S(1)} %convolution_convert_fusion.1, ...), kind=kLoop, calls=%fused_computation.39 | loop fusion | flops 5898240 | bytes 5252096 | tf_op jit(solution)/shard_map/convert_element_type | solution.py:94
  31.0 14.0 %shard_map.163 = bf16[512,1280]{1,0:T(8,128)(2,1)} custom-call(bf16[512,1280]{1,0:T(8,128)(2,1)} %bitcast.98, bf16[1280,2560]{1,0:T(8,128)(2,1)} %w1_ref.2, bf16[2560,1280]{1,0:T(8,128)(2,1)} %w2_ref.2), custom_call_target="tpu_custom_call" | custom-call | flops 6710886400 | bytes 15728640 | tf_op jit(solution)/shard_map/pallas_call | solution.py:50
  45.0 0.4 collective-permute-start.1
  45.4 0.6 dynamic_slice.12
  48.0 0.0 copy-done.13
  48.0 0.1 constant_dynamic-slice_fusion.2
  48.1 0.1 add_select_fusion
  48.1 0.1 compare_and_fusion.1
  48.2 0.1 and.83
  48.3 0.1 collective-permute-done.1
  48.4 4.0 %add_convert_fusion.1 = bf16[2,256,1280]{2,1,0:T(8,128)(2,1)} fusion(bf16[2,256,1280]{2,1,0:T(8,128)(2,1)} %collective-permute-done.1, bf16[2,256,1280]{2,1,0:T(8,128)(2,1)} %bitcast.100, bf16[2,256,1280]{2,1,0:T(8,128)(2,1)} %copy-done.8, bf16[2,256,1280]{2,1,0:T(8,128)(2,1)S(1)} %copy-done.7, bf16[2,256,1280]{2,1,0:T(8,128)(2,1)S(1)} %copy-done.2), kind=kLoop, calls=%fused_computation.38 | loop fusion | flops 6553600 | bytes 7864320 | tf_op jit(solution)/shard_map/convert_element_type | solution.py:97
  52.4 3.1 %reshape.429 = bf16[2,8,2,8,2,1280]{5,4,3,2,1,0:T(2,128)(2,1)S(1)} reshape(bf16[2,256,1280]{2,1,0:T(8,128)(2,1)} %add_convert_fusion.1) | data formatting | bytes 2621440 | tf_op jit(solution)/shard_map/reshape | solution.py:143
  55.5 1.0 copy.44
  56.4 1.0 reshape.430
  57.5 0.0 copy-start.3
  57.5 4.1 %convolution_convert_fusion.3 = bf16[128,640]{1,0:T(8,128)(2,1)S(1)} fusion(bf16[128,5120]{1,0:T(8,128)(2,1)S(1)} %reshape.430, bf16[5120,640]{1,0:T(8,128)(2,1)} %param.27), kind=kOutput, calls=%fused_computation.56 | convolution fusion | flops 838942720 | bytes 8028160 | tf_op jit(solution)/shard_map/dot_general | solution.py:147
  61.6 0.0 copy-start.11
  61.7 5.5 %collective-permute-start.3 = (bf16[64,640]{1,0:T(8,128)(2,1)S(1)}, bf16[64,640]{1,0:T(8,128)(2,1)S(1)}, u32[]{:S(2)}, u32[]{:S(2)}) collective-permute-start(bf16[64,640]{1,0:T(8,128)(2,1)S(1)} %get-tuple-element.7), channel_id=1, source_target_pairs={{0,129},{1,128},{2,131},{3,130},{4,133},{5,132},{6,135},{7,134},{8... | collective-permute-start | bytes 245768 | tf_op jit(solution)/shard_map/ppermute | solution.py:159
  67.2 0.2 collective-permute-start.2
  67.4 0.1 fusion.35
  67.5 1.5 %collective-permute-start.5 = (bf16[64,640]{1,0:T(8,128)(2,1)S(1)}, bf16[64,640]{1,0:T(8,128)(2,1)S(1)}, u32[]{:S(2)}, u32[]{:S(2)}) collective-permute-start(bf16[64,640]{1,0:T(8,128)(2,1)S(1)} %get-tuple-element.8), channel_id=1, source_target_pairs={{0,3},{1,2},{2,1},{3,0},{4,7},{5,6},{6,5},{7,4},{8,11},{9,10},{10,... | collective-permute-start | bytes 245768 | tf_op jit(solution)/shard_map/ppermute | solution.py:159
  69.0 0.4 collective-permute-start.4
  69.4 0.8 collective-permute-done.3
  70.2 4.8 %collective-permute-done.2 = bf16[64,640]{1,0:T(8,128)(2,1)S(1)} collective-permute-done((bf16[64,640]{1,0:T(8,128)(2,1)S(1)}, bf16[64,640]{1,0:T(8,128)(2,1)S(1)}, u32[]{:S(2)}, u32[]{:S(2)}) %collective-permute-start.2) | collective-permute-done | bytes 81952 | tf_op jit(solution)/shard_map/ppermute | solution.py:159
  75.0 0.0 collective-permute-done.5
  75.0 0.0 collective-permute-done.4
  75.0 0.1 fusion.40
  75.1 0.2 convert_reduce_fusion
  75.3 0.5 fusion.15
  75.8 0.5 fusion.17
  76.3 6.4 %convolution_convert_fusion.2 = bf16[512,3,640]{2,0,1:T(8,128)(2,1)} fusion(bf16[1280,3,640]{2,0,1:T(8,128)(2,1)} %param.28, bf16[1,512,1280]{2,1,0:T(8,128)(2,1)S(1)} %fusion.17), kind=kOutput, calls=%fused_computation.46 | convolution fusion | flops 2517565440 | bytes 8192000 | tf_op jit(solution)/shard_map/bld,dkf->blkf/dot_general | solution.py:71
  82.7 4.0 %copy.34 = bf16[512,3,640]{0,2,1:T(8,128)(2,1)} copy(bf16[512,3,640]{2,0,1:T(8,128)(2,1)} %convolution_convert_fusion.2) | data formatting | bytes 3932160 | tf_op jit(solution)/shard_map/convert_element_type | solution.py:73
  86.7 7.7 %fusion.53 = (f32[8,512]{1,0:T(8,128)S(1)}, f32[8,512,512]{1,2,0:T(8,128)}) fusion(pred[512,512]{0,1:T(8,128)(4,1)S(1)} %fusion.35, bf16[1,512,3,8,80]{1,4,3,2,0:T(8,128)(2,1)} %bitcast.95), kind=kOutput, calls=%fused_computation.114 | convolution fusion | flops 343933440 | bytes 9977856 | tf_op jit(solution)/shard_map/sub | solution.py:82
  94.4 4.6 %fusion.30 = bf16[8,80,512]{2,1,0:T(8,128)(2,1)S(1)} fusion(f32[8,512,512]{1,2,0:T(8,128)} %get-tuple-element.20, f32[8,512]{1,0:T(8,128)S(1)} %get-tuple-element.19, bf16[1,512,3,8,80]{1,4,3,2,0:T(8,128)(2,1)} %bitcast.96), kind=kOutput, calls=%fused_computation.49 | convolution fusion | flops 340066304 | bytes 9715712 | tf_op jit(solution)/shard_map/bhqk,bkhd->bqhd/dot_general | solution.py:83
  99.0 1.2 fusion.14
  100.2 1.2 collective-permute-start.6
  101.4 2.7 %collective-permute-done.6 = bf16[1,512,1280]{2,1,0:T(8,128)(2,1)S(1)} collective-permute-done((bf16[1,512,1280]{2,1,0:T(8,128)(2,1)S(1)}, bf16[1,512,1280]{2,1,0:T(8,128)(2,1)S(1)}, u32[]{:S(2)}, u32[]{:S(2)}) %collective-permute-start.6) | collective-permute-done | bytes 1310752 | tf_op jit(solution)/shard_map/ppermute | solution.py:23
  104.0 0.6 fusion.50
  104.7 0.8 multiply_reduce_fusion
  105.4 0.0 copy-done.4
  105.5 1.8 %fusion.31.x_ref = bf16[512,1280]{1,0:T(8,128)(2,1)} fusion(f32[1280]{0:T(1024)S(1)} %copy-done.12, f32[512]{0:T(512)S(1)} %add_rsqrt_fusion, f32[512]{0:T(512)S(1)} %broadcast_multiply_fusion, bf16[1,512,1280]{2,1,0:T(8,128)(2,1)S(1)} %collective-permute-done.6, bf16[1,512,1280]{2,1,0:T(8,128)(2,1)S(1)} %fusion.14, bf16[1,384,1280]{2,1,0:T(8,128)(2,1)S(1)} %copy-done.3, ...), kind=kLoop, calls=%fused_computation.50 | loop fusion | flops 7864320 | bytes 5252096 | tf_op jit(solution)/shard_map/reshape | solution.py:96
  107.3 14.0 %shard_map.164 = bf16[512,1280]{1,0:T(8,128)(2,1)} custom-call(bf16[512,1280]{1,0:T(8,128)(2,1)} %fusion.31.x_ref, bf16[1280,2560]{1,0:T(8,128)(2,1)} %w1_ref.3, bf16[2560,1280]{1,0:T(8,128)(2,1)} %w2_ref.3), custom_call_target="tpu_custom_call" | custom-call | flops 6710886400 | bytes 15728640 | tf_op jit(solution)/shard_map/pallas_call | solution.py:50
  121.3 0.3 collective-permute-start.7
  121.6 2.9 %collective-permute-done.7 = bf16[1,512,1280]{2,1,0:T(8,128)(2,1)S(1)} collective-permute-done((bf16[1,512,1280]{2,1,0:T(8,128)(2,1)}, bf16[1,512,1280]{2,1,0:T(8,128)(2,1)S(1)}, u32[]{:S(2)}, u32[]{:S(2)}) %collective-permute-start.7) | collective-permute-done | bytes 1310752 | tf_op jit(solution)/shard_map/ppermute | solution.py:23
  124.5 4.2 %fusion.32 = bf16[1,512,1280]{2,1,0:T(8,128)(2,1)} fusion(bf16[1,512,1280]{2,1,0:T(8,128)(2,1)S(1)} %collective-permute-done.7, pred[512]{0:T(512)(128)(4,1)S(1)} %concatenate.47, bf16[512,1280]{1,0:T(8,128)(2,1)} %shard_map.164, bf16[1,512,1280]{2,1,0:T(8,128)(2,1)} %copy-done.5, bf16[1,512,1280]{2,1,0:T(8,128)(2,1)} %copy-done.4, ...), kind=kLoop, calls=%fused_computation.51 | loop fusion | flops 9175040 | bytes 7864832 | tf_op jit(solution)/shard_map/jit(_where)/select_n | solution.py:197
  (40 shorter events, 0.2 us)
Async XLA Ops:
  0.0 20.5 %copy-start = (bf16[640,1280]{1,0:T(8,128)(2,1)S(1)}, bf16[640,1280]{1,0:T(8,128)(2,1)}, u32[]{:S(2)}) copy-start(bf16[640,1280]{1,0:T(8,128)(2,1)} %param.22) | copy-start | bytes 4915204
  0.0 4.3 %copy-start.2 = (bf16[2,256,1280]{2,1,0:T(8,128)(2,1)S(1)}, bf16[2,256,1280]{2,1,0:T(8,128)(2,1)}, u32[]{:S(2)}) copy-start(bf16[2,256,1280]{2,1,0:T(8,128)(2,1)} %param.17) | copy-start | bytes 3932164
  0.0 4.3 %copy-start.9 = (f32[1280]{0:T(1024)S(1)}, f32[1280]{0:T(1024)}, u32[]{:S(2)}) copy-start(f32[1280]{0:T(1024)} %param.25) | copy-start | bytes 15364
  21.8 7.4 %copy-start.6 = (bf16[2,256,1280]{2,1,0:T(8,128)(2,1)}, bf16[2,256,1280]{2,1,0:T(8,128)(2,1)S(1)}, u32[]{:S(2)}) copy-start(bf16[2,256,1280]{2,1,0:T(8,128)(2,1)S(1)} %convolution_convert_fusion.1) | copy-start | bytes 3932164
  21.8 6.0 %collective-permute-start = (bf16[2,256,1280]{2,1,0:T(8,128)(2,1)S(1)}, bf16[2,256,1280]{2,1,0:T(8,128)(2,1)S(1)}, u32[]{:S(2)}, u32[]{:S(2)}) collective-permute-start(bf16[2,256,1280]{2,1,0:T(8,128)(2,1)S(1)} %convolution_convert_fusion.1), channel_id=1, source_target_pairs={{0,1},{1,0},{2,3},{3,2},{4,5},{5,4},{6,7},{7,6},{8,9},{9,8},{10,11... | collective-permute-start | bytes 3932168 | tf_op jit(solution)/shard_map/ppermute | solution.py:23
  27.8 1.4 %copy-start.8 = (bf16[2,256,1280]{2,1,0:T(8,128)(2,1)}, bf16[2,256,1280]{2,1,0:T(8,128)(2,1)S(1)}, u32[]{:S(2)}) copy-start(bf16[2,256,1280]{2,1,0:T(8,128)(2,1)S(1)} %collective-permute-done) | copy-start | bytes 3932164
  28.4 0.8 copy-start.10
  31.0 14.4 %copy-start.15 = (s32[256]{0:T(256)S(1)}, s32[256]{0:T(256)}, u32[]{:S(2)}) copy-start(s32[256]{0:T(256)} %param.19) | copy-start | bytes 3076
  31.0 17.0 %copy-start.13 = (s32[256,2]{0,1:T(2,128)S(1)}, s32[256,2]{0,1:T(2,128)}, u32[]{:S(2)}) copy-start(s32[256,2]{0,1:T(2,128)} %param.18) | copy-start | bytes 6148
  31.0 17.4 %copy-start.7 = (bf16[2,256,1280]{2,1,0:T(8,128)(2,1)S(1)}, bf16[2,256,1280]{2,1,0:T(8,128)(2,1)}, u32[]{:S(2)}) copy-start(bf16[2,256,1280]{2,1,0:T(8,128)(2,1)} %copy-done.6) | copy-start | bytes 3932164
  45.0 3.4 %collective-permute-start.1 = (bf16[2,256,1280]{2,1,0:T(8,128)(2,1)}, bf16[2,256,1280]{2,1,0:T(8,128)(2,1)}, u32[]{:S(2)}, u32[]{:S(2)}) collective-permute-start(bf16[2,256,1280]{2,1,0:T(8,128)(2,1)} %bitcast.99), channel_id=1, source_target_pairs={{0,1},{1,0},{2,3},{3,2},{4,5},{5,4},{6,7},{7,6},{8,9},{9,8},{10,11... | collective-permute-start | bytes 3932168 | tf_op jit(solution)/shard_map/ppermute | solution.py:23
  57.5 17.6 %copy-start.3 = (bf16[1,384,1280]{2,1,0:T(8,128)(2,1)S(1)}, bf16[1,384,1280]{2,1,0:T(8,128)(2,1)}, u32[]{:S(2)}) copy-start(bf16[1,384,1280]{2,1,0:T(8,128)(2,1)} %param.20) | copy-start | bytes 2949124
  61.6 14.2 %copy-start.11 = (f32[1280]{0:T(1024)S(1)}, f32[1280]{0:T(1024)}, u32[]{:S(2)}) copy-start(f32[1280]{0:T(1024)} %param.32) | copy-start | bytes 15364
  61.7 8.5 %collective-permute-start.3 = (bf16[64,640]{1,0:T(8,128)(2,1)S(1)}, bf16[64,640]{1,0:T(8,128)(2,1)S(1)}, u32[]{:S(2)}, u32[]{:S(2)}) collective-permute-start(bf16[64,640]{1,0:T(8,128)(2,1)S(1)} %get-tuple-element.7), channel_id=1, source_target_pairs={{0,129},{1,128},{2,131},{3,130},{4,133},{5,132},{6,135},{7,134},{8... | collective-permute-start | bytes 245768 | tf_op jit(solution)/shard_map/ppermute | solution.py:159
  67.2 7.8 %collective-permute-start.2 = (bf16[64,640]{1,0:T(8,128)(2,1)S(1)}, bf16[64,640]{1,0:T(8,128)(2,1)S(1)}, u32[]{:S(2)}, u32[]{:S(2)}) collective-permute-start(bf16[64,640]{1,0:T(8,128)(2,1)S(1)} %get-tuple-element.7), channel_id=1, source_target_pairs={{0,128},{1,129},{2,130},{3,131},{4,132},{5,133},{6,134},{7,135},{8... | collective-permute-start | bytes 245768 | tf_op jit(solution)/shard_map/ppermute | solution.py:159
  67.5 7.5 %collective-permute-start.5 = (bf16[64,640]{1,0:T(8,128)(2,1)S(1)}, bf16[64,640]{1,0:T(8,128)(2,1)S(1)}, u32[]{:S(2)}, u32[]{:S(2)}) collective-permute-start(bf16[64,640]{1,0:T(8,128)(2,1)S(1)} %get-tuple-element.8), channel_id=1, source_target_pairs={{0,3},{1,2},{2,1},{3,0},{4,7},{5,6},{6,5},{7,4},{8,11},{9,10},{10,... | collective-permute-start | bytes 245768 | tf_op jit(solution)/shard_map/ppermute | solution.py:159
  69.0 6.0 %collective-permute-start.4 = (bf16[64,640]{1,0:T(8,128)(2,1)S(1)}, bf16[64,640]{1,0:T(8,128)(2,1)S(1)}, u32[]{:S(2)}, u32[]{:S(2)}) collective-permute-start(bf16[64,640]{1,0:T(8,128)(2,1)S(1)} %get-tuple-element.8), channel_id=1, source_target_pairs={{0,2},{1,3},{2,0},{3,1},{4,6},{5,7},{6,4},{7,5},{8,10},{9,11},{10,... | collective-permute-start | bytes 245768 | tf_op jit(solution)/shard_map/ppermute | solution.py:159
  94.4 4.6 %copy-start.14 = (bf16[640,1280]{1,0:T(8,128)(2,1)S(1)}, bf16[640,1280]{1,0:T(8,128)(2,1)}, u32[]{:S(2)}) copy-start(bf16[640,1280]{1,0:T(8,128)(2,1)} %param.29) | copy-start | bytes 4915204
  100.2 5.3 %copy-start.4 = (bf16[1,512,1280]{2,1,0:T(8,128)(2,1)}, bf16[1,512,1280]{2,1,0:T(8,128)(2,1)S(1)}, u32[]{:S(2)}) copy-start(bf16[1,512,1280]{2,1,0:T(8,128)(2,1)S(1)} %fusion.14) | copy-start | bytes 3932164
  100.2 3.8 %collective-permute-start.6 = (bf16[1,512,1280]{2,1,0:T(8,128)(2,1)S(1)}, bf16[1,512,1280]{2,1,0:T(8,128)(2,1)S(1)}, u32[]{:S(2)}, u32[]{:S(2)}) collective-permute-start(bf16[1,512,1280]{2,1,0:T(8,128)(2,1)S(1)} %fusion.14), channel_id=1, source_target_pairs={{0,1},{1,0},{2,3},{3,2},{4,5},{5,4},{6,7},{7,6},{8,9},{9,8},{10,11... | collective-permute-start | bytes 3932168 | tf_op jit(solution)/shard_map/ppermute | solution.py:23
  104.0 1.4 %copy-start.5 = (bf16[1,512,1280]{2,1,0:T(8,128)(2,1)}, bf16[1,512,1280]{2,1,0:T(8,128)(2,1)S(1)}, u32[]{:S(2)}) copy-start(bf16[1,512,1280]{2,1,0:T(8,128)(2,1)S(1)} %collective-permute-done.6) | copy-start | bytes 3932164
  104.6 0.8 copy-start.12
  121.3 7.5 %copy-start.1 = (bf16[640,1280]{1,0:T(8,128)(2,1)S(1)}, bf16[640,1280]{1,0:T(8,128)(2,1)}, u32[]{:S(2)}) copy-start(bf16[640,1280]{1,0:T(8,128)(2,1)} %param.22) | copy-start | bytes 4915204
  121.3 3.2 %collective-permute-start.7 = (bf16[1,512,1280]{2,1,0:T(8,128)(2,1)}, bf16[1,512,1280]{2,1,0:T(8,128)(2,1)S(1)}, u32[]{:S(2)}, u32[]{:S(2)}) collective-permute-start(bf16[1,512,1280]{2,1,0:T(8,128)(2,1)} %bitcast.97), channel_id=1, source_target_pairs={{0,1},{1,0},{2,3},{3,2},{4,5},{5,4},{6,7},{7,6},{8,9},{9,8},{10,11... | collective-permute-start | bytes 3932168 | tf_op jit(solution)/shard_map/ppermute | solution.py:23
where the time goes:
time: 130 us; the launch traced here: 129 us
  matrix products  35.4 us (27%)
  Pallas kernels  28 us (22%)
  other arithmetic  21.6 us (17%)
  local copies, waits for them, and re-layouts  14.8 us (11%)
  waiting for transfers between devices  13.9 us (11%)
  starting transfers between devices  12.8 us (10%)
  between operations  2.3 us (2%)
    pallas_call x2, Pallas kernels, feed_forward(): pl.pallas_call(functools.partial(_feed_forward_kernel, rows_per_step), ou...  28 us
    dot_general x2, matrix products, attend(): jnp.einsum('bld,dkf->blkf', normed, attend_in, preferred_element_type=jnp...  12.9 us
    ppermute x4, waiting for transfers between devices, tensor_sum(): other = lax.ppermute(mine, 'tensor', [(0, 1), (1, 0)])  8.33 us
    sub x1, matrix products, attend(): probs = jax.nn.softmax(scores, axis=-1).astype(jnp.bfloat16)  7.69 us
    ppermute x4, starting transfers between devices, on_device(): halves.append(lax.ppermute(merged[j], ('req', 'tensor'), perm))  7.6 us
    dot_general x2, matrix products, attend(): jnp.einsum('bhqk,bkhd->bqhd', probs, value_rows, preferred_element_type=j...  6.17 us
    ppermute x4, waiting for transfers between devices, on_device(): halves.append(lax.ppermute(merged[j], ('req', 'tensor'), perm))  5.54 us
    ppermute x4, starting transfers between devices, tensor_sum(): other = lax.ppermute(mine, 'tensor', [(0, 1), (1, 0)])  5.21 us
  transfers between devices with their start and end apart: 8, of which 6 were waited for; matrix products, arithmetic and copies ran while one was open for 1% of the time, Pallas kernels for 0%

commit v1 on v0

--- a/solution.py
+++ b/solution.py
@@ -66,6 +66,45 @@
     )(x, expand, contract)
 
 
+def _merge_kernel(res_ref, mine_ref, other_ref, w_ref, o_ref):
+    cells, width = res_ref.shape[1], res_ref.shape[2]
+    half = GRID // 2
+    slot = lax.broadcasted_iota(jnp.int32, (half * half, cells), 0)
+    cell = lax.broadcasted_iota(jnp.int32, (half * half, cells), 1)
+    for i in range(res_ref.shape[0]):
+        encoded = (
+            res_ref[i] + (mine_ref[i].astype(jnp.float32) + other_ref[i].astype(jnp.float32))
+        ).astype(jnp.bfloat16)
+        total = None
+        for a in range(2):
+            for b in range(2):
+                wanted = (2 * (slot // half) + a) * GRID + 2 * (slot % half) + b
+                pick = jnp.where(cell == wanted, 1.0, 0.0).astype(jnp.bfloat16)
+                rows = jnp.dot(pick, encoded, preferred_element_type=jnp.float32).astype(jnp.bfloat16)
+                part = jnp.dot(
+                    rows,
+                    w_ref[pl.ds((2 * a + b) * width, width), :],
+                    preferred_element_type=jnp.float32,
+                )
+                total = part if total is None else total + part
+        o_ref[i] = total.astype(o_ref.dtype)
+
+
+def merge(residual, mine, other, merge_weight):
+    images, cells, width = residual.shape
+    half = GRID // 2
+    out_width = merge_weight.shape[1]
+    return pl.pallas_call(
+        _merge_kernel,
+        out_shape=jax.ShapeDtypeStruct((images, half * half, out_width), jnp.bfloat16),
+        cost_estimate=pl.CostEstimate(
+            flops=2 * images * cells * width * (out_width + half * half),
+            transcendentals=0,
+            bytes_accessed=images * cells * width * 8 + merge_weight.size * 2,
+        ),
+    )(residual, mine, other, merge_weight)
+
+
 def attend(normed, allowed, attend_in, attend_out):
     batch, length, width = normed.shape
     projected = jnp.einsum(
@@ -86,7 +125,7 @@
     return jnp.dot(mixed.reshape(batch, length, -1), attend_out, preferred_element_type=jnp.float32)
 
 
-def layer(inputs, allowed, attend_in, attend_out, expand, contract, gain_first, gain_second):
+def layer(inputs, allowed, attend_in, attend_out, expand, contract, gain_first, gain_second, split=False):
     widened = inputs.astype(jnp.float32)
     first = lax.optimization_barrier(normalize(widened, gain_first).astype(jnp.bfloat16))
     attended = attend(first, allowed, attend_in, attend_out)
@@ -94,7 +133,11 @@
     second = normalize(residual, gain_second).astype(jnp.bfloat16)
     batch, length, width = second.shape
     partial_out = feed_forward(second.reshape(batch * length, width), expand, contract)
-    return (residual + tensor_sum(partial_out.reshape(batch, length, width))).astype(jnp.bfloat16)
+    mine = partial_out.reshape(batch, length, width)
+    other = lax.ppermute(mine, "tensor", [(0, 1), (1, 0)])
+    if split:
+        return residual, mine, other
+    return (residual + (mine.astype(jnp.float32) + other.astype(jnp.float32))).astype(jnp.bfloat16)
 
 
 def on_device(
@@ -129,7 +172,7 @@
         (cells % side)[None, :] < local_grids[:, 1:2]
     )
     image_allowed = jnp.broadcast_to(cell_valid[:, None, :], (images_here, cell_count, cell_count))
-    encoded = layer(
+    residual, mine, other = layer(
         patches,
         image_allowed,
         encoder_attend_in,
@@ -138,14 +181,9 @@
         encoder_contract,
         encoder_gain_first,
         encoder_gain_second,
-    )
-    blocks = (
-        encoded.reshape(images_here, half, 2, half, 2, width)
-        .transpose(0, 1, 3, 2, 4, 5)
-        .reshape(images_here * slot_count, 4 * width)
-    )
-    merged = jnp.dot(blocks, merge_weight, preferred_element_type=jnp.float32).astype(jnp.bfloat16)
-    merged = merged.reshape(images_here, slot_count, -1)
+        split=True,
+    )
+    merged = merge(residual, mine, other, merge_weight)
 
     arrived = []
     for j in range(images_here):

time: 130 us -> 126 us (0.969)
  Pallas kernels: 28 us -> 36.3 us
  other arithmetic: 21.6 us -> 16.9 us
  matrix products: 35.4 us -> 31.2 us
  local copies, waits for them, and re-layouts: 14.8 us -> 12 us
    pallas_call x0 -> x1, Pallas kernels: none -> 8.44 us  [merge(): pl.pallas_call(_merge_kernel, out_shape=jax.ShapeDtypeStruct((images, hal...]
    reshape x3 -> x0, local copies, waits for them, and re-layouts: 5.05 us -> none  [the longest x2 4.04 us: on_device(): encoded.reshape(images_here, half, 2, half, 2, width)]
    dot_general x1 -> x0, matrix products: 4.14 us -> none  [on_device(): jnp.dot(blocks, merge_weight, preferred_element_type=jnp.float32)]
    convert_element_type x1 -> x0, other arithmetic: 3.96 us -> none  [layer(): (residual + tensor_sum(partial_out.reshape(batch, length, width))).astype...]
    ppermute x4 -> x2, waiting for transfers between devices: 8.33 us -> 5.32 us  [tensor_sum(): other = lax.ppermute(mine, 'tensor', [(0, 1), (1, 0)])]
    ppermute x0 -> x2, waiting for transfers between devices: none -> 2.88 us  [layer(): other = lax.ppermute(mine, 'tensor', [(0, 1), (1, 0)])]
    unnamed x32 -> x30, local copies, waits for them, and re-layouts: 0.07 us -> 1.37 us
    ppermute x4 -> x2, starting transfers between devices: 5.21 us -> 4.5 us  [tensor_sum(): other = lax.ppermute(mine, 'tensor', [(0, 1), (1, 0)])]
  transfers between devices with their start and end apart: 8 -> 8, of which waited for: 6 -> 5; matrix products, arithmetic and copies ran while one was open for 1% -> 1% of each run, Pallas kernels for 0% -> 0%
where the time goes in v1:
time: 126 us; the launch traced here: 125 us
  Pallas kernels  36.3 us (29%)
  matrix products  31.2 us (25%)
  other arithmetic  16.9 us (13%)
  waiting for transfers between devices  13.7 us (11%)
  starting transfers between devices  12.9 us (10%)
  local copies, waits for them, and re-layouts  12 us (10%)
  between operations  2.24 us (2%)
    pallas_call x2, Pallas kernels, feed_forward(): pl.pallas_call(functools.partial(_feed_forward_kernel, rows_per_step), ou...  27.9 us
    dot_general x2, matrix products, attend(): jnp.einsum('bld,dkf->blkf', normed, attend_in, preferred_element_type=jnp...  12.9 us
    pallas_call x1, Pallas kernels, merge(): pl.pallas_call(_merge_kernel, out_shape=jax.ShapeDtypeStruct((images, hal...  8.44 us
    sub x1, matrix products, attend(): probs = jax.nn.softmax(scores, axis=-1).astype(jnp.bfloat16)  7.69 us
    ppermute x4, starting transfers between devices, on_device(): halves.append(lax.ppermute(merged[j], ('req', 'tensor'), perm))  7.57 us
    dot_general x2, matrix products, attend(): jnp.einsum('bhqk,bkhd->bqhd', probs, value_rows, preferred_element_type=j...  6.14 us
    ppermute x4, waiting for transfers between devices, on_device(): halves.append(lax.ppermute(merged[j], ('req', 'tensor'), perm))  5.48 us
    ppermute x2, waiting for transfers between devices, tensor_sum(): other = lax.ppermute(mine, 'tensor', [(0, 1), (1, 0)])  5.32 us
  transfers between devices with their start and end apart: 8, of which 5 were waited for; matrix products, arithmetic and copies ran while one was open for 1% of the time, Pallas kernels for 0%

profile of v1, /device:TPU:1, one launch (start us, length us, event | category | flops | bytes accessed | tf_op | source)
XLA Modules:
  0.0 125.2 jit_solution(1385276708812879703)
XLA Ops:
  0.0 0.9 constant_dynamic-slice_fusion
  0.9 1.6 %convert_reduce_fusion.1 = f32[2,256]{1,0:T(2,128)S(1)} fusion(bf16[2,256,1280]{2,1,0:T(8,128)(2,1)} %param.17), kind=kLoop, calls=%fused_computation.20 | loop fusion | flops 1310208 | bytes 1312768 | tf_op jit(solution)/shard_map/reduce_sum | solution.py:16
  2.5 1.8 %fusion.18 = f32[2,256]{1,0:T(2,128)S(1)} fusion(bf16[2,256,1280]{2,1,0:T(8,128)(2,1)} %param.17, f32[2,256]{1,0:T(2,128)S(1)} %broadcast_multiply_fusion.3), kind=kLoop, calls=%fused_computation.32 | loop fusion | flops 2620928 | bytes 1314816 | tf_op jit(solution)/shard_map/reduce_sum | solution.py:17
  4.3 0.5 fusion.20
  4.8 6.5 %fusion.25 = bf16[2,256,3,640]{3,1,2,0:T(8,128)(2,1)} fusion(bf16[1280,3,640]{2,0,1:T(8,128)(2,1)} %param.21, bf16[2,256,1280]{2,1,0:T(8,128)(2,1)S(1)} %fusion.20), kind=kOutput, calls=%fused_computation.44 | convolution fusion | flops 2517565440 | bytes 8192000 | tf_op jit(solution)/shard_map/bld,dkf->blkf/dot_general | solution.py:110
  11.3 4.0 %copy.39 = bf16[2,256,3,640]{1,3,0,2:T(8,128)(2,1)} copy(bf16[2,256,3,640]{3,1,2,0:T(8,128)(2,1)} %fusion.25) | data formatting | bytes 3932160 | tf_op jit(solution)/shard_map/reshape | solution.py:113
  15.3 2.0 %fusion.38 = f32[2,8,256,256]{2,3,1,0:T(8,128)S(1)} fusion(bf16[2,256,3,8,80]{1,4,3,0,2:T(8,128)(2,1)} %bitcast.91), kind=kOutput, calls=%fused_computation.61 | convolution fusion | flops 167772160 | bytes 5505024 | tf_op jit(solution)/shard_map/bqhd,bkhd->bhqk/dot_general | solution.py:117
  17.3 0.1 compare_and_fusion
  17.4 1.5 %fusion.51 = (f32[2,8,256]{2,1,0:T(8,128)S(1)}, f32[2,8,256,256]{2,3,1,0:T(8,128)S(1)}) fusion(f32[2,8,256,256]{2,3,1,0:T(8,128)S(1)} %fusion.38, pred[2,256]{1,0:T(4,128)(4,1)S(1)} %compare_and_fusion), kind=kOutput, calls=%fused_computation.111 | output fusion | flops 6291711 | bytes 8405504 | tf_op jit(solution)/shard_map/sub | solution.py:121
  18.9 1.6 %fusion.29 = bf16[2,8,80,256]{3,2,1,0:T(8,128)(2,1)S(1)} fusion(f32[2,8,256,256]{2,3,1,0:T(8,128)S(1)} %get-tuple-element.20, f32[2,8,256]{2,1,0:T(8,128)S(1)} %get-tuple-element.19, bf16[2,256,3,8,80]{1,4,3,0,2:T(8,128)(2,1)} %bitcast.92), kind=kOutput, calls=%fused_computation.47 | convolution fusion | flops 170196992 | bytes 5521408 | tf_op jit(solution)/shard_map/bhqk,bkhd->bqhd/dot_general | solution.py:122
  20.5 0.0 copy-done
  20.5 1.2 convolution_convert_fusion.1
  21.7 3.3 %collective-permute-start = (bf16[2,256,1280]{2,1,0:T(8,128)(2,1)S(1)}, bf16[2,256,1280]{2,1,0:T(8,128)(2,1)S(1)}, u32[]{:S(2)}, u32[]{:S(2)}) collective-permute-start(bf16[2,256,1280]{2,1,0:T(8,128)(2,1)S(1)} %convolution_convert_fusion.1), channel_id=1, source_target_pairs={{0,1},{1,0},{2,3},{3,2},{4,5},{5,4},{6,7},{7,6},{8,9},{9,8},{10,11... | collective-permute-start | bytes 3932168 | tf_op jit(solution)/shard_map/ppermute | solution.py:23
  25.1 2.7 %collective-permute-done = bf16[2,256,1280]{2,1,0:T(8,128)(2,1)S(1)} collective-permute-done((bf16[2,256,1280]{2,1,0:T(8,128)(2,1)S(1)}, bf16[2,256,1280]{2,1,0:T(8,128)(2,1)S(1)}, u32[]{:S(2)}, u32[]{:S(2)}) %collective-permute-start) | collective-permute-done | bytes 1310752 | tf_op jit(solution)/shard_map/ppermute | solution.py:23
  27.7 0.6 fusion.50
  28.3 0.0 copy-start.9
  28.3 0.4 multiply_reduce_fusion.1
  28.8 0.3 copy-done.9
  29.0 1.5 %multiply_convert_fusion.1 = bf16[2,256,1280]{2,1,0:T(8,128)(2,1)} fusion(f32[2,256,1280]{2,1,0:T(8,128)S(1)} %get-tuple-element.6.res_ref, f32[1280]{0:T(1024)S(1)} %copy-done.9, f32[2,256]{1,0:T(2,128)S(1)} %add_rsqrt_fusion.2, f32[2,256]{1,0:T(2,128)S(1)} %broadcast_multiply_fusion.2), kind=kLoop, calls=%fused_computation.38 | loop fusion | flops 2621440 | bytes 3941376 | tf_op jit(solution)/shard_map/convert_element_type | solution.py:133
  30.5 0.0 copy-done.3
  30.5 14.0 %shard_map.163 = bf16[512,1280]{1,0:T(8,128)(2,1)} custom-call(bf16[512,1280]{1,0:T(8,128)(2,1)} %bitcast.97, bf16[1280,2560]{1,0:T(8,128)(2,1)} %w1_ref.2, bf16[2560,1280]{1,0:T(8,128)(2,1)} %w2_ref.2), custom_call_target="tpu_custom_call" | custom-call | flops 6710886400 | bytes 15728640 | tf_op jit(solution)/shard_map/pallas_call | solution.py:50
  44.4 0.4 collective-permute-start.1
  44.9 0.6 dynamic_slice.12
  47.4 0.0 copy-done.12
  47.4 0.1 constant_dynamic-slice_fusion.2
  47.5 0.1 add_select_fusion
  47.6 0.1 compare_and_fusion.1
  47.7 0.1 and.83
  47.8 0.0 collective-permute-done.1.other_ref
  47.8 0.0 copy-start.7
  47.8 1.0 copy-done.7
  48.8 8.4 %shard_map.164 = bf16[2,64,640]{2,1,0:T(8,128)(2,1)} custom-call(f32[2,256,1280]{2,1,0:T(8,128)} %copy-done.3, bf16[2,256,1280]{2,1,0:T(8,128)(2,1)} %bitcast.96, bf16[2,256,1280]{2,1,0:T(8,128)(2,1)} %copy-done.7, bf16[5120,640]{1,0:T(8,128)(2,1)} %w_ref.1), custom_call_target="tpu_custom_call" | custom-call | flops 922746880 | bytes 11796480 | tf_op jit(solution)/shard_map/pallas_call | solution.py:97
  57.3 1.0 slice_bitcast_fusion.21
  58.2 5.4 %collective-permute-start.3 = (bf16[64,640]{1,0:T(8,128)(2,1)S(1)}, bf16[64,640]{1,0:T(8,128)(2,1)S(1)}, u32[]{:S(2)}, u32[]{:S(2)}) collective-permute-start(bf16[64,640]{1,0:T(8,128)(2,1)S(1)} %get-tuple-element.9), channel_id=1, source_target_pairs={{0,129},{1,128},{2,131},{3,130},{4,133},{5,132},{6,135},{7,134},{8... | collective-permute-start | bytes 245768 | tf_op jit(solution)/shard_map/ppermute | solution.py:197
  63.7 0.2 collective-permute-start.2
  63.9 0.1 fusion.35
  64.0 1.4 %collective-permute-start.5 = (bf16[64,640]{1,0:T(8,128)(2,1)S(1)}, bf16[64,640]{1,0:T(8,128)(2,1)S(1)}, u32[]{:S(2)}, u32[]{:S(2)}) collective-permute-start(bf16[64,640]{1,0:T(8,128)(2,1)S(1)} %get-tuple-element.10), channel_id=1, source_target_pairs={{0,3},{1,2},{2,1},{3,0},{4,7},{5,6},{6,5},{7,4},{8,11},{9,10},{10,... | collective-permute-start | bytes 245768 | tf_op jit(solution)/shard_map/ppermute | solution.py:197
  65.5 0.5 collective-permute-start.4
  66.0 0.7 collective-permute-done.3
  66.7 4.7 %collective-permute-done.2 = bf16[64,640]{1,0:T(8,128)(2,1)S(1)} collective-permute-done((bf16[64,640]{1,0:T(8,128)(2,1)S(1)}, bf16[64,640]{1,0:T(8,128)(2,1)S(1)}, u32[]{:S(2)}, u32[]{:S(2)}) %collective-permute-start.2) | collective-permute-done | bytes 81952 | tf_op jit(solution)/shard_map/ppermute | solution.py:197
  71.5 0.0 collective-permute-done.5
  71.5 0.0 collective-permute-done.4
  71.5 0.1 fusion.40
  71.6 0.0 copy-done.2
  71.6 0.2 convert_reduce_fusion
  71.8 0.5 fusion.15
  72.3 0.5 fusion.17
  72.8 6.4 %convolution_convert_fusion.2 = bf16[512,3,640]{2,0,1:T(8,128)(2,1)} fusion(bf16[1280,3,640]{2,0,1:T(8,128)(2,1)} %param.28, bf16[1,512,1280]{2,1,0:T(8,128)(2,1)S(1)} %fusion.17), kind=kOutput, calls=%fused_computation.45 | convolution fusion | flops 2517565440 | bytes 8192000 | tf_op jit(solution)/shard_map/bld,dkf->blkf/dot_general | solution.py:110
  79.2 4.0 %copy.33 = bf16[512,3,640]{0,2,1:T(8,128)(2,1)} copy(bf16[512,3,640]{2,0,1:T(8,128)(2,1)} %convolution_convert_fusion.2) | data formatting | bytes 3932160 | tf_op jit(solution)/shard_map/convert_element_type | solution.py:112
  83.2 7.7 %fusion.52 = (f32[8,512]{1,0:T(8,128)S(1)}, f32[8,512,512]{1,2,0:T(8,128)}) fusion(pred[512,512]{0,1:T(8,128)(4,1)S(1)} %fusion.35, bf16[1,512,3,8,80]{1,4,3,2,0:T(8,128)(2,1)} %bitcast.93), kind=kOutput, calls=%fused_computation.112 | convolution fusion | flops 343933440 | bytes 9977856 | tf_op jit(solution)/shard_map/sub | solution.py:121
  90.9 4.6 %fusion.30 = bf16[8,80,512]{2,1,0:T(8,128)(2,1)S(1)} fusion(f32[8,512,512]{1,2,0:T(8,128)} %get-tuple-element.22, f32[8,512]{1,0:T(8,128)S(1)} %get-tuple-element.21, bf16[1,512,3,8,80]{1,4,3,2,0:T(8,128)(2,1)} %bitcast.94), kind=kOutput, calls=%fused_computation.48 | convolution fusion | flops 340066304 | bytes 9715712 | tf_op jit(solution)/shard_map/bhqk,bkhd->bqhd/dot_general | solution.py:122
  95.5 1.2 fusion.14
  96.7 1.2 collective-permute-start.6
  97.9 2.7 %collective-permute-done.6 = bf16[1,512,1280]{2,1,0:T(8,128)(2,1)S(1)} collective-permute-done((bf16[1,512,1280]{2,1,0:T(8,128)(2,1)S(1)}, bf16[1,512,1280]{2,1,0:T(8,128)(2,1)S(1)}, u32[]{:S(2)}, u32[]{:S(2)}) %collective-permute-start.6) | collective-permute-done | bytes 1310752 | tf_op jit(solution)/shard_map/ppermute | solution.py:23
  100.5 0.6 fusion.49
  101.2 0.8 multiply_reduce_fusion
  102.0 0.0 copy-done.6
  102.0 0.0 copy-done.11
  102.0 1.8 %fusion.31.x_ref = bf16[512,1280]{1,0:T(8,128)(2,1)} fusion(f32[1280]{0:T(1024)S(1)} %copy-done.11, f32[512]{0:T(512)S(1)} %add_rsqrt_fusion, f32[512]{0:T(512)S(1)} %broadcast_multiply_fusion, bf16[1,512,1280]{2,1,0:T(8,128)(2,1)S(1)} %collective-permute-done.6, bf16[1,512,1280]{2,1,0:T(8,128)(2,1)S(1)} %fusion.14, bf16[1,384,1280]{2,1,0:T(8,128)(2,1)S(1)} %copy-done.2, ...), kind=kLoop, calls=%fused_computation.49 | loop fusion | flops 7864320 | bytes 5252096 | tf_op jit(solution)/shard_map/reshape | solution.py:135
  103.8 13.9 %shard_map.165 = bf16[512,1280]{1,0:T(8,128)(2,1)} custom-call(bf16[512,1280]{1,0:T(8,128)(2,1)} %fusion.31.x_ref, bf16[1280,2560]{1,0:T(8,128)(2,1)} %w1_ref.3, bf16[2560,1280]{1,0:T(8,128)(2,1)} %w2_ref.3), custom_call_target="tpu_custom_call" | custom-call | flops 6710886400 | bytes 15728640 | tf_op jit(solution)/shard_map/pallas_call | solution.py:50
  117.7 0.4 collective-permute-start.7
  118.1 2.9 %collective-permute-done.7 = bf16[1,512,1280]{2,1,0:T(8,128)(2,1)S(1)} collective-permute-done((bf16[1,512,1280]{2,1,0:T(8,128)(2,1)}, bf16[1,512,1280]{2,1,0:T(8,128)(2,1)S(1)}, u32[]{:S(2)}, u32[]{:S(2)}) %collective-permute-start.7) | collective-permute-done | bytes 1310752 | tf_op jit(solution)/shard_map/ppermute | solution.py:137
  121.0 4.2 %fusion.32 = bf16[1,512,1280]{2,1,0:T(8,128)(2,1)} fusion(bf16[1,512,1280]{2,1,0:T(8,128)(2,1)S(1)} %collective-permute-done.7, pred[512]{0:T(512)(128)(4,1)S(1)} %concatenate.47, bf16[512,1280]{1,0:T(8,128)(2,1)} %shard_map.165, bf16[1,512,1280]{2,1,0:T(8,128)(2,1)} %copy-done.6, bf16[1,512,1280]{2,1,0:T(8,128)(2,1)} %copy-done.5, ...), kind=kLoop, calls=%fused_computation.50 | loop fusion | flops 9175040 | bytes 7864832 | tf_op jit(solution)/shard_map/jit(_where)/select_n | solution.py:235
  125.2 0.0 copy-done.1
  (34 shorter events, 0.2 us)
Async XLA Ops:
  0.0 20.5 %copy-start = (bf16[640,1280]{1,0:T(8,128)(2,1)S(1)}, bf16[640,1280]{1,0:T(8,128)(2,1)}, u32[]{:S(2)}) copy-start(bf16[640,1280]{1,0:T(8,128)(2,1)} %param.22) | copy-start | bytes 4915204
  0.0 4.3 %copy-start.4 = (bf16[2,256,1280]{2,1,0:T(8,128)(2,1)S(1)}, bf16[2,256,1280]{2,1,0:T(8,128)(2,1)}, u32[]{:S(2)}) copy-start(bf16[2,256,1280]{2,1,0:T(8,128)(2,1)} %param.17) | copy-start | bytes 3932164
  0.0 4.3 %copy-start.8 = (f32[1280]{0:T(1024)S(1)}, f32[1280]{0:T(1024)}, u32[]{:S(2)}) copy-start(f32[1280]{0:T(1024)} %param.25) | copy-start | bytes 15364
  21.7 6.0 %collective-permute-start = (bf16[2,256,1280]{2,1,0:T(8,128)(2,1)S(1)}, bf16[2,256,1280]{2,1,0:T(8,128)(2,1)S(1)}, u32[]{:S(2)}, u32[]{:S(2)}) collective-permute-start(bf16[2,256,1280]{2,1,0:T(8,128)(2,1)S(1)} %convolution_convert_fusion.1), channel_id=1, source_target_pairs={{0,1},{1,0},{2,3},{3,2},{4,5},{5,4},{6,7},{7,6},{8,9},{9,8},{10,11... | collective-permute-start | bytes 3932168 | tf_op jit(solution)/shard_map/ppermute | solution.py:23
  28.3 2.2 %copy-start.3 = (f32[2,256,1280]{2,1,0:T(8,128)}, f32[2,256,1280]{2,1,0:T(8,128)S(1)}, u32[]{:S(2)}) copy-start(f32[2,256,1280]{2,1,0:T(8,128)S(1)} %get-tuple-element.6.res_ref) | copy-start | bytes 7864324
  28.3 0.7 copy-start.9
  30.5 14.4 %copy-start.14 = (s32[256]{0:T(256)S(1)}, s32[256]{0:T(256)}, u32[]{:S(2)}) copy-start(s32[256]{0:T(256)} %param.19) | copy-start | bytes 3076
  30.5 16.9 %copy-start.12 = (s32[256,2]{0,1:T(2,128)S(1)}, s32[256,2]{0,1:T(2,128)}, u32[]{:S(2)}) copy-start(s32[256,2]{0,1:T(2,128)} %param.18) | copy-start | bytes 6148
  44.4 3.3 %collective-permute-start.1 = (bf16[2,256,1280]{2,1,0:T(8,128)(2,1)}, bf16[2,256,1280]{2,1,0:T(8,128)(2,1)S(1)}, u32[]{:S(2)}, u32[]{:S(2)}) collective-permute-start(bf16[2,256,1280]{2,1,0:T(8,128)(2,1)} %bitcast.95), channel_id=1, source_target_pairs={{0,1},{1,0},{2,3},{3,2},{4,5},{5,4},{6,7},{7,6},{8,9},{9,8},{10,11... | collective-permute-start | bytes 3932168 | tf_op jit(solution)/shard_map/ppermute | solution.py:137
  47.8 23.8 %copy-start.2 = (bf16[1,384,1280]{2,1,0:T(8,128)(2,1)S(1)}, bf16[1,384,1280]{2,1,0:T(8,128)(2,1)}, u32[]{:S(2)}) copy-start(bf16[1,384,1280]{2,1,0:T(8,128)(2,1)} %param.20) | copy-start | bytes 2949124
  47.8 1.1 copy-start.7
  57.3 15.1 %copy-start.10 = (f32[1280]{0:T(1024)S(1)}, f32[1280]{0:T(1024)}, u32[]{:S(2)}) copy-start(f32[1280]{0:T(1024)} %param.32) | copy-start | bytes 15364
  58.2 8.5 %collective-permute-start.3 = (bf16[64,640]{1,0:T(8,128)(2,1)S(1)}, bf16[64,640]{1,0:T(8,128)(2,1)S(1)}, u32[]{:S(2)}, u32[]{:S(2)}) collective-permute-start(bf16[64,640]{1,0:T(8,128)(2,1)S(1)} %get-tuple-element.9), channel_id=1, source_target_pairs={{0,129},{1,128},{2,131},{3,130},{4,133},{5,132},{6,135},{7,134},{8... | collective-permute-start | bytes 245768 | tf_op jit(solution)/shard_map/ppermute | solution.py:197
  63.7 7.8 %collective-permute-start.2 = (bf16[64,640]{1,0:T(8,128)(2,1)S(1)}, bf16[64,640]{1,0:T(8,128)(2,1)S(1)}, u32[]{:S(2)}, u32[]{:S(2)}) collective-permute-start(bf16[64,640]{1,0:T(8,128)(2,1)S(1)} %get-tuple-element.9), channel_id=1, source_target_pairs={{0,128},{1,129},{2,130},{3,131},{4,132},{5,133},{6,134},{7,135},{8... | collective-permute-start | bytes 245768 | tf_op jit(solution)/shard_map/ppermute | solution.py:197
  64.0 7.4 %collective-permute-start.5 = (bf16[64,640]{1,0:T(8,128)(2,1)S(1)}, bf16[64,640]{1,0:T(8,128)(2,1)S(1)}, u32[]{:S(2)}, u32[]{:S(2)}) collective-permute-start(bf16[64,640]{1,0:T(8,128)(2,1)S(1)} %get-tuple-element.10), channel_id=1, source_target_pairs={{0,3},{1,2},{2,1},{3,0},{4,7},{5,6},{6,5},{7,4},{8,11},{9,10},{10,... | collective-permute-start | bytes 245768 | tf_op jit(solution)/shard_map/ppermute | solution.py:197
  65.5 6.0 %collective-permute-start.4 = (bf16[64,640]{1,0:T(8,128)(2,1)S(1)}, bf16[64,640]{1,0:T(8,128)(2,1)S(1)}, u32[]{:S(2)}, u32[]{:S(2)}) collective-permute-start(bf16[64,640]{1,0:T(8,128)(2,1)S(1)} %get-tuple-element.10), channel_id=1, source_target_pairs={{0,2},{1,3},{2,0},{3,1},{4,6},{5,7},{6,4},{7,5},{8,10},{9,11},{10,... | collective-permute-start | bytes 245768 | tf_op jit(solution)/shard_map/ppermute | solution.py:197
  90.9 4.6 %copy-start.13 = (bf16[640,1280]{1,0:T(8,128)(2,1)S(1)}, bf16[640,1280]{1,0:T(8,128)(2,1)}, u32[]{:S(2)}) copy-start(bf16[640,1280]{1,0:T(8,128)(2,1)} %param.29) | copy-start | bytes 4915204
  96.7 5.3 %copy-start.5 = (bf16[1,512,1280]{2,1,0:T(8,128)(2,1)}, bf16[1,512,1280]{2,1,0:T(8,128)(2,1)S(1)}, u32[]{:S(2)}) copy-start(bf16[1,512,1280]{2,1,0:T(8,128)(2,1)S(1)} %fusion.14) | copy-start | bytes 3932164
  96.7 3.9 %collective-permute-start.6 = (bf16[1,512,1280]{2,1,0:T(8,128)(2,1)S(1)}, bf16[1,512,1280]{2,1,0:T(8,128)(2,1)S(1)}, u32[]{:S(2)}, u32[]{:S(2)}) collective-permute-start(bf16[1,512,1280]{2,1,0:T(8,128)(2,1)S(1)} %fusion.14), channel_id=1, source_target_pairs={{0,1},{1,0},{2,3},{3,2},{4,5},{5,4},{6,7},{7,6},{8,9},{9,8},{10,11... | collective-permute-start | bytes 3932168 | tf_op jit(solution)/shard_map/ppermute | solution.py:23
  100.5 1.4 %copy-start.6 = (bf16[1,512,1280]{2,1,0:T(8,128)(2,1)}, bf16[1,512,1280]{2,1,0:T(8,128)(2,1)S(1)}, u32[]{:S(2)}) copy-start(bf16[1,512,1280]{2,1,0:T(8,128)(2,1)S(1)} %collective-permute-done.6) | copy-start | bytes 3932164
  101.1 0.8 copy-start.11
  117.7 7.5 %copy-start.1 = (bf16[640,1280]{1,0:T(8,128)(2,1)S(1)}, bf16[640,1280]{1,0:T(8,128)(2,1)}, u32[]{:S(2)}) copy-start(bf16[640,1280]{1,0:T(8,128)(2,1)} %param.22) | copy-start | bytes 4915204
  117.7 3.2 %collective-permute-start.7 = (bf16[1,512,1280]{2,1,0:T(8,128)(2,1)}, bf16[1,512,1280]{2,1,0:T(8,128)(2,1)S(1)}, u32[]{:S(2)}, u32[]{:S(2)}) collective-permute-start(bf16[1,512,1280]{2,1,0:T(8,128)(2,1)} %bitcast.98), channel_id=1, source_target_pairs={{0,1},{1,0},{2,3},{3,2},{4,5},{5,4},{6,7},{7,6},{8,9},{9,8},{10,11... | collective-permute-start | bytes 3932168 | tf_op jit(solution)/shard_map/ppermute | solution.py:137

commit v2 on v1

--- a/solution.py
+++ b/solution.py
@@ -24,11 +24,15 @@
     return mine.astype(jnp.float32) + other.astype(jnp.float32)
 
 
-def _feed_forward_kernel(rows_per_step, x_ref, w1_ref, w2_ref, o_ref, acc_ref):
+def _feed_forward_kernel(rows_per_step, res_ref, gain_ref, w1_ref, w2_ref, o_ref, x_ref, acc_ref):
     k = pl.program_id(0)
 
     @pl.when(k == 0)
     def _():
+        values = res_ref[...]
+        center = values - jnp.mean(values, axis=-1, keepdims=True)
+        spread = jnp.mean(center * center, axis=-1, keepdims=True)
+        x_ref[...] = (center * lax.rsqrt(spread + 1e-06) * gain_ref[...]).astype(x_ref.dtype)
         acc_ref[...] = jnp.zeros_like(acc_ref)
 
     w1 = w1_ref[...]
@@ -44,8 +48,8 @@
         o_ref[...] = acc_ref[...].astype(o_ref.dtype)
 
 
-def feed_forward(x, expand, contract, hidden_step=512, rows_per_step=128):
-    length, width = x.shape
+def feed_forward(residual, gain, expand, contract, hidden_step=512, rows_per_step=128):
+    length, width = residual.shape
     hidden = expand.shape[1]
     return pl.pallas_call(
         functools.partial(_feed_forward_kernel, rows_per_step),
@@ -53,50 +57,65 @@
         grid=(hidden // hidden_step,),
         in_specs=[
             pl.BlockSpec((length, width), lambda k: (0, 0)),
+            pl.BlockSpec((1, width), lambda k: (0, 0)),
             pl.BlockSpec((width, hidden_step), lambda k: (0, k)),
             pl.BlockSpec((hidden_step, width), lambda k: (k, 0)),
         ],
         out_specs=pl.BlockSpec((length, width), lambda k: (0, 0)),
-        scratch_shapes=[pltpu.VMEM((length, width), jnp.float32)],
+        scratch_shapes=[
+            pltpu.VMEM((length, width), jnp.bfloat16),
+            pltpu.VMEM((length, width), jnp.float32),
+        ],
         cost_estimate=pl.CostEstimate(
             flops=4 * length * width * hidden,
             transcendentals=length * hidden,
-            bytes_accessed=2 * (2 * width * hidden + 2 * length * width),
+            bytes_accessed=2 * (2 * width * hidden + 3 * length * width),
         ),
-    )(x, expand, contract)
-
-
-def _merge_kernel(res_ref, mine_ref, other_ref, w_ref, o_ref):
-    cells, width = res_ref.shape[1], res_ref.shape[2]
+    )(residual, gain.reshape(1, width), expand, contract)
+
+
+def _merge_kernel(res_ref, mine_ref, other_ref, w_ref, o_ref, enc_ref, acc_ref):
+    step = pl.program_id(0)
+    images, cells = res_ref.shape[0], res_ref.shape[1]
     half = GRID // 2
+
+    @pl.when(step == 0)
+    def _():
+        for i in range(images):
+            enc_ref[i] = (
+                res_ref[i] + (mine_ref[i].astype(jnp.float32) + other_ref[i].astype(jnp.float32))
+            ).astype(enc_ref.dtype)
+        acc_ref[...] = jnp.zeros_like(acc_ref)
+
     slot = lax.broadcasted_iota(jnp.int32, (half * half, cells), 0)
     cell = lax.broadcasted_iota(jnp.int32, (half * half, cells), 1)
-    for i in range(res_ref.shape[0]):
-        encoded = (
-            res_ref[i] + (mine_ref[i].astype(jnp.float32) + other_ref[i].astype(jnp.float32))
-        ).astype(jnp.bfloat16)
-        total = None
-        for a in range(2):
-            for b in range(2):
-                wanted = (2 * (slot // half) + a) * GRID + 2 * (slot % half) + b
-                pick = jnp.where(cell == wanted, 1.0, 0.0).astype(jnp.bfloat16)
-                rows = jnp.dot(pick, encoded, preferred_element_type=jnp.float32).astype(jnp.bfloat16)
-                part = jnp.dot(
-                    rows,
-                    w_ref[pl.ds((2 * a + b) * width, width), :],
-                    preferred_element_type=jnp.float32,
-                )
-                total = part if total is None else total + part
-        o_ref[i] = total.astype(o_ref.dtype)
+    wanted = (2 * (slot // half) + step // 2) * GRID + 2 * (slot % half) + step % 2
+    pick = jnp.where(cell == wanted, 1.0, 0.0).astype(jnp.bfloat16)
+    weight = w_ref[...]
+    for i in range(images):
+        rows = jnp.dot(pick, enc_ref[i], preferred_element_type=jnp.float32).astype(jnp.bfloat16)
+        acc_ref[i] += jnp.dot(rows, weight, preferred_element_type=jnp.float32)
+
+    @pl.when(step == pl.num_programs(0) - 1)
+    def _():
+        o_ref[...] = acc_ref[...].astype(o_ref.dtype)
 
 
 def merge(residual, mine, other, merge_weight):
     images, cells, width = residual.shape
     half = GRID // 2
     out_width = merge_weight.shape[1]
+    whole = pl.BlockSpec((images, cells, width), lambda s: (0, 0, 0))
     return pl.pallas_call(
         _merge_kernel,
         out_shape=jax.ShapeDtypeStruct((images, half * half, out_width), jnp.bfloat16),
+        grid=(4,),
+        in_specs=[whole, whole, whole, pl.BlockSpec((width, out_width), lambda s: (s, 0))],
+        out_specs=pl.BlockSpec((images, half * half, out_width), lambda s: (0, 0, 0)),
+        scratch_shapes=[
+            pltpu.VMEM((images, cells, width), jnp.bfloat16),
+            pltpu.VMEM((images, half * half, out_width), jnp.float32),
+        ],
         cost_estimate=pl.CostEstimate(
             flops=2 * images * cells * width * (out_width + half * half),
             transcendentals=0,
@@ -130,9 +149,8 @@
     first = lax.optimization_barrier(normalize(widened, gain_first).astype(jnp.bfloat16))
     attended = attend(first, allowed, attend_in, attend_out)
     residual = widened + tensor_sum(attended)
-    second = normalize(residual, gain_second).astype(jnp.bfloat16)
-    batch, length, width = second.shape
-    partial_out = feed_forward(second.reshape(batch * length, width), expand, contract)
+    batch, length, width = residual.shape
+    partial_out = feed_forward(residual.reshape(batch * length, width), gain_second, expand, contract)
     mine = partial_out.reshape(batch, length, width)
     other = lax.ppermute(mine, "tensor", [(0, 1), (1, 0)])
     if split:

time: 126 us -> 128 us (1.016)
  Pallas kernels: 36.3 us -> 38.7 us
  local copies, waits for them, and re-layouts: 12 us -> 14 us
  other arithmetic: 16.9 us -> 15.1 us
    pallas_call x2, Pallas kernels: 27.9 us -> 30.2 us  [feed_forward(): pl.pallas_call(functools.partial(_feed_forward_kernel, rows_per_step), ou...]
    add x0 -> x1, other arithmetic: none -> 1.94 us  [layer(): residual = widened + tensor_sum(attended)]
    ppermute x4, waiting for transfers between devices: 5.48 us -> 7.2 us  [on_device(): halves.append(lax.ppermute(merged[j], ('req', 'tensor'), perm))]
    convert_element_type x1 -> x0, other arithmetic: 1.46 us -> none  [layer(): second = normalize(residual, gain_second).astype(jnp.bfloat16)]
    reduce_sum x4 -> x2, other arithmetic: 3 us -> 1.81 us  [normalize(): center = values - jnp.mean(values, axis=-1, keepdims=True)]
    reduce_sum x4 -> x2, other arithmetic: 3.45 us -> 2.28 us  [normalize(): spread = jnp.mean(center * center, axis=-1, keepdims=True)]
  transfers between devices with their start and end apart: 8 -> 8, of which waited for: 5 -> 5; matrix products, arithmetic and copies ran while one was open for 1% -> 2% of each run, Pallas kernels for 0% -> 0%
where the time goes in v2:
time: 128 us
  Pallas kernels  38.7 us (30%)
  matrix products  31.3 us (24%)
  other arithmetic  15.1 us (12%)
  waiting for transfers between devices  14.4 us (11%)
  local copies, waits for them, and re-layouts  14 us (11%)
  starting transfers between devices  12.5 us (10%)
  between operations  1.98 us (2%)
    pallas_call x2, Pallas kernels, feed_forward(): pl.pallas_call(functools.partial(_feed_forward_kernel, rows_per_step), ou...  30.2 us
    dot_general x2, matrix products, attend(): jnp.einsum('bld,dkf->blkf', normed, attend_in, preferred_element_type=jnp...  13 us
    pallas_call x1, Pallas kernels, merge(): pl.pallas_call(_merge_kernel, out_shape=jax.ShapeDtypeStruct((images, hal...  8.49 us
    sub x1, matrix products, attend(): probs = jax.nn.softmax(scores, axis=-1).astype(jnp.bfloat16)  7.7 us
    ppermute x4, starting transfers between devices, on_device(): halves.append(lax.ppermute(merged[j], ('req', 'tensor'), perm))  7.68 us
    ppermute x4, waiting for transfers between devices, on_device(): halves.append(lax.ppermute(merged[j], ('req', 'tensor'), perm))  7.2 us
    dot_general x2, matrix products, attend(): jnp.einsum('bhqk,bkhd->bqhd', probs, value_rows, preferred_element_type=j...  6.14 us
    select_n x1, other arithmetic, on_device(): jnp.where(prompt_valid[None, :, None], decoded, jnp.zeros_like(decoded))  4.21 us
  transfers between devices with their start and end apart: 8, of which 5 were waited for; matrix products, arithmetic and copies ran while one was open for 2% of the time, Pallas kernels for 0%

profile of v2, /device:TPU:1, one launch (start us, length us, event | category | flops | bytes accessed | tf_op | source)
XLA Modules:
  0.0 127.9 jit_solution(5529425148181954728)
XLA Ops:
  0.0 0.0 copy-start
  0.0 0.9 constant_dynamic-slice_fusion
  0.9 1.6 %convert_reduce_fusion.1 = f32[2,256]{1,0:T(2,128)S(1)} fusion(bf16[2,256,1280]{2,1,0:T(8,128)(2,1)} %param.17), kind=kLoop, calls=%fused_computation.20 | loop fusion | flops 1310208 | bytes 1312768 | tf_op jit(solution)/shard_map/reduce_sum | solution.py:16
  2.5 1.8 %fusion.18 = f32[2,256]{1,0:T(2,128)S(1)} fusion(bf16[2,256,1280]{2,1,0:T(8,128)(2,1)} %param.17, f32[2,256]{1,0:T(2,128)S(1)} %broadcast_multiply_fusion.1), kind=kLoop, calls=%fused_computation.32 | loop fusion | flops 2620928 | bytes 1314816 | tf_op jit(solution)/shard_map/reduce_sum | solution.py:17
  4.3 0.0 copy-done.3
  4.3 0.0 copy-done.7
  4.3 0.5 fusion.20
  4.8 6.5 %fusion.25 = bf16[2,256,3,640]{3,1,2,0:T(8,128)(2,1)} fusion(bf16[1280,3,640]{2,0,1:T(8,128)(2,1)} %param.21, bf16[2,256,1280]{2,1,0:T(8,128)(2,1)S(1)} %fusion.20), kind=kOutput, calls=%fused_computation.40 | convolution fusion | flops 2517565440 | bytes 8192000 | tf_op jit(solution)/shard_map/bld,dkf->blkf/dot_general | solution.py:129
  11.3 4.0 %copy.39 = bf16[2,256,3,640]{1,3,0,2:T(8,128)(2,1)} copy(bf16[2,256,3,640]{3,1,2,0:T(8,128)(2,1)} %fusion.25) | data formatting | bytes 3932160 | tf_op jit(solution)/shard_map/reshape | solution.py:132
  15.3 2.0 %fusion.38 = f32[2,8,256,256]{2,3,1,0:T(8,128)S(1)} fusion(bf16[2,256,3,8,80]{1,4,3,0,2:T(8,128)(2,1)} %bitcast.92), kind=kOutput, calls=%fused_computation.57 | convolution fusion | flops 167772160 | bytes 5505024 | tf_op jit(solution)/shard_map/bqhd,bkhd->bhqk/dot_general | solution.py:136
  17.3 0.1 compare_and_fusion
  17.4 1.5 %fusion.49 = (f32[2,8,256]{2,1,0:T(8,128)S(1)}, f32[2,8,256,256]{2,3,1,0:T(8,128)S(1)}) fusion(f32[2,8,256,256]{2,3,1,0:T(8,128)S(1)} %fusion.38, pred[2,256]{1,0:T(4,128)(4,1)S(1)} %compare_and_fusion), kind=kOutput, calls=%fused_computation.101 | output fusion | flops 6291711 | bytes 8405504 | tf_op jit(solution)/shard_map/sub | solution.py:140
  19.0 1.6 %fusion.30 = bf16[2,8,80,256]{3,2,1,0:T(8,128)(2,1)S(1)} fusion(f32[2,8,256,256]{2,3,1,0:T(8,128)S(1)} %get-tuple-element.18, f32[2,8,256]{2,1,0:T(8,128)S(1)} %get-tuple-element.17, bf16[2,256,3,8,80]{1,4,3,0,2:T(8,128)(2,1)} %bitcast.93), kind=kOutput, calls=%fused_computation.44 | convolution fusion | flops 170196992 | bytes 5521408 | tf_op jit(solution)/shard_map/bhqk,bkhd->bqhd/dot_general | solution.py:141
  20.5 0.0 copy-done
  20.6 1.2 convolution_convert_fusion.1
  21.8 3.3 %collective-permute-start = (bf16[2,256,1280]{2,1,0:T(8,128)(2,1)S(1)}, bf16[2,256,1280]{2,1,0:T(8,128)(2,1)S(1)}, u32[]{:S(2)}, u32[]{:S(2)}) collective-permute-start(bf16[2,256,1280]{2,1,0:T(8,128)(2,1)S(1)} %convolution_convert_fusion.1), channel_id=1, source_target_pairs={{0,1},{1,0},{2,3},{3,2},{4,5},{5,4},{6,7},{7,6},{8,9},{9,8},{10,11... | collective-permute-start | bytes 3932168 | tf_op jit(solution)/shard_map/ppermute | solution.py:23
  25.1 0.0 copy-done.9
  25.1 0.6 reshape.385.gain_ref
  25.7 2.1 %collective-permute-done = bf16[2,256,1280]{2,1,0:T(8,128)(2,1)S(1)} collective-permute-done((bf16[2,256,1280]{2,1,0:T(8,128)(2,1)S(1)}, bf16[2,256,1280]{2,1,0:T(8,128)(2,1)S(1)}, u32[]{:S(2)}, u32[]{:S(2)}) %collective-permute-start) | collective-permute-done | bytes 1310752 | tf_op jit(solution)/shard_map/ppermute | solution.py:23
  27.8 1.9 %convert_add_fusion.1.res_ref = f32[2,256,1280]{2,1,0:T(8,128)} fusion(bf16[2,256,1280]{2,1,0:T(8,128)(2,1)S(1)} %copy-done.3, bf16[2,256,1280]{2,1,0:T(8,128)(2,1)S(1)} %collective-permute-done, bf16[2,256,1280]{2,1,0:T(8,128)(2,1)S(1)} %convolution_convert_fusion.1), kind=kLoop, calls=%fused_computation.18 | loop fusion | flops 3276800 | bytes 6553600 | tf_op jit(solution)/shard_map/add | solution.py:151
  29.7 15.1 %shard_map.163 = bf16[512,1280]{1,0:T(8,128)(2,1)} custom-call(f32[512,1280]{1,0:T(8,128)} %bitcast.91, f32[1,1280]{1,0:T(1,128)} %reshape.385.gain_ref, bf16[1280,2560]{1,0:T(8,128)(2,1)} %w1_ref.2, bf16[2560,1280]{1,0:T(8,128)(2,1)} %w2_ref.2), custom_call_target="tpu_custom_call" | custom-call | flops 6710886400 | bytes 17039360 | tf_op jit(solution)/shard_map/pallas_call | solution.py:54
  44.8 0.4 collective-permute-start.1
  45.2 0.0 copy-done.13
  45.2 0.6 dynamic_slice.12
  47.6 0.0 copy-done.11
  47.6 0.1 constant_dynamic-slice_fusion.2
  47.7 0.1 add_select_fusion
  47.7 0.1 compare_and_fusion.1
  47.8 0.1 and.83
  47.9 0.2 collective-permute-done.1.other_ref
  48.1 1.1 copy-done.6
  49.2 8.5 %shard_map.164 = bf16[2,64,640]{2,1,0:T(8,128)(2,1)} custom-call(f32[2,256,1280]{2,1,0:T(8,128)} %convert_add_fusion.1.res_ref, bf16[2,256,1280]{2,1,0:T(8,128)(2,1)} %bitcast.97, bf16[2,256,1280]{2,1,0:T(8,128)(2,1)} %copy-done.6, bf16[5120,640]{1,0:T(8,128)(2,1)} %w_ref.1), custom_call_target="tpu_custom_call" | custom-call | flops 922746880 | bytes 11796480 | tf_op jit(solution)/shard_map/pallas_call | solution.py:109
  57.6 1.0 slice_bitcast_fusion.21
  58.6 5.3 %collective-permute-start.2 = (bf16[64,640]{1,0:T(8,128)(2,1)S(1)}, bf16[64,640]{1,0:T(8,128)(2,1)S(1)}, u32[]{:S(2)}, u32[]{:S(2)}) collective-permute-start(bf16[64,640]{1,0:T(8,128)(2,1)S(1)} %get-tuple-element.7), channel_id=1, source_target_pairs={{0,128},{1,129},{2,130},{3,131},{4,132},{5,133},{6,134},{7,135},{8... | collective-permute-start | bytes 245768 | tf_op jit(solution)/shard_map/ppermute | solution.py:215
  63.9 0.7 collective-permute-start.3
  64.6 0.1 fusion.35
  64.8 1.1 collective-permute-start.4
  65.9 0.6 collective-permute-start.5
  66.4 0.0 collective-permute-done.2
  66.4 7.2 %collective-permute-done.3 = bf16[64,640]{1,0:T(8,128)(2,1)S(1)} collective-permute-done((bf16[64,640]{1,0:T(8,128)(2,1)S(1)}, bf16[64,640]{1,0:T(8,128)(2,1)S(1)}, u32[]{:S(2)}, u32[]{:S(2)}) %collective-permute-start.3) | collective-permute-done | bytes 81952 | tf_op jit(solution)/shard_map/ppermute | solution.py:215
  73.7 0.0 collective-permute-done.4
  73.7 0.0 collective-permute-done.5
  73.7 0.1 fusion.40
  73.8 0.0 copy-done.2
  73.8 0.2 convert_reduce_fusion
  74.0 0.5 fusion.15
  74.5 0.0 copy-done.8
  74.5 0.5 fusion.17
  75.0 6.5 %convolution_convert_fusion.2 = bf16[512,3,640]{2,0,1:T(8,128)(2,1)} fusion(bf16[1280,3,640]{2,0,1:T(8,128)(2,1)} %param.28, bf16[1,512,1280]{2,1,0:T(8,128)(2,1)S(1)} %fusion.17), kind=kOutput, calls=%fused_computation.41 | convolution fusion | flops 2517565440 | bytes 8192000 | tf_op jit(solution)/shard_map/bld,dkf->blkf/dot_general | solution.py:129
  81.5 4.0 %copy.33 = bf16[512,3,640]{0,2,1:T(8,128)(2,1)} copy(bf16[512,3,640]{2,0,1:T(8,128)(2,1)} %convolution_convert_fusion.2) | data formatting | bytes 3932160 | tf_op jit(solution)/shard_map/convert_element_type | solution.py:131
  85.4 7.7 %fusion.50 = (f32[8,512]{1,0:T(8,128)S(1)}, f32[8,512,512]{1,2,0:T(8,128)}) fusion(pred[512,512]{0,1:T(8,128)(4,1)S(1)} %fusion.35, bf16[1,512,3,8,80]{1,4,3,2,0:T(8,128)(2,1)} %bitcast.94), kind=kOutput, calls=%fused_computation.102 | convolution fusion | flops 343933440 | bytes 9977856 | tf_op jit(solution)/shard_map/sub | solution.py:140
  93.1 4.6 %fusion.31 = bf16[8,80,512]{2,1,0:T(8,128)(2,1)S(1)} fusion(f32[8,512,512]{1,2,0:T(8,128)} %get-tuple-element.20, f32[8,512]{1,0:T(8,128)S(1)} %get-tuple-element.19, bf16[1,512,3,8,80]{1,4,3,2,0:T(8,128)(2,1)} %bitcast.95), kind=kOutput, calls=%fused_computation.45 | convolution fusion | flops 340066304 | bytes 9715712 | tf_op jit(solution)/shard_map/bhqk,bkhd->bqhd/dot_general | solution.py:141
  97.7 0.0 copy-done.12
  97.7 0.0 copy-start.10
  97.7 1.2 fusion.14
  98.9 0.8 collective-permute-start.6
  99.7 0.6 reshape.394.gain_ref
  100.3 2.1 %collective-permute-done.6 = bf16[1,512,1280]{2,1,0:T(8,128)(2,1)S(1)} collective-permute-done((bf16[1,512,1280]{2,1,0:T(8,128)(2,1)S(1)}, bf16[1,512,1280]{2,1,0:T(8,128)(2,1)S(1)}, u32[]{:S(2)}, u32[]{:S(2)}) %collective-permute-start.6) | collective-permute-done | bytes 1310752 | tf_op jit(solution)/shard_map/ppermute | solution.py:23
  102.4 1.0 copy-done.5
  103.4 1.9 %fusion.28.res_ref = f32[512,1280]{1,0:T(8,128)} fusion(bf16[1,512,1280]{2,1,0:T(8,128)(2,1)S(1)} %collective-permute-done.6, bf16[1,512,1280]{2,1,0:T(8,128)(2,1)S(1)} %fusion.14, bf16[1,384,1280]{2,1,0:T(8,128)(2,1)S(1)} %copy-done.2, bf16[1,128,1280]{2,1,0:T(8,128)(2,1)S(1)} %fusion.40), kind=kLoop, calls=%fused_computation.42 | loop fusion | flops 5242880 | bytes 6553600 | tf_op jit(solution)/shard_map/reshape | solution.py:153
  105.4 15.1 %shard_map.165 = bf16[512,1280]{1,0:T(8,128)(2,1)} custom-call(f32[512,1280]{1,0:T(8,128)} %fusion.28.res_ref, f32[1,1280]{1,0:T(1,128)} %reshape.394.gain_ref, bf16[1280,2560]{1,0:T(8,128)(2,1)} %w1_ref.3, bf16[2560,1280]{1,0:T(8,128)(2,1)} %w2_ref.3), custom_call_target="tpu_custom_call" | custom-call | flops 6710886400 | bytes 17039360 | tf_op jit(solution)/shard_map/pallas_call | solution.py:54
  120.5 0.3 collective-permute-start.7
  120.8 2.9 %collective-permute-done.7 = bf16[1,512,1280]{2,1,0:T(8,128)(2,1)S(1)} collective-permute-done((bf16[1,512,1280]{2,1,0:T(8,128)(2,1)}, bf16[1,512,1280]{2,1,0:T(8,128)(2,1)S(1)}, u32[]{:S(2)}, u32[]{:S(2)}) %collective-permute-start.7) | collective-permute-done | bytes 1310752 | tf_op jit(solution)/shard_map/ppermute | solution.py:155
  123.7 4.2 %fusion.32 = bf16[1,512,1280]{2,1,0:T(8,128)(2,1)} fusion(bf16[1,512,1280]{2,1,0:T(8,128)(2,1)S(1)} %collective-permute-done.7, bf16[1,512,1280]{2,1,0:T(8,128)(2,1)} %copy-done.5, bf16[1,512,1280]{2,1,0:T(8,128)(2,1)} %copy-done.4, pred[512]{0:T(512)(128)(4,1)S(1)} %concatenate.47, bf16[512,1280]{1,0:T(8,128)(2,1)} %shard_map.165, ...), kind=kLoop, calls=%fused_computation.46 | loop fusion | flops 9175040 | bytes 7864832 | tf_op jit(solution)/shard_map/jit(_where)/select_n | solution.py:253
  (26 shorter events, 0.1 us)
Async XLA Ops:
  0.0 20.5 %copy-start = (bf16[640,1280]{1,0:T(8,128)(2,1)S(1)}, bf16[640,1280]{1,0:T(8,128)(2,1)}, u32[]{:S(2)}) copy-start(bf16[640,1280]{1,0:T(8,128)(2,1)} %param.22) | copy-start | bytes 4915204
  0.0 4.3 %copy-start.3 = (bf16[2,256,1280]{2,1,0:T(8,128)(2,1)S(1)}, bf16[2,256,1280]{2,1,0:T(8,128)(2,1)}, u32[]{:S(2)}) copy-start(bf16[2,256,1280]{2,1,0:T(8,128)(2,1)} %param.17) | copy-start | bytes 3932164
  0.0 4.3 %copy-start.7 = (f32[1280]{0:T(1024)S(1)}, f32[1280]{0:T(1024)}, u32[]{:S(2)}) copy-start(f32[1280]{0:T(1024)} %param.25) | copy-start | bytes 15364
  20.5 4.6 %copy-start.9 = (f32[1280]{0:T(1024)S(1)}, f32[1280]{0:T(1024)}, u32[]{:S(2)}) copy-start(f32[1280]{0:T(1024)} %param.26) | copy-start | bytes 15364
  21.8 6.0 %collective-permute-start = (bf16[2,256,1280]{2,1,0:T(8,128)(2,1)S(1)}, bf16[2,256,1280]{2,1,0:T(8,128)(2,1)S(1)}, u32[]{:S(2)}, u32[]{:S(2)}) collective-permute-start(bf16[2,256,1280]{2,1,0:T(8,128)(2,1)S(1)} %convolution_convert_fusion.1), channel_id=1, source_target_pairs={{0,1},{1,0},{2,3},{3,2},{4,5},{5,4},{6,7},{7,6},{8,9},{9,8},{10,11... | collective-permute-start | bytes 3932168 | tf_op jit(solution)/shard_map/ppermute | solution.py:23
  29.7 15.5 %copy-start.13 = (s32[256]{0:T(256)S(1)}, s32[256]{0:T(256)}, u32[]{:S(2)}) copy-start(s32[256]{0:T(256)} %param.19) | copy-start | bytes 3076
  29.7 17.9 %copy-start.11 = (s32[256,2]{0,1:T(2,128)S(1)}, s32[256,2]{0,1:T(2,128)}, u32[]{:S(2)}) copy-start(s32[256,2]{0,1:T(2,128)} %param.18) | copy-start | bytes 6148
  44.8 3.3 %collective-permute-start.1 = (bf16[2,256,1280]{2,1,0:T(8,128)(2,1)}, bf16[2,256,1280]{2,1,0:T(8,128)(2,1)S(1)}, u32[]{:S(2)}, u32[]{:S(2)}) collective-permute-start(bf16[2,256,1280]{2,1,0:T(8,128)(2,1)} %bitcast.96), channel_id=1, source_target_pairs={{0,1},{1,0},{2,3},{3,2},{4,5},{5,4},{6,7},{7,6},{8,9},{9,8},{10,11... | collective-permute-start | bytes 3932168 | tf_op jit(solution)/shard_map/ppermute | solution.py:155
  47.9 25.9 %copy-start.2 = (bf16[1,384,1280]{2,1,0:T(8,128)(2,1)S(1)}, bf16[1,384,1280]{2,1,0:T(8,128)(2,1)}, u32[]{:S(2)}) copy-start(bf16[1,384,1280]{2,1,0:T(8,128)(2,1)} %param.20) | copy-start | bytes 2949124
  48.1 1.1 copy-start.6
  57.6 16.9 %copy-start.8 = (f32[1280]{0:T(1024)S(1)}, f32[1280]{0:T(1024)}, u32[]{:S(2)}) copy-start(f32[1280]{0:T(1024)} %param.32) | copy-start | bytes 15364
  58.6 7.8 %collective-permute-start.2 = (bf16[64,640]{1,0:T(8,128)(2,1)S(1)}, bf16[64,640]{1,0:T(8,128)(2,1)S(1)}, u32[]{:S(2)}, u32[]{:S(2)}) collective-permute-start(bf16[64,640]{1,0:T(8,128)(2,1)S(1)} %get-tuple-element.7), channel_id=1, source_target_pairs={{0,128},{1,129},{2,130},{3,131},{4,132},{5,133},{6,134},{7,135},{8... | collective-permute-start | bytes 245768 | tf_op jit(solution)/shard_map/ppermute | solution.py:215
  63.9 9.8 %collective-permute-start.3 = (bf16[64,640]{1,0:T(8,128)(2,1)S(1)}, bf16[64,640]{1,0:T(8,128)(2,1)S(1)}, u32[]{:S(2)}, u32[]{:S(2)}) collective-permute-start(bf16[64,640]{1,0:T(8,128)(2,1)S(1)} %get-tuple-element.7), channel_id=1, source_target_pairs={{0,129},{1,128},{2,131},{3,130},{4,133},{5,132},{6,135},{7,134},{8... | collective-permute-start | bytes 245768 | tf_op jit(solution)/shard_map/ppermute | solution.py:215
  64.8 8.9 %collective-permute-start.4 = (bf16[64,640]{1,0:T(8,128)(2,1)S(1)}, bf16[64,640]{1,0:T(8,128)(2,1)S(1)}, u32[]{:S(2)}, u32[]{:S(2)}) collective-permute-start(bf16[64,640]{1,0:T(8,128)(2,1)S(1)} %get-tuple-element.8), channel_id=1, source_target_pairs={{0,2},{1,3},{2,0},{3,1},{4,6},{5,7},{6,4},{7,5},{8,10},{9,11},{10,... | collective-permute-start | bytes 245768 | tf_op jit(solution)/shard_map/ppermute | solution.py:215
  65.9 7.8 %collective-permute-start.5 = (bf16[64,640]{1,0:T(8,128)(2,1)S(1)}, bf16[64,640]{1,0:T(8,128)(2,1)S(1)}, u32[]{:S(2)}, u32[]{:S(2)}) collective-permute-start(bf16[64,640]{1,0:T(8,128)(2,1)S(1)} %get-tuple-element.8), channel_id=1, source_target_pairs={{0,3},{1,2},{2,1},{3,0},{4,7},{5,6},{6,5},{7,4},{8,11},{9,10},{10,... | collective-permute-start | bytes 245768 | tf_op jit(solution)/shard_map/ppermute | solution.py:215
  93.1 4.6 %copy-start.12 = (bf16[640,1280]{1,0:T(8,128)(2,1)S(1)}, bf16[640,1280]{1,0:T(8,128)(2,1)}, u32[]{:S(2)}) copy-start(bf16[640,1280]{1,0:T(8,128)(2,1)} %param.29) | copy-start | bytes 4915204
  97.7 2.0 %copy-start.10 = (f32[1280]{0:T(1024)S(1)}, f32[1280]{0:T(1024)}, u32[]{:S(2)}) copy-start(f32[1280]{0:T(1024)} %param.33) | copy-start | bytes 15364
  98.9 6.4 %copy-start.4 = (bf16[1,512,1280]{2,1,0:T(8,128)(2,1)}, bf16[1,512,1280]{2,1,0:T(8,128)(2,1)S(1)}, u32[]{:S(2)}) copy-start(bf16[1,512,1280]{2,1,0:T(8,128)(2,1)S(1)} %fusion.14) | copy-start | bytes 3932164
  98.9 3.4 %collective-permute-start.6 = (bf16[1,512,1280]{2,1,0:T(8,128)(2,1)S(1)}, bf16[1,512,1280]{2,1,0:T(8,128)(2,1)S(1)}, u32[]{:S(2)}, u32[]{:S(2)}) collective-permute-start(bf16[1,512,1280]{2,1,0:T(8,128)(2,1)S(1)} %fusion.14), channel_id=1, source_target_pairs={{0,1},{1,0},{2,3},{3,2},{4,5},{5,4},{6,7},{7,6},{8,9},{9,8},{10,11... | collective-permute-start | bytes 3932168 | tf_op jit(solution)/shard_map/ppermute | solution.py:23
  102.4 1.0 copy-start.5
  120.5 7.5 %copy-start.1 = (bf16[640,1280]{1,0:T(8,128)(2,1)S(1)}, bf16[640,1280]{1,0:T(8,128)(2,1)}, u32[]{:S(2)}) copy-start(bf16[640,1280]{1,0:T(8,128)(2,1)} %param.22) | copy-start | bytes 4915204
  120.5 3.2 %collective-permute-start.7 = (bf16[1,512,1280]{2,1,0:T(8,128)(2,1)}, bf16[1,512,1280]{2,1,0:T(8,128)(2,1)S(1)}, u32[]{:S(2)}, u32[]{:S(2)}) collective-permute-start(bf16[1,512,1280]{2,1,0:T(8,128)(2,1)} %bitcast.98), channel_id=1, source_target_pairs={{0,1},{1,0},{2,3},{3,2},{4,5},{5,4},{6,7},{7,6},{8,9},{9,8},{10,11... | collective-permute-start | bytes 3932168 | tf_op jit(solution)/shard_map/ppermute | solution.py:155

commit v3 on v1

--- a/solution.py
+++ b/solution.py
@@ -105,30 +105,63 @@
     )(residual, mine, other, merge_weight)
 
 
-def attend(normed, allowed, attend_in, attend_out):
-    batch, length, width = normed.shape
-    projected = jnp.einsum(
-        "bld,dkf->blkf", normed, attend_in, preferred_element_type=jnp.float32
-    ).astype(jnp.bfloat16)
-    projected = projected.reshape(batch, length, 3, -1, HEAD_DIM)
-    queries = projected[:, :, 0]
-    key_rows = projected[:, :, 1]
-    value_rows = projected[:, :, 2]
-    scores = jnp.einsum(
-        "bqhd,bkhd->bhqk", queries, key_rows, preferred_element_type=jnp.float32
-    ) * HEAD_DIM ** (-0.5)
-    scores = jnp.where(allowed[:, None], scores, jnp.float32(-1e30))
-    probs = jax.nn.softmax(scores, axis=-1).astype(jnp.bfloat16)
-    mixed = jnp.einsum(
-        "bhqk,bkhd->bqhd", probs, value_rows, preferred_element_type=jnp.float32
-    ).astype(jnp.bfloat16)
-    return jnp.dot(mixed.reshape(batch, length, -1), attend_out, preferred_element_type=jnp.float32)
-
-
-def layer(inputs, allowed, attend_in, attend_out, expand, contract, gain_first, gain_second, split=False):
+def _attention_kernel(causal, q_ref, k_ref, v_ref, valid_ref, o_ref, acc_ref):
+    length, width = q_ref.shape[2], q_ref.shape[3]
+    window = 256
+    keys = valid_ref[0] > 0
+    if causal:
+        row = lax.broadcasted_iota(jnp.int32, (length, length), 0)
+        col = lax.broadcasted_iota(jnp.int32, (length, length), 1)
+        allowed = keys & (col <= row)
+    else:
+        allowed = jnp.broadcast_to(keys, (length, length))
+    acc_ref[...] = jnp.zeros_like(acc_ref)
+    for h in range(width // HEAD_DIM):
+        start = min((h * HEAD_DIM) // 128 * 128, width - window)
+        lanes = pl.ds(start, window)
+        lane = lax.broadcasted_iota(jnp.int32, (1, window), 1) + start
+        mine = (lane >= h * HEAD_DIM) & (lane < (h + 1) * HEAD_DIM)
+        zero = jnp.zeros((), q_ref.dtype)
+        queries = jnp.where(mine, q_ref[0, 0, :, lanes], zero)
+        scores = lax.dot_general(
+            queries, k_ref[0, 0, :, lanes], (((1,), (1,)), ((), ())),
+            preferred_element_type=jnp.float32,
+        ) * HEAD_DIM ** (-0.5)
+        scores = jnp.where(allowed, scores, jnp.float32(-1e30))
+        top = jnp.max(scores, axis=-1, keepdims=True)
+        raised = jnp.exp(scores - top)
+        probs = (raised / jnp.sum(raised, axis=-1, keepdims=True)).astype(jnp.bfloat16)
+        values = jnp.where(mine, v_ref[0, 0, :, lanes], zero)
+        acc_ref[:, lanes] += jnp.dot(probs, values, preferred_element_type=jnp.float32)
+    o_ref[0] = acc_ref[...].astype(o_ref.dtype)
+
+
+def attend(projected, key_valid, causal, attend_out):
+    batch, _, length, width = projected.shape
+    part = lambda j: pl.BlockSpec((1, 1, length, width), lambda b: (b, j, 0, 0))
+    mixed = pl.pallas_call(
+        functools.partial(_attention_kernel, causal),
+        out_shape=jax.ShapeDtypeStruct((batch, length, width), jnp.bfloat16),
+        grid=(batch,),
+        in_specs=[part(0), part(1), part(2), pl.BlockSpec((1, 1, length), lambda b: (b, 0, 0))],
+        out_specs=pl.BlockSpec((1, length, width), lambda b: (b, 0, 0)),
+        scratch_shapes=[pltpu.VMEM((length, width), jnp.float32)],
+        cost_estimate=pl.CostEstimate(
+            flops=4 * batch * length * length * 256 * (width // HEAD_DIM),
+            transcendentals=batch * length * length * (width // HEAD_DIM),
+            bytes_accessed=2 * 4 * batch * length * width,
+        ),
+    )(projected, projected, projected, key_valid.astype(jnp.int32).reshape(batch, 1, length))
+    return jnp.dot(mixed, attend_out, preferred_element_type=jnp.float32)
+
+
+def layer(inputs, key_valid, causal, attend_in, attend_out, expand, contract, gain_first, gain_second, split=False):
     widened = inputs.astype(jnp.float32)
     first = lax.optimization_barrier(normalize(widened, gain_first).astype(jnp.bfloat16))
-    attended = attend(first, allowed, attend_in, attend_out)
+    projected = jnp.einsum(
+        "bld,dkf->bklf", first, attend_in, preferred_element_type=jnp.float32
+    ).astype(jnp.bfloat16)
+    attended = attend(projected, key_valid, causal, attend_out)
     residual = widened + tensor_sum(attended)
     second = normalize(residual, gain_second).astype(jnp.bfloat16)
     batch, length, width = second.shape
@@ -171,10 +204,10 @@
     cell_valid = ((cells // side)[None, :] < local_grids[:, 0:1]) & (
         (cells % side)[None, :] < local_grids[:, 1:2]
     )
-    image_allowed = jnp.broadcast_to(cell_valid[:, None, :], (images_here, cell_count, cell_count))
     residual, mine, other = layer(
         patches,
-        image_allowed,
+        cell_valid,
+        False,
         encoder_attend_in,
         encoder_attend_out,
         encoder_expand,
@@ -219,12 +252,10 @@
     prompt_valid = jnp.concatenate(
         [merged_valid.reshape(-1), jnp.ones((text_count,), bool)], axis=0
     )
-    length = prompt.shape[1]
-    positions = jnp.arange(length)
-    prompt_allowed = (prompt_valid[None, :] & (positions[None, :] <= positions[:, None]))[None]
     decoded = layer(
         prompt,
-        prompt_allowed,
+        prompt_valid[None],
+        True,
         decoder_attend_in,
         decoder_attend_out,
         decoder_expand,

time: 126 us -> 116 us (0.921)
  matrix products: 31.2 us -> 18.1 us
  Pallas kernels: 36.3 us -> 47.4 us
  local copies, waits for them, and re-layouts: 12 us -> 4 us
    pallas_call x0 -> x2, Pallas kernels: none -> 11.1 us  [attend(): pl.pallas_call(functools.partial(_attention_kernel, causal), out_shape=ja...]
    sub x1 -> x0, matrix products: 7.69 us -> none  [attend(): probs = jax.nn.softmax(scores, axis=-1).astype(jnp.bfloat16)]
    dot_general x7 -> x4, matrix products: 23.5 us -> 18.1 us  [the longest x2 13 us: layer(): jnp.einsum('bld,dkf->bklf', first, attend_in, preferred_element_type=jnp....]
    convert_element_type x1 -> x0, local copies, waits for them, and re-layouts: 3.98 us -> none  [attend(): projected = jnp.einsum('bld,dkf->blkf', normed, attend_in, preferred_elem...]
    reshape x1 -> x0, local copies, waits for them, and re-layouts: 3.98 us -> none  [attend(): projected = projected.reshape(batch, length, 3, -1, HEAD_DIM)]
    sub x1 -> x0, other arithmetic: 1.53 us -> none  [attend(): probs = jax.nn.softmax(scores, axis=-1).astype(jnp.bfloat16)]
where the time goes in v3:
time: 116 us
  Pallas kernels  47.4 us (41%)
  matrix products  18.1 us (16%)
  other arithmetic  16.6 us (14%)
  starting transfers between devices  13.9 us (12%)
  waiting for transfers between devices  13.5 us (12%)
  local copies, waits for them, and re-layouts  4 us (3%)
  between operations  2.21 us (2%)
    pallas_call x2, Pallas kernels, feed_forward(): pl.pallas_call(functools.partial(_feed_forward_kernel, rows_per_step), ou...  27.9 us
    dot_general x2, matrix products, layer(): jnp.einsum('bld,dkf->bklf', first, attend_in, preferred_element_type=jnp....  13 us
    pallas_call x2, Pallas kernels, attend(): pl.pallas_call(functools.partial(_attention_kernel, causal), out_shape=ja...  11.1 us
    pallas_call x1, Pallas kernels, merge(): pl.pallas_call(_merge_kernel, out_shape=jax.ShapeDtypeStruct((images, hal...  8.45 us
    ppermute x4, starting transfers between devices, on_device(): halves.append(lax.ppermute(merged[j], ('req', 'tensor'), perm))  7.67 us
    ppermute x2, starting transfers between devices, tensor_sum(): other = lax.ppermute(mine, 'tensor', [(0, 1), (1, 0)])  5.53 us
    ppermute x2, waiting for transfers between devices, tensor_sum(): other = lax.ppermute(mine, 'tensor', [(0, 1), (1, 0)])  5.32 us
    ppermute x4, waiting for transfers between devices, on_device(): halves.append(lax.ppermute(merged[j], ('req', 'tensor'), perm))  5.27 us
  transfers between devices with their start and end apart: 8, of which 5 were waited for; matrix products, arithmetic and copies ran while one was open for 1% of the time, Pallas kernels for 0%

profile of v3, /device:TPU:1, one launch (start us, length us, event | category | flops | bytes accessed | tf_op | source)
XLA Modules:
  0.0 115.7 jit_solution(2412498149504592895)
XLA Ops:
  0.0 0.0 copy-start
  0.0 0.9 constant_dynamic-slice_fusion
  0.9 1.6 %convert_reduce_fusion.1 = f32[2,256]{1,0:T(2,128)S(1)} fusion(bf16[2,256,1280]{2,1,0:T(8,128)(2,1)} %param.17), kind=kLoop, calls=%fused_computation.7 | loop fusion | flops 1310208 | bytes 1312768 | tf_op jit(solution)/shard_map/reduce_sum | solution.py:16
  2.5 1.8 %fusion.10 = f32[2,256]{1,0:T(2,128)S(1)} fusion(bf16[2,256,1280]{2,1,0:T(8,128)(2,1)} %param.17, f32[2,256]{1,0:T(2,128)S(1)} %broadcast_multiply_fusion.3), kind=kLoop, calls=%fused_computation.18 | loop fusion | flops 2620928 | bytes 1314816 | tf_op jit(solution)/shard_map/reduce_sum | solution.py:17
  4.3 0.0 copy-done.4
  4.3 0.0 copy-done.8
  4.3 0.5 fusion.12
  4.8 6.5 %convert_bitcast_fusion.1.q_ref.k_ref.v_ref = bf16[2,3,256,640]{3,2,1,0:T(8,128)(2,1)} fusion(bf16[1280,3,640]{2,0,1:T(8,128)(2,1)} %param.21, bf16[2,256,1280]{2,1,0:T(8,128)(2,1)S(1)} %fusion.12), kind=kOutput, calls=%fused_computation.27 | convolution fusion | flops 2517565440 | bytes 8192000 | tf_op jit(solution)/shard_map/bld,dkf->bklf/dot_general | solution.py:161
  11.3 0.6 and_convert_fusion.valid_ref
  12.0 5.4 %shard_map.163 = bf16[2,256,640]{2,1,0:T(8,128)(2,1)} custom-call(bf16[2,3,256,640]{3,2,1,0:T(8,128)(2,1)} %convert_bitcast_fusion.1.q_ref.k_ref.v_ref, bf16[2,3,256,640]{3,2,1,0:T(8,128)(2,1)} %convert_bitcast_fusion.1.q_ref.k_ref.v_ref, bf16[2,3,256,640]{3,2,1,0:T(8,128)(2,1)} %convert_bitcast_fusion.1.q_ref.k_ref.v_ref, ...), custom_call_target="tpu_custom_call" | custom-call | flops 1073741824 | bytes 2621440 | tf_op jit(solution)/shard_map/pallas_call | solution.py:142
  17.3 0.0 copy-done
  17.3 2.3 %convolution_convert_fusion.1 = bf16[2,256,1280]{2,1,0:T(8,128)(2,1)S(1)} fusion(bf16[2,256,640]{2,1,0:T(8,128)(2,1)} %shard_map.163, bf16[640,1280]{1,0:T(8,128)(2,1)S(1)} %copy-done), kind=kOutput, calls=%fused_computation.13 | convolution fusion | flops 839516160 | bytes 3604480 | tf_op jit(solution)/shard_map/dot_general | solution.py:155
  19.6 3.3 %collective-permute-start = (bf16[2,256,1280]{2,1,0:T(8,128)(2,1)S(1)}, bf16[2,256,1280]{2,1,0:T(8,128)(2,1)S(1)}, u32[]{:S(2)}, u32[]{:S(2)}) collective-permute-start(bf16[2,256,1280]{2,1,0:T(8,128)(2,1)S(1)} %convolution_convert_fusion.1), channel_id=1, source_target_pairs={{0,1},{1,0},{2,3},{3,2},{4,5},{5,4},{6,7},{7,6},{8,9},{9,8},{10,11... | collective-permute-start | bytes 3932168 | tf_op jit(solution)/shard_map/ppermute | solution.py:23
  22.9 2.7 %collective-permute-done = bf16[2,256,1280]{2,1,0:T(8,128)(2,1)S(1)} collective-permute-done((bf16[2,256,1280]{2,1,0:T(8,128)(2,1)S(1)}, bf16[2,256,1280]{2,1,0:T(8,128)(2,1)S(1)}, u32[]{:S(2)}, u32[]{:S(2)}) %collective-permute-start) | collective-permute-done | bytes 1310752 | tf_op jit(solution)/shard_map/ppermute | solution.py:23
  25.6 0.6 fusion.27
  26.2 0.0 copy-start.9
  26.2 0.4 multiply_reduce_fusion.1
  26.6 0.3 copy-done.9
  26.9 1.5 %multiply_convert_fusion.1 = bf16[2,256,1280]{2,1,0:T(8,128)(2,1)} fusion(f32[2,256,1280]{2,1,0:T(8,128)S(1)} %get-tuple-element.6.res_ref, f32[1280]{0:T(1024)S(1)} %copy-done.9, f32[2,256]{1,0:T(2,128)S(1)} %add_rsqrt_fusion.2, f32[2,256]{1,0:T(2,128)S(1)} %broadcast_multiply_fusion.2), kind=kLoop, calls=%fused_computation.24 | loop fusion | flops 2621440 | bytes 3941376 | tf_op jit(solution)/shard_map/convert_element_type | solution.py:166
  28.3 0.0 copy-done.3
  28.4 14.0 %shard_map.164 = bf16[512,1280]{1,0:T(8,128)(2,1)} custom-call(bf16[512,1280]{1,0:T(8,128)(2,1)} %bitcast.57, bf16[1280,2560]{1,0:T(8,128)(2,1)} %w1_ref.2, bf16[2560,1280]{1,0:T(8,128)(2,1)} %w2_ref.2), custom_call_target="tpu_custom_call" | custom-call | flops 6710886400 | bytes 15728640 | tf_op jit(solution)/shard_map/pallas_call | solution.py:50
  42.3 0.4 collective-permute-start.1
  42.7 0.0 copy-done.13
  42.7 0.6 dynamic_slice.12
  45.2 0.0 copy-done.12
  45.2 0.1 constant_dynamic-slice_fusion.2
  45.3 0.1 add_select_fusion
  45.4 0.1 compare_and_fusion
  45.5 0.1 and.78
  45.6 0.0 collective-permute-done.1.other_ref
  45.6 1.1 copy-done.7
  46.6 8.5 %shard_map.165 = bf16[2,64,640]{2,1,0:T(8,128)(2,1)} custom-call(f32[2,256,1280]{2,1,0:T(8,128)} %copy-done.3, bf16[2,256,1280]{2,1,0:T(8,128)(2,1)} %bitcast.56, bf16[2,256,1280]{2,1,0:T(8,128)(2,1)} %copy-done.7, bf16[5120,640]{1,0:T(8,128)(2,1)} %w_ref.1), custom_call_target="tpu_custom_call" | custom-call | flops 922746880 | bytes 11796480 | tf_op jit(solution)/shard_map/pallas_call | solution.py:97
  55.1 1.0 slice_bitcast_fusion.1
  56.0 5.7 %collective-permute-start.3 = (bf16[64,640]{1,0:T(8,128)(2,1)S(1)}, bf16[64,640]{1,0:T(8,128)(2,1)S(1)}, u32[]{:S(2)}, u32[]{:S(2)}) collective-permute-start(bf16[64,640]{1,0:T(8,128)(2,1)S(1)} %get-tuple-element.9), channel_id=1, source_target_pairs={{0,129},{1,128},{2,131},{3,130},{4,133},{5,132},{6,135},{7,134},{8... | collective-permute-start | bytes 245768 | tf_op jit(solution)/shard_map/ppermute | solution.py:230
  61.8 0.1 collective-permute-start.2
  61.9 0.6 fusion.28
  62.5 1.5 %collective-permute-start.5 = (bf16[64,640]{1,0:T(8,128)(2,1)S(1)}, bf16[64,640]{1,0:T(8,128)(2,1)S(1)}, u32[]{:S(2)}, u32[]{:S(2)}) collective-permute-start(bf16[64,640]{1,0:T(8,128)(2,1)S(1)} %get-tuple-element.10), channel_id=1, source_target_pairs={{0,3},{1,2},{2,1},{3,0},{4,7},{5,6},{6,5},{7,4},{8,11},{9,10},{10,... | collective-permute-start | bytes 245768 | tf_op jit(solution)/shard_map/ppermute | solution.py:230
  63.9 0.4 collective-permute-start.4
  64.3 0.4 collective-permute-done.3
  64.7 4.9 %collective-permute-done.2 = bf16[64,640]{1,0:T(8,128)(2,1)S(1)} collective-permute-done((bf16[64,640]{1,0:T(8,128)(2,1)S(1)}, bf16[64,640]{1,0:T(8,128)(2,1)S(1)}, u32[]{:S(2)}, u32[]{:S(2)}) %collective-permute-start.2) | collective-permute-done | bytes 81952 | tf_op jit(solution)/shard_map/ppermute | solution.py:230
  69.6 0.0 collective-permute-done.5
  69.6 0.0 collective-permute-done.4
  69.6 0.1 fusion.21
  69.7 0.0 copy-done.2
  69.7 0.2 convert_reduce_fusion
  70.0 0.5 fusion.7
  70.5 0.0 copy-done.10
  70.5 0.5 fusion.9
  70.9 6.5 %convert_bitcast_fusion.q_ref.k_ref.v_ref = bf16[1,3,512,640]{3,2,1,0:T(8,128)(2,1)} fusion(bf16[1280,3,640]{2,0,1:T(8,128)(2,1)} %param.28, bf16[1,512,1280]{2,1,0:T(8,128)(2,1)S(1)} %fusion.9), kind=kOutput, calls=%fused_computation.26 | convolution fusion | flops 2517565440 | bytes 8192000 | tf_op jit(solution)/shard_map/bld,dkf->bklf/dot_general | solution.py:161
  77.4 5.8 %shard_map.166 = bf16[1,512,640]{2,1,0:T(8,128)(2,1)} custom-call(bf16[1,3,512,640]{3,2,1,0:T(8,128)(2,1)} %convert_bitcast_fusion.q_ref.k_ref.v_ref, bf16[1,3,512,640]{3,2,1,0:T(8,128)(2,1)} %convert_bitcast_fusion.q_ref.k_ref.v_ref, bf16[1,3,512,640]{3,2,1,0:T(8,128)(2,1)} %convert_bitcast_fusion.q_ref.k_ref.v_ref, s32[1,1,512]{2,1,0:T(1,128)} %bitcast.59), custom_call_target="tpu_custom_call" | custom-call | flops 2147483648 | bytes 2621440 | tf_op jit(solution)/shard_map/pallas_call | solution.py:142
  83.2 2.8 %fusion.6 = bf16[1,512,1280]{2,1,0:T(8,128)(2,1)S(1)} fusion(bf16[640,1280]{1,0:T(8,128)(2,1)} %param.29, bf16[1,512,640]{2,1,0:T(8,128)(2,1)} %shard_map.166), kind=kOutput, calls=%fused_computation.14 | convolution fusion | flops 839516160 | bytes 3604480 | tf_op jit(solution)/shard_map/dot_general | solution.py:155
  86.0 0.0 copy-start.5
  86.0 2.2 %collective-permute-start.6 = (bf16[1,512,1280]{2,1,0:T(8,128)(2,1)S(1)}, bf16[1,512,1280]{2,1,0:T(8,128)(2,1)S(1)}, u32[]{:S(2)}, u32[]{:S(2)}) collective-permute-start(bf16[1,512,1280]{2,1,0:T(8,128)(2,1)S(1)} %fusion.6), channel_id=1, source_target_pairs={{0,1},{1,0},{2,3},{3,2},{4,5},{5,4},{6,7},{7,6},{8,9},{9,8},{10,11... | collective-permute-start | bytes 3932168 | tf_op jit(solution)/shard_map/ppermute | solution.py:23
  88.2 2.7 %collective-permute-done.6 = bf16[1,512,1280]{2,1,0:T(8,128)(2,1)S(1)} collective-permute-done((bf16[1,512,1280]{2,1,0:T(8,128)(2,1)S(1)}, bf16[1,512,1280]{2,1,0:T(8,128)(2,1)S(1)}, u32[]{:S(2)}, u32[]{:S(2)}) %collective-permute-start.6) | collective-permute-done | bytes 1310752 | tf_op jit(solution)/shard_map/ppermute | solution.py:23
  90.9 0.6 fusion.26
  91.5 0.8 multiply_reduce_fusion
  92.3 0.0 copy-done.5
  92.3 0.0 copy-done.6
  92.3 0.0 copy-done.11
  92.3 1.8 %fusion.16.x_ref = bf16[512,1280]{1,0:T(8,128)(2,1)} fusion(f32[1280]{0:T(1024)S(1)} %copy-done.11, f32[512]{0:T(512)S(1)} %add_rsqrt_fusion, f32[512]{0:T(512)S(1)} %broadcast_multiply_fusion, bf16[1,512,1280]{2,1,0:T(8,128)(2,1)S(1)} %collective-permute-done.6, bf16[1,512,1280]{2,1,0:T(8,128)(2,1)S(1)} %fusion.6, bf16[1,384,1280]{2,1,0:T(8,128)(2,1)S(1)} %copy-done.2, ...), kind=kLoop, calls=%fused_computation.29 | loop fusion | flops 7864320 | bytes 5252096 | tf_op jit(solution)/shard_map/reshape | solution.py:168
  94.2 13.9 %shard_map.167 = bf16[512,1280]{1,0:T(8,128)(2,1)} custom-call(bf16[512,1280]{1,0:T(8,128)(2,1)} %fusion.16.x_ref, bf16[1280,2560]{1,0:T(8,128)(2,1)} %w1_ref.3, bf16[2560,1280]{1,0:T(8,128)(2,1)} %w2_ref.3), custom_call_target="tpu_custom_call" | custom-call | flops 6710886400 | bytes 15728640 | tf_op jit(solution)/shard_map/pallas_call | solution.py:50
  108.1 0.4 collective-permute-start.7
  108.5 2.9 %collective-permute-done.7 = bf16[1,512,1280]{2,1,0:T(8,128)(2,1)S(1)} collective-permute-done((bf16[1,512,1280]{2,1,0:T(8,128)(2,1)}, bf16[1,512,1280]{2,1,0:T(8,128)(2,1)S(1)}, u32[]{:S(2)}, u32[]{:S(2)}) %collective-permute-start.7) | collective-permute-done | bytes 1310752 | tf_op jit(solution)/shard_map/ppermute | solution.py:170
  111.3 4.3 %fusion.17 = bf16[1,512,1280]{2,1,0:T(8,128)(2,1)} fusion(bf16[1,512,1280]{2,1,0:T(8,128)(2,1)S(1)} %collective-permute-done.7, pred[512]{0:T(512)(128)(4,1)S(1)} %get-tuple-element.19, bf16[512,1280]{1,0:T(8,128)(2,1)} %shard_map.167, bf16[1,512,1280]{2,1,0:T(8,128)(2,1)} %copy-done.6, bf16[1,512,1280]{2,1,0:T(8,128)(2,1)} %copy-done.5, ...), kind=kLoop, calls=%fused_computation.30 | loop fusion | flops 9175040 | bytes 7864832 | tf_op jit(solution)/shard_map/jit(_where)/select_n | solution.py:266
  (26 shorter events, 0.1 us)
Async XLA Ops:
  0.0 17.3 %copy-start = (bf16[640,1280]{1,0:T(8,128)(2,1)S(1)}, bf16[640,1280]{1,0:T(8,128)(2,1)}, u32[]{:S(2)}) copy-start(bf16[640,1280]{1,0:T(8,128)(2,1)} %param.22) | copy-start | bytes 4915204
  0.0 4.3 %copy-start.4 = (bf16[2,256,1280]{2,1,0:T(8,128)(2,1)S(1)}, bf16[2,256,1280]{2,1,0:T(8,128)(2,1)}, u32[]{:S(2)}) copy-start(bf16[2,256,1280]{2,1,0:T(8,128)(2,1)} %param.17) | copy-start | bytes 3932164
  0.0 4.3 %copy-start.8 = (f32[1280]{0:T(1024)S(1)}, f32[1280]{0:T(1024)}, u32[]{:S(2)}) copy-start(f32[1280]{0:T(1024)} %param.25) | copy-start | bytes 15364
  19.6 6.0 %collective-permute-start = (bf16[2,256,1280]{2,1,0:T(8,128)(2,1)S(1)}, bf16[2,256,1280]{2,1,0:T(8,128)(2,1)S(1)}, u32[]{:S(2)}, u32[]{:S(2)}) collective-permute-start(bf16[2,256,1280]{2,1,0:T(8,128)(2,1)S(1)} %convolution_convert_fusion.1), channel_id=1, source_target_pairs={{0,1},{1,0},{2,3},{3,2},{4,5},{5,4},{6,7},{7,6},{8,9},{9,8},{10,11... | collective-permute-start | bytes 3932168 | tf_op jit(solution)/shard_map/ppermute | solution.py:23
  26.2 2.2 %copy-start.3 = (f32[2,256,1280]{2,1,0:T(8,128)}, f32[2,256,1280]{2,1,0:T(8,128)S(1)}, u32[]{:S(2)}) copy-start(f32[2,256,1280]{2,1,0:T(8,128)S(1)} %get-tuple-element.6.res_ref) | copy-start | bytes 7864324
  26.2 0.7 copy-start.9
  28.3 14.3 %copy-start.13 = (s32[256]{0:T(256)S(1)}, s32[256]{0:T(256)}, u32[]{:S(2)}) copy-start(s32[256]{0:T(256)} %param.19) | copy-start | bytes 3076
  28.4 16.9 %copy-start.12 = (s32[256,2]{0,1:T(2,128)S(1)}, s32[256,2]{0,1:T(2,128)}, u32[]{:S(2)}) copy-start(s32[256,2]{0,1:T(2,128)} %param.18) | copy-start | bytes 6148
  42.3 3.3 %collective-permute-start.1 = (bf16[2,256,1280]{2,1,0:T(8,128)(2,1)}, bf16[2,256,1280]{2,1,0:T(8,128)(2,1)S(1)}, u32[]{:S(2)}, u32[]{:S(2)}) collective-permute-start(bf16[2,256,1280]{2,1,0:T(8,128)(2,1)} %bitcast.55), channel_id=1, source_target_pairs={{0,1},{1,0},{2,3},{3,2},{4,5},{5,4},{6,7},{7,6},{8,9},{9,8},{10,11... | collective-permute-start | bytes 3932168 | tf_op jit(solution)/shard_map/ppermute | solution.py:170
  45.6 24.1 %copy-start.2 = (bf16[1,384,1280]{2,1,0:T(8,128)(2,1)S(1)}, bf16[1,384,1280]{2,1,0:T(8,128)(2,1)}, u32[]{:S(2)}) copy-start(bf16[1,384,1280]{2,1,0:T(8,128)(2,1)} %param.20) | copy-start | bytes 2949124
  45.6 1.1 copy-start.7
  55.1 15.4 %copy-start.10 = (f32[1280]{0:T(1024)S(1)}, f32[1280]{0:T(1024)}, u32[]{:S(2)}) copy-start(f32[1280]{0:T(1024)} %param.32) | copy-start | bytes 15364
  56.0 8.7 %collective-permute-start.3 = (bf16[64,640]{1,0:T(8,128)(2,1)S(1)}, bf16[64,640]{1,0:T(8,128)(2,1)S(1)}, u32[]{:S(2)}, u32[]{:S(2)}) collective-permute-start(bf16[64,640]{1,0:T(8,128)(2,1)S(1)} %get-tuple-element.9), channel_id=1, source_target_pairs={{0,129},{1,128},{2,131},{3,130},{4,133},{5,132},{6,135},{7,134},{8... | collective-permute-start | bytes 245768 | tf_op jit(solution)/shard_map/ppermute | solution.py:230
  61.8 7.8 %collective-permute-start.2 = (bf16[64,640]{1,0:T(8,128)(2,1)S(1)}, bf16[64,640]{1,0:T(8,128)(2,1)S(1)}, u32[]{:S(2)}, u32[]{:S(2)}) collective-permute-start(bf16[64,640]{1,0:T(8,128)(2,1)S(1)} %get-tuple-element.9), channel_id=1, source_target_pairs={{0,128},{1,129},{2,130},{3,131},{4,132},{5,133},{6,134},{7,135},{8... | collective-permute-start | bytes 245768 | tf_op jit(solution)/shard_map/ppermute | solution.py:230
  62.5 7.1 %collective-permute-start.5 = (bf16[64,640]{1,0:T(8,128)(2,1)S(1)}, bf16[64,640]{1,0:T(8,128)(2,1)S(1)}, u32[]{:S(2)}, u32[]{:S(2)}) collective-permute-start(bf16[64,640]{1,0:T(8,128)(2,1)S(1)} %get-tuple-element.10), channel_id=1, source_target_pairs={{0,3},{1,2},{2,1},{3,0},{4,7},{5,6},{6,5},{7,4},{8,11},{9,10},{10,... | collective-permute-start | bytes 245768 | tf_op jit(solution)/shard_map/ppermute | solution.py:230
  63.9 5.7 %collective-permute-start.4 = (bf16[64,640]{1,0:T(8,128)(2,1)S(1)}, bf16[64,640]{1,0:T(8,128)(2,1)S(1)}, u32[]{:S(2)}, u32[]{:S(2)}) collective-permute-start(bf16[64,640]{1,0:T(8,128)(2,1)S(1)} %get-tuple-element.10), channel_id=1, source_target_pairs={{0,2},{1,3},{2,0},{3,1},{4,6},{5,7},{6,4},{7,5},{8,10},{9,11},{10,... | collective-permute-start | bytes 245768 | tf_op jit(solution)/shard_map/ppermute | solution.py:230
  86.0 6.3 %copy-start.5 = (bf16[1,512,1280]{2,1,0:T(8,128)(2,1)}, bf16[1,512,1280]{2,1,0:T(8,128)(2,1)S(1)}, u32[]{:S(2)}) copy-start(bf16[1,512,1280]{2,1,0:T(8,128)(2,1)S(1)} %fusion.6) | copy-start | bytes 3932164
  86.0 4.9 %collective-permute-start.6 = (bf16[1,512,1280]{2,1,0:T(8,128)(2,1)S(1)}, bf16[1,512,1280]{2,1,0:T(8,128)(2,1)S(1)}, u32[]{:S(2)}, u32[]{:S(2)}) collective-permute-start(bf16[1,512,1280]{2,1,0:T(8,128)(2,1)S(1)} %fusion.6), channel_id=1, source_target_pairs={{0,1},{1,0},{2,3},{3,2},{4,5},{5,4},{6,7},{7,6},{8,9},{9,8},{10,11... | collective-permute-start | bytes 3932168 | tf_op jit(solution)/shard_map/ppermute | solution.py:23
  90.9 1.4 %copy-start.6 = (bf16[1,512,1280]{2,1,0:T(8,128)(2,1)}, bf16[1,512,1280]{2,1,0:T(8,128)(2,1)S(1)}, u32[]{:S(2)}) copy-start(bf16[1,512,1280]{2,1,0:T(8,128)(2,1)S(1)} %collective-permute-done.6) | copy-start | bytes 3932164
  91.5 0.8 copy-start.11
  108.1 3.3 %collective-permute-start.7 = (bf16[1,512,1280]{2,1,0:T(8,128)(2,1)}, bf16[1,512,1280]{2,1,0:T(8,128)(2,1)S(1)}, u32[]{:S(2)}, u32[]{:S(2)}) collective-permute-start(bf16[1,512,1280]{2,1,0:T(8,128)(2,1)} %bitcast.58), channel_id=1, source_target_pairs={{0,1},{1,0},{2,3},{3,2},{4,5},{5,4},{6,7},{7,6},{8,9},{9,8},{10,11... | collective-permute-start | bytes 3932168 | tf_op jit(solution)/shard_map/ppermute | solution.py:170
  111.3 4.3 %copy-start.1 = (bf16[640,1280]{1,0:T(8,128)(2,1)S(1)}, bf16[640,1280]{1,0:T(8,128)(2,1)}, u32[]{:S(2)}) copy-start(bf16[640,1280]{1,0:T(8,128)(2,1)} %param.22) | copy-start | bytes 4915204

commit v4 on v3

--- a/solution.py
+++ b/solution.py
@@ -105,9 +105,15 @@
     )(residual, mine, other, merge_weight)
 
 
-def _attention_kernel(causal, q_ref, k_ref, v_ref, valid_ref, o_ref, acc_ref):
-    length, width = q_ref.shape[2], q_ref.shape[3]
+def _attention_kernel(causal, x_ref, gain_ref, w_ref, valid_ref, o_ref, q_ref, k_ref, v_ref, acc_ref):
+    length, width = q_ref.shape
     window = 256
+    values = x_ref[0].astype(jnp.float32)
+    center = values - jnp.mean(values, axis=-1, keepdims=True)
+    spread = jnp.mean(center * center, axis=-1, keepdims=True)
+    first = (center * lax.rsqrt(spread + 1e-06) * gain_ref[...]).astype(jnp.bfloat16)
+    for j, ref in enumerate((q_ref, k_ref, v_ref)):
+        ref[...] = jnp.dot(first, w_ref[j], preferred_element_type=jnp.float32).astype(ref.dtype)
     keys = valid_ref[0] > 0
     if causal:
         row = lax.broadcasted_iota(jnp.int32, (length, length), 0)
@@ -122,46 +128,54 @@
         lane = lax.broadcasted_iota(jnp.int32, (1, window), 1) + start
         mine = (lane >= h * HEAD_DIM) & (lane < (h + 1) * HEAD_DIM)
         zero = jnp.zeros((), q_ref.dtype)
-        queries = jnp.where(mine, q_ref[0, 0, :, lanes], zero)
+        queries = jnp.where(mine, q_ref[:, lanes], zero)
         scores = lax.dot_general(
-            queries, k_ref[0, 0, :, lanes], (((1,), (1,)), ((), ())),
+            queries, k_ref[:, lanes], (((1,), (1,)), ((), ())),
             preferred_element_type=jnp.float32,
         ) * HEAD_DIM ** (-0.5)
         scores = jnp.where(allowed, scores, jnp.float32(-1e30))
         top = jnp.max(scores, axis=-1, keepdims=True)
         raised = jnp.exp(scores - top)
         probs = (raised / jnp.sum(raised, axis=-1, keepdims=True)).astype(jnp.bfloat16)
-        values = jnp.where(mine, v_ref[0, 0, :, lanes], zero)
-        acc_ref[:, lanes] += jnp.dot(probs, values, preferred_element_type=jnp.float32)
+        values_h = jnp.where(mine, v_ref[:, lanes], zero)
+        acc_ref[:, lanes] += jnp.dot(probs, values_h, preferred_element_type=jnp.float32)
     o_ref[0] = acc_ref[...].astype(o_ref.dtype)
 
 
-def attend(projected, key_valid, causal, attend_out):
-    batch, _, length, width = projected.shape
-    part = lambda j: pl.BlockSpec((1, 1, length, width), lambda b: (b, j, 0, 0))
+def attend(inputs, gain_first, attend_in, key_valid, causal, attend_out):
+    batch, length, model_width = inputs.shape
+    width = attend_in.shape[2]
+    weight = jnp.transpose(attend_in, (1, 0, 2))
     mixed = pl.pallas_call(
         functools.partial(_attention_kernel, causal),
         out_shape=jax.ShapeDtypeStruct((batch, length, width), jnp.bfloat16),
         grid=(batch,),
-        in_specs=[part(0), part(1), part(2), pl.BlockSpec((1, 1, length), lambda b: (b, 0, 0))],
+        in_specs=[
+            pl.BlockSpec((1, length, model_width), lambda b: (b, 0, 0)),
+            pl.BlockSpec((1, model_width), lambda b: (0, 0)),
+            pl.BlockSpec((3, model_width, width), lambda b: (0, 0, 0)),
+            pl.BlockSpec((1, 1, length), lambda b: (b, 0, 0)),
+        ],
         out_specs=pl.BlockSpec((1, length, width), lambda b: (b, 0, 0)),
-        scratch_shapes=[pltpu.VMEM((length, width), jnp.float32)],
+        scratch_shapes=[pltpu.VMEM((length, width), jnp.bfloat16)] * 3
+        + [pltpu.VMEM((length, width), jnp.float32)],
         cost_estimate=pl.CostEstimate(
-            flops=4 * batch * length * length * 256 * (width // HEAD_DIM),
+            flops=batch * length * (6 * model_width * width + 4 * length * 256 * (width // HEAD_DIM)),
             transcendentals=batch * length * length * (width // HEAD_DIM),
-            bytes_accessed=2 * 4 * batch * length * width,
+            bytes_accessed=2 * (batch * length * (model_width + width) + 3 * model_width * width),
         ),
-    )(projected, projected, projected, key_valid.astype(jnp.int32).reshape(batch, 1, length))
+    )(
+        inputs,
+        gain_first.reshape(1, model_width),
+        weight,
+        key_valid.astype(jnp.int32).reshape(batch, 1, length),
+    )
     return jnp.dot(mixed, attend_out, preferred_element_type=jnp.float32)
 
 
 def layer(inputs, key_valid, causal, attend_in, attend_out, expand, contract, gain_first, gain_second, split=False):
     widened = inputs.astype(jnp.float32)
-    first = lax.optimization_barrier(normalize(widened, gain_first).astype(jnp.bfloat16))
-    projected = jnp.einsum(
-        "bld,dkf->bklf", first, attend_in, preferred_element_type=jnp.float32
-    ).astype(jnp.bfloat16)
-    attended = attend(projected, key_valid, causal, attend_out)
+    attended = attend(inputs, gain_first, attend_in, key_valid, causal, attend_out)
     residual = widened + tensor_sum(attended)
     second = normalize(residual, gain_second).astype(jnp.bfloat16)
     batch, length, width = second.shape

time: 116 us -> 110 us (0.948)
  matrix products: 18.1 us -> 5.2 us
  Pallas kernels: 47.4 us -> 57 us
  other arithmetic: 16.6 us -> 12.7 us
  local copies, waits for them, and re-layouts: 4 us -> 5.84 us
    dot_general x2 -> x0, matrix products: 13 us -> none  [layer(): jnp.einsum('bld,dkf->bklf', first, attend_in, preferred_element_type=jnp....]
    pallas_call x2, Pallas kernels: 11.1 us -> 20.6 us  [attend(): pl.pallas_call(functools.partial(_attention_kernel, causal), out_shape=ja...]
    reduce_sum x4 -> x2, other arithmetic: 3.45 us -> 1.17 us  [normalize(): spread = jnp.mean(center * center, axis=-1, keepdims=True)]
    reshape x0 -> x2, local copies, waits for them, and re-layouts: none -> 1.89 us  [attend(): gain_first.reshape(1, model_width)]
    reduce_sum x4 -> x2, other arithmetic: 3 us -> 1.19 us  [normalize(): center = values - jnp.mean(values, axis=-1, keepdims=True)]
  transfers between devices with their start and end apart: 8 -> 8, of which waited for: 5 -> 5; matrix products, arithmetic and copies ran while one was open for 1% -> 2% of each run, Pallas kernels for 0% -> 0%
where the time goes in v4:
time: 110 us; the launch traced here: 109 us
  Pallas kernels  57 us (52%)
  waiting for transfers between devices  13.2 us (12%)
  starting transfers between devices  13 us (12%)
  other arithmetic  12.7 us (12%)
  local copies, waits for them, and re-layouts  5.84 us (5%)
  matrix products  5.2 us (5%)
  between operations  2.14 us (2%)
    pallas_call x2, Pallas kernels, feed_forward(): pl.pallas_call(functools.partial(_feed_forward_kernel, rows_per_step), ou...  27.9 us
    pallas_call x2, Pallas kernels, attend(): pl.pallas_call(functools.partial(_attention_kernel, causal), out_shape=ja...  20.6 us
    pallas_call x1, Pallas kernels, merge(): pl.pallas_call(_merge_kernel, out_shape=jax.ShapeDtypeStruct((images, hal...  8.44 us
    ppermute x4, starting transfers between devices, on_device(): halves.append(lax.ppermute(merged[j], ('req', 'tensor'), perm))  7.49 us
    ppermute x2, waiting for transfers between devices, tensor_sum(): other = lax.ppermute(mine, 'tensor', [(0, 1), (1, 0)])  5.32 us
    dot_general x2, matrix products, attend(): return jnp.dot(mixed, attend_out, preferred_element_type=jnp.float32)  5.2 us
    ppermute x4, waiting for transfers between devices, on_device(): halves.append(lax.ppermute(merged[j], ('req', 'tensor'), perm))  4.91 us
    ppermute x2, starting transfers between devices, tensor_sum(): other = lax.ppermute(mine, 'tensor', [(0, 1), (1, 0)])  4.87 us
  transfers between devices with their start and end apart: 8, of which 5 were waited for; matrix products, arithmetic and copies ran while one was open for 2% of the time, Pallas kernels for 0%

profile of v4, /device:TPU:1, one launch (start us, length us, event | category | flops | bytes accessed | tf_op | source)
XLA Modules:
  0.0 109.1 jit_solution(11578237355124214330)
XLA Ops:
  0.0 0.0 copy-start
  0.0 0.9 constant_dynamic-slice_fusion
  0.9 1.3 %reshape.282.gain_ref = f32[1,1280]{1,0:T(1,128)} reshape(f32[1280]{0:T(1024)} %param.25) | data formatting | bytes 10240 | tf_op jit(solution)/shard_map/reshape | solution.py:169
  2.2 0.7 and_convert_fusion.valid_ref
  2.8 9.9 %shard_map.163 = bf16[2,256,640]{2,1,0:T(8,128)(2,1)} custom-call(bf16[2,256,1280]{2,1,0:T(8,128)(2,1)} %x_ref.1, f32[1,1280]{1,0:T(1,128)} %reshape.282.gain_ref, bf16[3,1280,640]{2,1,0:T(8,128)(2,1)} %bitcast.46, s32[2,1,256]{2,1,0:T(1,128)} %and_convert_fusion.valid_ref), custom_call_target="tpu_custom_call" | custom-call | flops 3590324224 | bytes 6881280 | tf_op jit(solution)/shard_map/pallas_call | solution.py:149
  12.7 0.0 copy-done
  12.7 0.0 copy-start.7
  12.7 2.4 %convolution_convert_fusion.1 = bf16[2,256,1280]{2,1,0:T(8,128)(2,1)S(1)} fusion(bf16[2,256,640]{2,1,0:T(8,128)(2,1)} %shard_map.163, bf16[640,1280]{1,0:T(8,128)(2,1)S(1)} %copy-done), kind=kOutput, calls=%fused_computation.1 | convolution fusion | flops 839516160 | bytes 3604480 | tf_op jit(solution)/shard_map/dot_general | solution.py:173
  15.1 3.3 %collective-permute-start = (bf16[2,256,1280]{2,1,0:T(8,128)(2,1)S(1)}, bf16[2,256,1280]{2,1,0:T(8,128)(2,1)S(1)}, u32[]{:S(2)}, u32[]{:S(2)}) collective-permute-start(bf16[2,256,1280]{2,1,0:T(8,128)(2,1)S(1)} %convolution_convert_fusion.1), channel_id=1, source_target_pairs={{0,1},{1,0},{2,3},{3,2},{4,5},{5,4},{6,7},{7,6},{8,9},{9,8},{10,11... | collective-permute-start | bytes 3932168 | tf_op jit(solution)/shard_map/ppermute | solution.py:23
  18.4 2.7 %collective-permute-done = bf16[2,256,1280]{2,1,0:T(8,128)(2,1)S(1)} collective-permute-done((bf16[2,256,1280]{2,1,0:T(8,128)(2,1)S(1)}, bf16[2,256,1280]{2,1,0:T(8,128)(2,1)S(1)}, u32[]{:S(2)}, u32[]{:S(2)}) %collective-permute-start) | collective-permute-done | bytes 1310752 | tf_op jit(solution)/shard_map/ppermute | solution.py:23
  21.1 0.0 copy-done.7
  21.1 0.6 fusion.10
  21.7 0.0 copy-start.2
  21.7 0.0 copy-start.8
  21.7 0.4 multiply_reduce_fusion.1
  22.1 0.3 copy-done.8
  22.4 1.5 %multiply_convert_fusion.1 = bf16[2,256,1280]{2,1,0:T(8,128)(2,1)} fusion(f32[2,256,1280]{2,1,0:T(8,128)S(1)} %get-tuple-element.6.res_ref, f32[1280]{0:T(1024)S(1)} %copy-done.8, f32[2,256]{1,0:T(2,128)S(1)} %add_rsqrt_fusion.1, f32[2,256]{1,0:T(2,128)S(1)} %broadcast_multiply_fusion.1), kind=kLoop, calls=%fused_computation.7 | loop fusion | flops 2621440 | bytes 3941376 | tf_op jit(solution)/shard_map/convert_element_type | solution.py:180
  23.8 0.0 copy-done.2
  23.8 0.0 copy-start.12
  23.9 0.0 copy-start.11
  23.9 0.0 copy-start.10
  23.9 13.9 %shard_map.164 = bf16[512,1280]{1,0:T(8,128)(2,1)} custom-call(bf16[512,1280]{1,0:T(8,128)(2,1)} %bitcast.43, bf16[1280,2560]{1,0:T(8,128)(2,1)} %w1_ref.2, bf16[2560,1280]{1,0:T(8,128)(2,1)} %w2_ref.2), custom_call_target="tpu_custom_call" | custom-call | flops 6710886400 | bytes 15728640 | tf_op jit(solution)/shard_map/pallas_call | solution.py:50
  37.8 0.4 collective-permute-start.1
  38.2 0.0 copy-done.12
  38.2 0.6 dynamic_slice.12
  40.7 0.0 copy-done.11
  40.8 0.1 constant_dynamic-slice_fusion.2
  40.8 0.1 add_select_fusion
  40.9 0.1 compare_and_fusion
  41.0 0.1 and.78
  41.1 0.0 copy-done.10
  41.1 0.6 reshape.285.gain_ref
  41.7 0.0 collective-permute-done.1.other_ref
  41.7 1.1 copy-done.6
  42.8 8.4 %shard_map.165 = bf16[2,64,640]{2,1,0:T(8,128)(2,1)} custom-call(f32[2,256,1280]{2,1,0:T(8,128)} %copy-done.2, bf16[2,256,1280]{2,1,0:T(8,128)(2,1)} %bitcast.42, bf16[2,256,1280]{2,1,0:T(8,128)(2,1)} %copy-done.6, bf16[5120,640]{1,0:T(8,128)(2,1)} %w_ref.1), custom_call_target="tpu_custom_call" | custom-call | flops 922746880 | bytes 11796480 | tf_op jit(solution)/shard_map/pallas_call | solution.py:97
  51.2 0.9 slice_bitcast_fusion.1
  52.1 5.3 %collective-permute-start.3 = (bf16[64,640]{1,0:T(8,128)(2,1)S(1)}, bf16[64,640]{1,0:T(8,128)(2,1)S(1)}, u32[]{:S(2)}, u32[]{:S(2)}) collective-permute-start(bf16[64,640]{1,0:T(8,128)(2,1)S(1)} %get-tuple-element.9), channel_id=1, source_target_pairs={{0,129},{1,128},{2,131},{3,130},{4,133},{5,132},{6,135},{7,134},{8... | collective-permute-start | bytes 245768 | tf_op jit(solution)/shard_map/ppermute | solution.py:244
  57.5 0.2 collective-permute-start.2
  57.7 0.6 fusion.11
  58.2 1.6 %collective-permute-start.5 = (bf16[64,640]{1,0:T(8,128)(2,1)S(1)}, bf16[64,640]{1,0:T(8,128)(2,1)S(1)}, u32[]{:S(2)}, u32[]{:S(2)}) collective-permute-start(bf16[64,640]{1,0:T(8,128)(2,1)S(1)} %get-tuple-element.10), channel_id=1, source_target_pairs={{0,3},{1,2},{2,1},{3,0},{4,7},{5,6},{6,5},{7,4},{8,11},{9,10},{10,... | collective-permute-start | bytes 245768 | tf_op jit(solution)/shard_map/ppermute | solution.py:244
  59.8 0.4 collective-permute-start.4
  60.2 0.2 collective-permute-done.3
  60.4 4.7 %collective-permute-done.2 = bf16[64,640]{1,0:T(8,128)(2,1)S(1)} collective-permute-done((bf16[64,640]{1,0:T(8,128)(2,1)S(1)}, bf16[64,640]{1,0:T(8,128)(2,1)S(1)}, u32[]{:S(2)}, u32[]{:S(2)}) %collective-permute-start.2) | collective-permute-done | bytes 81952 | tf_op jit(solution)/shard_map/ppermute | solution.py:244
  65.1 0.0 collective-permute-done.5
  65.1 0.0 collective-permute-done.4
  65.2 0.1 maximum_select_fusion
  65.3 0.0 copy-done.3
  65.3 1.1 %maximum_bitcast_fusion.x_ref = bf16[1,512,1280]{2,1,0:T(8,128)(2,1)} fusion(bf16[384,1280]{1,0:T(8,128)(2,1)S(1)} %bitcast.36, bf16[128,1280]{1,0:T(8,128)(2,1)S(1)} %maximum_select_fusion), kind=kLoop, calls=%fused_computation.13 | loop fusion | flops 2621440 | bytes 2621440 | tf_op jit(solution)/shard_map/broadcast_in_dim | solution.py:264
  66.4 10.8 %shard_map.166 = bf16[1,512,640]{2,1,0:T(8,128)(2,1)} custom-call(bf16[1,512,1280]{2,1,0:T(8,128)(2,1)} %maximum_bitcast_fusion.x_ref, f32[1,1280]{1,0:T(1,128)} %reshape.285.gain_ref, bf16[3,1280,640]{2,1,0:T(8,128)(2,1)} %bitcast.47, s32[1,1,512]{2,1,0:T(1,128)} %bitcast.45), custom_call_target="tpu_custom_call" | custom-call | flops 4664066048 | bytes 6881280 | tf_op jit(solution)/shard_map/pallas_call | solution.py:149
  77.2 2.8 %fusion = bf16[1,512,1280]{2,1,0:T(8,128)(2,1)S(1)} fusion(bf16[640,1280]{1,0:T(8,128)(2,1)} %param.29, bf16[1,512,640]{2,1,0:T(8,128)(2,1)} %shard_map.166), kind=kOutput, calls=%fused_computation.2 | convolution fusion | flops 839516160 | bytes 3604480 | tf_op jit(solution)/shard_map/dot_general | solution.py:173
  80.0 0.0 copy-start.4
  80.0 1.5 %collective-permute-start.6 = (bf16[1,512,1280]{2,1,0:T(8,128)(2,1)S(1)}, bf16[1,512,1280]{2,1,0:T(8,128)(2,1)S(1)}, u32[]{:S(2)}, u32[]{:S(2)}) collective-permute-start(bf16[1,512,1280]{2,1,0:T(8,128)(2,1)S(1)} %fusion), channel_id=1, source_target_pairs={{0,1},{1,0},{2,3},{3,2},{4,5},{5,4},{6,7},{7,6},{8,9},{9,8},{10,11... | collective-permute-start | bytes 3932168 | tf_op jit(solution)/shard_map/ppermute | solution.py:23
  81.5 2.7 %collective-permute-done.6 = bf16[1,512,1280]{2,1,0:T(8,128)(2,1)S(1)} collective-permute-done((bf16[1,512,1280]{2,1,0:T(8,128)(2,1)S(1)}, bf16[1,512,1280]{2,1,0:T(8,128)(2,1)S(1)}, u32[]{:S(2)}, u32[]{:S(2)}) %collective-permute-start.6) | collective-permute-done | bytes 1310752 | tf_op jit(solution)/shard_map/ppermute | solution.py:23
  84.2 0.6 fusion.9
  84.8 0.8 multiply_reduce_fusion
  85.6 0.0 copy-done.4
  85.6 0.0 copy-done.5
  85.6 0.0 copy-done.9
  85.6 1.8 %fusion.2.x_ref = bf16[512,1280]{1,0:T(8,128)(2,1)} fusion(f32[1280]{0:T(1024)S(1)} %copy-done.9, f32[512]{0:T(512)S(1)} %add_rsqrt_fusion, f32[512]{0:T(512)S(1)} %broadcast_multiply_fusion, bf16[1,512,1280]{2,1,0:T(8,128)(2,1)S(1)} %collective-permute-done.6, bf16[1,512,1280]{2,1,0:T(8,128)(2,1)S(1)} %fusion, bf16[1,384,1280]{2,1,0:T(8,128)(2,1)S(1)} %copy-done.3, ...), kind=kLoop, calls=%fused_computation.11 | loop fusion | flops 7864320 | bytes 5252096 | tf_op jit(solution)/shard_map/reshape | solution.py:182
  87.5 14.0 %shard_map.167 = bf16[512,1280]{1,0:T(8,128)(2,1)} custom-call(bf16[512,1280]{1,0:T(8,128)(2,1)} %fusion.2.x_ref, bf16[1280,2560]{1,0:T(8,128)(2,1)} %w1_ref.3, bf16[2560,1280]{1,0:T(8,128)(2,1)} %w2_ref.3), custom_call_target="tpu_custom_call" | custom-call | flops 6710886400 | bytes 15728640 | tf_op jit(solution)/shard_map/pallas_call | solution.py:50
  101.5 0.3 collective-permute-start.7
  101.8 2.9 %collective-permute-done.7 = bf16[1,512,1280]{2,1,0:T(8,128)(2,1)S(1)} collective-permute-done((bf16[1,512,1280]{2,1,0:T(8,128)(2,1)}, bf16[1,512,1280]{2,1,0:T(8,128)(2,1)S(1)}, u32[]{:S(2)}, u32[]{:S(2)}) %collective-permute-start.7) | collective-permute-done | bytes 1310752 | tf_op jit(solution)/shard_map/ppermute | solution.py:184
  104.7 4.3 %fusion.3 = bf16[1,512,1280]{2,1,0:T(8,128)(2,1)} fusion(bf16[1,512,1280]{2,1,0:T(8,128)(2,1)S(1)} %collective-permute-done.7, pred[512]{0:T(512)(128)(4,1)S(1)} %get-tuple-element.19, bf16[512,1280]{1,0:T(8,128)(2,1)} %shard_map.167, bf16[1,512,1280]{2,1,0:T(8,128)(2,1)} %copy-done.5, bf16[1,512,1280]{2,1,0:T(8,128)(2,1)} %copy-done.4, ...), kind=kLoop, calls=%fused_computation.12 | loop fusion | flops 9175040 | bytes 7864832 | tf_op jit(solution)/shard_map/jit(_where)/select_n | solution.py:280
  109.1 0.0 copy-done.1
  (15 shorter events, 0.1 us)
Async XLA Ops:
  0.0 12.7 %copy-start = (bf16[640,1280]{1,0:T(8,128)(2,1)S(1)}, bf16[640,1280]{1,0:T(8,128)(2,1)}, u32[]{:S(2)}) copy-start(bf16[640,1280]{1,0:T(8,128)(2,1)} %param.22) | copy-start | bytes 4915204
  12.7 8.4 %copy-start.7 = (bf16[2,256,1280]{2,1,0:T(8,128)(2,1)S(1)}, bf16[2,256,1280]{2,1,0:T(8,128)(2,1)}, u32[]{:S(2)}) copy-start(bf16[2,256,1280]{2,1,0:T(8,128)(2,1)} %x_ref.1) | copy-start | bytes 3932164
  15.1 6.0 %collective-permute-start = (bf16[2,256,1280]{2,1,0:T(8,128)(2,1)S(1)}, bf16[2,256,1280]{2,1,0:T(8,128)(2,1)S(1)}, u32[]{:S(2)}, u32[]{:S(2)}) collective-permute-start(bf16[2,256,1280]{2,1,0:T(8,128)(2,1)S(1)} %convolution_convert_fusion.1), channel_id=1, source_target_pairs={{0,1},{1,0},{2,3},{3,2},{4,5},{5,4},{6,7},{7,6},{8,9},{9,8},{10,11... | collective-permute-start | bytes 3932168 | tf_op jit(solution)/shard_map/ppermute | solution.py:23
  21.7 2.2 %copy-start.2 = (f32[2,256,1280]{2,1,0:T(8,128)}, f32[2,256,1280]{2,1,0:T(8,128)S(1)}, u32[]{:S(2)}) copy-start(f32[2,256,1280]{2,1,0:T(8,128)S(1)} %get-tuple-element.6.res_ref) | copy-start | bytes 7864324
  21.7 0.7 copy-start.8
  23.8 14.3 %copy-start.12 = (s32[256]{0:T(256)S(1)}, s32[256]{0:T(256)}, u32[]{:S(2)}) copy-start(s32[256]{0:T(256)} %param.19) | copy-start | bytes 3076
  23.9 16.9 %copy-start.11 = (s32[256,2]{0,1:T(2,128)S(1)}, s32[256,2]{0,1:T(2,128)}, u32[]{:S(2)}) copy-start(s32[256,2]{0,1:T(2,128)} %param.18) | copy-start | bytes 6148
  23.9 17.2 %copy-start.10 = (f32[1280]{0:T(1024)S(1)}, f32[1280]{0:T(1024)}, u32[]{:S(2)}) copy-start(f32[1280]{0:T(1024)} %param.32) | copy-start | bytes 15364
  37.8 3.9 %collective-permute-start.1 = (bf16[2,256,1280]{2,1,0:T(8,128)(2,1)}, bf16[2,256,1280]{2,1,0:T(8,128)(2,1)S(1)}, u32[]{:S(2)}, u32[]{:S(2)}) collective-permute-start(bf16[2,256,1280]{2,1,0:T(8,128)(2,1)} %bitcast.41), channel_id=1, source_target_pairs={{0,1},{1,0},{2,3},{3,2},{4,5},{5,4},{6,7},{7,6},{8,9},{9,8},{10,11... | collective-permute-start | bytes 3932168 | tf_op jit(solution)/shard_map/ppermute | solution.py:184
  41.7 23.6 %copy-start.3 = (bf16[1,384,1280]{2,1,0:T(8,128)(2,1)S(1)}, bf16[1,384,1280]{2,1,0:T(8,128)(2,1)}, u32[]{:S(2)}) copy-start(bf16[1,384,1280]{2,1,0:T(8,128)(2,1)} %param.20) | copy-start | bytes 2949124
  41.7 1.1 copy-start.6
  52.1 8.3 %collective-permute-start.3 = (bf16[64,640]{1,0:T(8,128)(2,1)S(1)}, bf16[64,640]{1,0:T(8,128)(2,1)S(1)}, u32[]{:S(2)}, u32[]{:S(2)}) collective-permute-start(bf16[64,640]{1,0:T(8,128)(2,1)S(1)} %get-tuple-element.9), channel_id=1, source_target_pairs={{0,129},{1,128},{2,131},{3,130},{4,133},{5,132},{6,135},{7,134},{8... | collective-permute-start | bytes 245768 | tf_op jit(solution)/shard_map/ppermute | solution.py:244
  57.5 7.6 %collective-permute-start.2 = (bf16[64,640]{1,0:T(8,128)(2,1)S(1)}, bf16[64,640]{1,0:T(8,128)(2,1)S(1)}, u32[]{:S(2)}, u32[]{:S(2)}) collective-permute-start(bf16[64,640]{1,0:T(8,128)(2,1)S(1)} %get-tuple-element.9), channel_id=1, source_target_pairs={{0,128},{1,129},{2,130},{3,131},{4,132},{5,133},{6,134},{7,135},{8... | collective-permute-start | bytes 245768 | tf_op jit(solution)/shard_map/ppermute | solution.py:244
  58.2 6.9 %collective-permute-start.5 = (bf16[64,640]{1,0:T(8,128)(2,1)S(1)}, bf16[64,640]{1,0:T(8,128)(2,1)S(1)}, u32[]{:S(2)}, u32[]{:S(2)}) collective-permute-start(bf16[64,640]{1,0:T(8,128)(2,1)S(1)} %get-tuple-element.10), channel_id=1, source_target_pairs={{0,3},{1,2},{2,1},{3,0},{4,7},{5,6},{6,5},{7,4},{8,11},{9,10},{10,... | collective-permute-start | bytes 245768 | tf_op jit(solution)/shard_map/ppermute | solution.py:244
  59.8 5.3 %collective-permute-start.4 = (bf16[64,640]{1,0:T(8,128)(2,1)S(1)}, bf16[64,640]{1,0:T(8,128)(2,1)S(1)}, u32[]{:S(2)}, u32[]{:S(2)}) collective-permute-start(bf16[64,640]{1,0:T(8,128)(2,1)S(1)} %get-tuple-element.10), channel_id=1, source_target_pairs={{0,2},{1,3},{2,0},{3,1},{4,6},{5,7},{6,4},{7,5},{8,10},{9,11},{10,... | collective-permute-start | bytes 245768 | tf_op jit(solution)/shard_map/ppermute | solution.py:244
  80.0 5.6 %copy-start.4 = (bf16[1,512,1280]{2,1,0:T(8,128)(2,1)}, bf16[1,512,1280]{2,1,0:T(8,128)(2,1)S(1)}, u32[]{:S(2)}) copy-start(bf16[1,512,1280]{2,1,0:T(8,128)(2,1)S(1)} %fusion) | copy-start | bytes 3932164
  80.0 4.2 %collective-permute-start.6 = (bf16[1,512,1280]{2,1,0:T(8,128)(2,1)S(1)}, bf16[1,512,1280]{2,1,0:T(8,128)(2,1)S(1)}, u32[]{:S(2)}, u32[]{:S(2)}) collective-permute-start(bf16[1,512,1280]{2,1,0:T(8,128)(2,1)S(1)} %fusion), channel_id=1, source_target_pairs={{0,1},{1,0},{2,3},{3,2},{4,5},{5,4},{6,7},{7,6},{8,9},{9,8},{10,11... | collective-permute-start | bytes 3932168 | tf_op jit(solution)/shard_map/ppermute | solution.py:23
  84.2 1.4 %copy-start.5 = (bf16[1,512,1280]{2,1,0:T(8,128)(2,1)}, bf16[1,512,1280]{2,1,0:T(8,128)(2,1)S(1)}, u32[]{:S(2)}) copy-start(bf16[1,512,1280]{2,1,0:T(8,128)(2,1)S(1)} %collective-permute-done.6) | copy-start | bytes 3932164
  84.8 0.8 copy-start.9
  101.5 3.2 %collective-permute-start.7 = (bf16[1,512,1280]{2,1,0:T(8,128)(2,1)}, bf16[1,512,1280]{2,1,0:T(8,128)(2,1)S(1)}, u32[]{:S(2)}, u32[]{:S(2)}) collective-permute-start(bf16[1,512,1280]{2,1,0:T(8,128)(2,1)} %bitcast.44), channel_id=1, source_target_pairs={{0,1},{1,0},{2,3},{3,2},{4,5},{5,4},{6,7},{7,6},{8,9},{9,8},{10,11... | collective-permute-start | bytes 3932168 | tf_op jit(solution)/shard_map/ppermute | solution.py:184
  104.7 4.3 %copy-start.1 = (bf16[640,1280]{1,0:T(8,128)(2,1)S(1)}, bf16[640,1280]{1,0:T(8,128)(2,1)}, u32[]{:S(2)}) copy-start(bf16[640,1280]{1,0:T(8,128)(2,1)} %param.22) | copy-start | bytes 4915204

commit v5 on v4

--- a/solution.py
+++ b/solution.py
@@ -44,7 +44,7 @@
         o_ref[...] = acc_ref[...].astype(o_ref.dtype)
 
 
-def feed_forward(x, expand, contract, hidden_step=512, rows_per_step=128):
+def feed_forward(x, expand, contract, hidden_step=512, rows_per_step=256):
     length, width = x.shape
     hidden = expand.shape[1]
     return pl.pallas_call(
@@ -105,7 +105,7 @@
     )(residual, mine, other, merge_weight)
 
 
-def _attention_kernel(causal, x_ref, gain_ref, w_ref, valid_ref, o_ref, q_ref, k_ref, v_ref, acc_ref):
+def _attention_kernel(causal, x_ref, gain_ref, w_ref, valid_ref, wo_ref, o_ref, q_ref, k_ref, v_ref, acc_ref):
     length, width = q_ref.shape
     window = 256
     values = x_ref[0].astype(jnp.float32)
@@ -139,7 +139,8 @@
         probs = (raised / jnp.sum(raised, axis=-1, keepdims=True)).astype(jnp.bfloat16)
         values_h = jnp.where(mine, v_ref[:, lanes], zero)
         acc_ref[:, lanes] += jnp.dot(probs, values_h, preferred_element_type=jnp.float32)
-    o_ref[0] = acc_ref[...].astype(o_ref.dtype)
+    mixed = acc_ref[...].astype(jnp.bfloat16)
+    o_ref[0] = jnp.dot(mixed, wo_ref[...], preferred_element_type=jnp.float32).astype(o_ref.dtype)
 
 
 def attend(inputs, gain_first, attend_in, key_valid, causal, attend_out):
@@ -148,29 +149,31 @@
     weight = jnp.transpose(attend_in, (1, 0, 2))
     mixed = pl.pallas_call(
         functools.partial(_attention_kernel, causal),
-        out_shape=jax.ShapeDtypeStruct((batch, length, width), jnp.bfloat16),
+        out_shape=jax.ShapeDtypeStruct((batch, length, model_width), jnp.bfloat16),
         grid=(batch,),
         in_specs=[
             pl.BlockSpec((1, length, model_width), lambda b: (b, 0, 0)),
             pl.BlockSpec((1, model_width), lambda b: (0, 0)),
             pl.BlockSpec((3, model_width, width), lambda b: (0, 0, 0)),
             pl.BlockSpec((1, 1, length), lambda b: (b, 0, 0)),
+            pl.BlockSpec((width, model_width), lambda b: (0, 0)),
         ],
-        out_specs=pl.BlockSpec((1, length, width), lambda b: (b, 0, 0)),
+        out_specs=pl.BlockSpec((1, length, model_width), lambda b: (b, 0, 0)),
         scratch_shapes=[pltpu.VMEM((length, width), jnp.bfloat16)] * 3
         + [pltpu.VMEM((length, width), jnp.float32)],
         cost_estimate=pl.CostEstimate(
-            flops=batch * length * (6 * model_width * width + 4 * length * 256 * (width // HEAD_DIM)),
+            flops=batch * length * (8 * model_width * width + 4 * length * 256 * (width // HEAD_DIM)),
             transcendentals=batch * length * length * (width // HEAD_DIM),
-            bytes_accessed=2 * (batch * length * (model_width + width) + 3 * model_width * width),
+            bytes_accessed=2 * (2 * batch * length * model_width + 4 * model_width * width),
         ),
     )(
         inputs,
         gain_first.reshape(1, model_width),
         weight,
         key_valid.astype(jnp.int32).reshape(batch, 1, length),
-    )
-    return jnp.dot(mixed, attend_out, preferred_element_type=jnp.float32)
+        attend_out,
+    )
+    return mixed
 
 
 def layer(inputs, key_valid, causal, attend_in, attend_out, expand, contract, gain_first, gain_second, split=False):

time: 110 us -> 108 us (0.982)
  matrix products: 5.2 us -> 0 us
  other arithmetic: 12.7 us -> 15.3 us
    dot_general x2 -> x0, matrix products: 5.2 us -> none  [attend(): return jnp.dot(mixed, attend_out, preferred_element_type=jnp.float32)]
    pallas_call x2, Pallas kernels: 20.6 us -> 24.3 us  [attend(): pl.pallas_call(functools.partial(_attention_kernel, causal), out_shape=ja...]
    reduce_sum x2, other arithmetic: 1.19 us -> 4.31 us  [normalize(): center = values - jnp.mean(values, axis=-1, keepdims=True)]
    pallas_call x2, Pallas kernels: 27.9 us -> 25 us  [feed_forward(): pl.pallas_call(functools.partial(_feed_forward_kernel, rows_per_step), ou...]
where the time goes in v5:
time: 108 us; the launch traced here: 107 us
  Pallas kernels  57.7 us (53%)
  other arithmetic  15.3 us (14%)
  waiting for transfers between devices  13.5 us (12%)
  starting transfers between devices  12.8 us (12%)
  local copies, waits for them, and re-layouts  5.74 us (5%)
  between operations  2.12 us (2%)
    pallas_call x2, Pallas kernels, feed_forward(): pl.pallas_call(functools.partial(_feed_forward_kernel, rows_per_step), ou...  25 us
    pallas_call x2, Pallas kernels, attend(): pl.pallas_call(functools.partial(_attention_kernel, causal), out_shape=ja...  24.3 us
    pallas_call x1, Pallas kernels, merge(): pl.pallas_call(_merge_kernel, out_shape=jax.ShapeDtypeStruct((images, hal...  8.44 us
    ppermute x4, starting transfers between devices, on_device(): halves.append(lax.ppermute(merged[j], ('req', 'tensor'), perm))  7.49 us
    ppermute x2, waiting for transfers between devices, tensor_sum(): other = lax.ppermute(mine, 'tensor', [(0, 1), (1, 0)])  5.74 us
    ppermute x4, waiting for transfers between devices, on_device(): halves.append(lax.ppermute(merged[j], ('req', 'tensor'), perm))  4.82 us
    ppermute x2, starting transfers between devices, tensor_sum(): other = lax.ppermute(mine, 'tensor', [(0, 1), (1, 0)])  4.53 us
    reduce_sum x2, other arithmetic, normalize(): center = values - jnp.mean(values, axis=-1, keepdims=True)  4.31 us
  transfers between devices with their start and end apart: 8, of which 5 were waited for; matrix products, arithmetic and copies ran while one was open for 2% of the time, Pallas kernels for 0%

profile of v5, /device:TPU:1, one launch (start us, length us, event | category | flops | bytes accessed | tf_op | source)
XLA Modules:
  0.0 107.0 jit_solution(1780769517342197353)
XLA Ops:
  0.0 0.7 constant_dynamic-slice_fusion
  0.8 1.3 %reshape.275.gain_ref = f32[1,1280]{1,0:T(1,128)} reshape(f32[1280]{0:T(1024)} %param.25) | data formatting | bytes 10240 | tf_op jit(solution)/shard_map/reshape | solution.py:171
  2.1 0.7 and_convert_fusion.valid_ref
  2.7 0.0 copy-start.5
  2.7 11.6 %shard_map.163 = bf16[2,256,1280]{2,1,0:T(8,128)(2,1)} custom-call(bf16[2,256,1280]{2,1,0:T(8,128)(2,1)} %x_ref.1, f32[1,1280]{1,0:T(1,128)} %reshape.275.gain_ref, bf16[3,1280,640]{2,1,0:T(8,128)(2,1)} %bitcast.36, s32[2,1,256]{2,1,0:T(1,128)} %and_convert_fusion.valid_ref, bf16[640,1280]{1,0:T(8,128)(2,1)} %wo_ref.2), custom_call_target="tpu_custom_call" | custom-call | flops 4429185024 | bytes 9175040 | tf_op jit(solution)/shard_map/pallas_call | solution.py:150
  14.3 3.2 %collective-permute-start = (bf16[2,256,1280]{2,1,0:T(8,128)(2,1)}, bf16[2,256,1280]{2,1,0:T(8,128)(2,1)S(1)}, u32[]{:S(2)}, u32[]{:S(2)}) collective-permute-start(bf16[2,256,1280]{2,1,0:T(8,128)(2,1)} %shard_map.163), channel_id=1, source_target_pairs={{0,1},{1,0},{2,3},{3,2},{4,5},{5,4},{6,7},{7,6},{8,9},{9,8},{10,11... | collective-permute-start | bytes 3932168 | tf_op jit(solution)/shard_map/ppermute | solution.py:23
  17.6 2.9 %collective-permute-done = bf16[2,256,1280]{2,1,0:T(8,128)(2,1)S(1)} collective-permute-done((bf16[2,256,1280]{2,1,0:T(8,128)(2,1)}, bf16[2,256,1280]{2,1,0:T(8,128)(2,1)S(1)}, u32[]{:S(2)}, u32[]{:S(2)}) %collective-permute-start) | collective-permute-done | bytes 1310752 | tf_op jit(solution)/shard_map/ppermute | solution.py:23
  20.4 0.0 copy-done.5
  20.4 1.9 %fusion.7 = (f32[2,256]{1,0:T(2,128)S(1)}, f32[2,256,1280]{2,1,0:T(8,128)S(1)}) fusion(bf16[2,256,1280]{2,1,0:T(8,128)(2,1)S(1)} %collective-permute-done, bf16[2,256,1280]{2,1,0:T(8,128)(2,1)} %shard_map.163, bf16[2,256,1280]{2,1,0:T(8,128)(2,1)S(1)} %copy-done.5), kind=kLoop, calls=%fused_computation.47 | loop fusion | flops 3931648 | bytes 6555648 | tf_op jit(solution)/shard_map/reduce_sum | solution.py:16
  22.4 0.0 copy-start
  22.4 0.0 copy-start.6
  22.4 0.4 multiply_reduce_fusion.1
  22.8 0.3 copy-done.6
  23.1 1.5 %multiply_convert_fusion.1 = bf16[2,256,1280]{2,1,0:T(8,128)(2,1)} fusion(f32[2,256,1280]{2,1,0:T(8,128)S(1)} %get-tuple-element.6.res_ref, f32[1280]{0:T(1024)S(1)} %copy-done.6, f32[2,256]{1,0:T(2,128)S(1)} %add_rsqrt_fusion.1, f32[2,256]{1,0:T(2,128)S(1)} %broadcast_multiply_fusion.1), kind=kLoop, calls=%fused_computation.4 | loop fusion | flops 2621440 | bytes 3941376 | tf_op jit(solution)/shard_map/convert_element_type | solution.py:183
  24.5 0.0 copy-done
  24.5 0.0 copy-start.10
  24.6 0.0 copy-start.9
  24.6 0.0 copy-start.8
  24.6 12.5 %shard_map.164 = bf16[512,1280]{1,0:T(8,128)(2,1)} custom-call(bf16[512,1280]{1,0:T(8,128)(2,1)} %bitcast.33, bf16[1280,2560]{1,0:T(8,128)(2,1)} %w1_ref.2, bf16[2560,1280]{1,0:T(8,128)(2,1)} %w2_ref.2), custom_call_target="tpu_custom_call" | custom-call | flops 6710886400 | bytes 15728640 | tf_op jit(solution)/shard_map/pallas_call | solution.py:50
  37.1 0.4 collective-permute-start.1
  37.4 0.0 copy-done.10
  37.4 0.6 dynamic_slice.12
  40.0 0.0 copy-done.9
  40.0 0.1 constant_dynamic-slice_fusion.2
  40.1 0.1 add_select_fusion
  40.2 0.1 compare_and_fusion
  40.3 0.1 and.78
  40.3 0.0 copy-done.8
  40.4 0.6 reshape.278.gain_ref
  41.0 0.0 copy-start.1
  41.0 0.0 collective-permute-done.1.other_ref
  41.0 0.0 copy-start.4
  41.0 1.1 copy-done.4
  42.0 8.4 %shard_map.165 = bf16[2,64,640]{2,1,0:T(8,128)(2,1)} custom-call(f32[2,256,1280]{2,1,0:T(8,128)} %copy-done, bf16[2,256,1280]{2,1,0:T(8,128)(2,1)} %bitcast.32, bf16[2,256,1280]{2,1,0:T(8,128)(2,1)} %copy-done.4, bf16[5120,640]{1,0:T(8,128)(2,1)} %w_ref.1), custom_call_target="tpu_custom_call" | custom-call | flops 922746880 | bytes 11796480 | tf_op jit(solution)/shard_map/pallas_call | solution.py:97
  50.5 0.9 slice_bitcast_fusion.1
  51.4 5.3 %collective-permute-start.3 = (bf16[64,640]{1,0:T(8,128)(2,1)S(1)}, bf16[64,640]{1,0:T(8,128)(2,1)S(1)}, u32[]{:S(2)}, u32[]{:S(2)}) collective-permute-start(bf16[64,640]{1,0:T(8,128)(2,1)S(1)} %get-tuple-element.9), channel_id=1, source_target_pairs={{0,129},{1,128},{2,131},{3,130},{4,133},{5,132},{6,135},{7,134},{8... | collective-permute-start | bytes 245768 | tf_op jit(solution)/shard_map/ppermute | solution.py:247
  56.7 0.2 collective-permute-start.2
  56.9 0.6 fusion.8
  57.5 1.4 %collective-permute-start.5 = (bf16[64,640]{1,0:T(8,128)(2,1)S(1)}, bf16[64,640]{1,0:T(8,128)(2,1)S(1)}, u32[]{:S(2)}, u32[]{:S(2)}) collective-permute-start(bf16[64,640]{1,0:T(8,128)(2,1)S(1)} %get-tuple-element.10), channel_id=1, source_target_pairs={{0,3},{1,2},{2,1},{3,0},{4,7},{5,6},{6,5},{7,4},{8,11},{9,10},{10,... | collective-permute-start | bytes 245768 | tf_op jit(solution)/shard_map/ppermute | solution.py:247
  58.9 0.6 collective-permute-start.4
  59.5 0.2 collective-permute-done.3
  59.7 4.6 %collective-permute-done.2 = bf16[64,640]{1,0:T(8,128)(2,1)S(1)} collective-permute-done((bf16[64,640]{1,0:T(8,128)(2,1)S(1)}, bf16[64,640]{1,0:T(8,128)(2,1)S(1)}, u32[]{:S(2)}, u32[]{:S(2)}) %collective-permute-start.2) | collective-permute-done | bytes 81952 | tf_op jit(solution)/shard_map/ppermute | solution.py:247
  64.3 0.0 collective-permute-done.5
  64.3 0.0 collective-permute-done.4
  64.3 0.1 maximum_select_fusion
  64.4 0.0 copy-done.1
  64.4 1.1 %maximum_bitcast_fusion.x_ref = bf16[1,512,1280]{2,1,0:T(8,128)(2,1)} fusion(bf16[384,1280]{1,0:T(8,128)(2,1)S(1)} %bitcast.26, bf16[128,1280]{1,0:T(8,128)(2,1)S(1)} %maximum_select_fusion), kind=kLoop, calls=%fused_computation.9 | loop fusion | flops 2621440 | bytes 2621440 | tf_op jit(solution)/shard_map/broadcast_in_dim | solution.py:267
  65.6 12.7 %shard_map.166 = bf16[1,512,1280]{2,1,0:T(8,128)(2,1)} custom-call(bf16[1,512,1280]{2,1,0:T(8,128)(2,1)} %maximum_bitcast_fusion.x_ref, f32[1,1280]{1,0:T(1,128)} %reshape.278.gain_ref, bf16[3,1280,640]{2,1,0:T(8,128)(2,1)} %bitcast.37, s32[1,1,512]{2,1,0:T(1,128)} %bitcast.35, bf16[640,1280]{1,0:T(8,128)(2,1)} %wo_ref.3), custom_call_target="tpu_custom_call" | custom-call | flops 5502926848 | bytes 9175040 | tf_op jit(solution)/shard_map/pallas_call | solution.py:150
  78.2 0.0 copy-start.2
  78.2 1.3 %collective-permute-start.6 = (bf16[1,512,1280]{2,1,0:T(8,128)(2,1)}, bf16[1,512,1280]{2,1,0:T(8,128)(2,1)S(1)}, u32[]{:S(2)}, u32[]{:S(2)}) collective-permute-start(bf16[1,512,1280]{2,1,0:T(8,128)(2,1)} %shard_map.166), channel_id=1, source_target_pairs={{0,1},{1,0},{2,3},{3,2},{4,5},{5,4},{6,7},{7,6},{8,9},{9,8},{10,11... | collective-permute-start | bytes 3932168 | tf_op jit(solution)/shard_map/ppermute | solution.py:23
  79.5 2.9 %collective-permute-done.6 = bf16[1,512,1280]{2,1,0:T(8,128)(2,1)S(1)} collective-permute-done((bf16[1,512,1280]{2,1,0:T(8,128)(2,1)}, bf16[1,512,1280]{2,1,0:T(8,128)(2,1)S(1)}, u32[]{:S(2)}, u32[]{:S(2)}) %collective-permute-start.6) | collective-permute-done | bytes 1310752 | tf_op jit(solution)/shard_map/ppermute | solution.py:23
  82.4 0.0 copy-start.3
  82.4 2.4 %fusion.6 = f32[512]{0:T(512)S(1)} fusion(bf16[1,512,1280]{2,1,0:T(8,128)(2,1)S(1)} %collective-permute-done.6, bf16[1,512,1280]{2,1,0:T(8,128)(2,1)} %shard_map.166, bf16[1,384,1280]{2,1,0:T(8,128)(2,1)S(1)} %copy-done.1, bf16[1,128,1280]{2,1,0:T(8,128)(2,1)S(1)} %bitcast.27), kind=kLoop, calls=%fused_computation.46 | loop fusion | flops 5897728 | bytes 3934208 | tf_op jit(solution)/shard_map/reduce_sum | solution.py:16
  84.8 0.0 copy-start.7
  84.8 0.0 copy-done.2
  84.8 0.8 multiply_reduce_fusion
  85.6 0.0 copy-done.3
  85.6 0.0 copy-done.7
  85.6 1.8 %fusion.x_ref = bf16[512,1280]{1,0:T(8,128)(2,1)} fusion(f32[1280]{0:T(1024)S(1)} %copy-done.7, f32[512]{0:T(512)S(1)} %add_rsqrt_fusion, f32[512]{0:T(512)S(1)} %broadcast_multiply_fusion, bf16[1,512,1280]{2,1,0:T(8,128)(2,1)S(1)} %collective-permute-done.6, bf16[1,512,1280]{2,1,0:T(8,128)(2,1)S(1)} %copy-done.2, bf16[1,384,1280]{2,1,0:T(8,128)(2,1)S(1)} %copy-done.1, ...), kind=kLoop, calls=%fused_computation.7 | loop fusion | flops 7864320 | bytes 5252096 | tf_op jit(solution)/shard_map/reshape | solution.py:185
  87.5 12.5 %shard_map.167 = bf16[512,1280]{1,0:T(8,128)(2,1)} custom-call(bf16[512,1280]{1,0:T(8,128)(2,1)} %fusion.x_ref, bf16[1280,2560]{1,0:T(8,128)(2,1)} %w1_ref.3, bf16[2560,1280]{1,0:T(8,128)(2,1)} %w2_ref.3), custom_call_target="tpu_custom_call" | custom-call | flops 6710886400 | bytes 15728640 | tf_op jit(solution)/shard_map/pallas_call | solution.py:50
  100.0 0.4 collective-permute-start.7
  100.3 2.9 %collective-permute-done.7 = bf16[1,512,1280]{2,1,0:T(8,128)(2,1)S(1)} collective-permute-done((bf16[1,512,1280]{2,1,0:T(8,128)(2,1)}, bf16[1,512,1280]{2,1,0:T(8,128)(2,1)S(1)}, u32[]{:S(2)}, u32[]{:S(2)}) %collective-permute-start.7) | collective-permute-done | bytes 1310752 | tf_op jit(solution)/shard_map/ppermute | solution.py:187
  103.2 3.8 %fusion.1 = bf16[1,512,1280]{2,1,0:T(8,128)(2,1)} fusion(bf16[1,512,1280]{2,1,0:T(8,128)(2,1)S(1)} %collective-permute-done.7, pred[512]{0:T(512)(128)(4,1)S(1)} %get-tuple-element.19, bf16[512,1280]{1,0:T(8,128)(2,1)} %shard_map.167, bf16[1,512,1280]{2,1,0:T(8,128)(2,1)} %copy-done.3, bf16[1,512,1280]{2,1,0:T(8,128)(2,1)S(1)} %copy-done.2, ...), kind=kLoop, calls=%fused_computation.8 | loop fusion | flops 9175040 | bytes 7864832 | tf_op jit(solution)/shard_map/jit(_where)/select_n | solution.py:283
  (10 shorter events, 0.1 us)
Async XLA Ops:
  2.7 17.7 %copy-start.5 = (bf16[2,256,1280]{2,1,0:T(8,128)(2,1)S(1)}, bf16[2,256,1280]{2,1,0:T(8,128)(2,1)}, u32[]{:S(2)}) copy-start(bf16[2,256,1280]{2,1,0:T(8,128)(2,1)} %x_ref.1) | copy-start | bytes 3932164
  14.3 6.1 %collective-permute-start = (bf16[2,256,1280]{2,1,0:T(8,128)(2,1)}, bf16[2,256,1280]{2,1,0:T(8,128)(2,1)S(1)}, u32[]{:S(2)}, u32[]{:S(2)}) collective-permute-start(bf16[2,256,1280]{2,1,0:T(8,128)(2,1)} %shard_map.163), channel_id=1, source_target_pairs={{0,1},{1,0},{2,3},{3,2},{4,5},{5,4},{6,7},{7,6},{8,9},{9,8},{10,11... | collective-permute-start | bytes 3932168 | tf_op jit(solution)/shard_map/ppermute | solution.py:23
  22.4 2.2 %copy-start = (f32[2,256,1280]{2,1,0:T(8,128)}, f32[2,256,1280]{2,1,0:T(8,128)S(1)}, u32[]{:S(2)}) copy-start(f32[2,256,1280]{2,1,0:T(8,128)S(1)} %get-tuple-element.6.res_ref) | copy-start | bytes 7864324
  22.4 0.7 copy-start.6
  24.5 12.9 %copy-start.10 = (s32[256]{0:T(256)S(1)}, s32[256]{0:T(256)}, u32[]{:S(2)}) copy-start(s32[256]{0:T(256)} %param.19) | copy-start | bytes 3076
  24.6 15.5 %copy-start.9 = (s32[256,2]{0,1:T(2,128)S(1)}, s32[256,2]{0,1:T(2,128)}, u32[]{:S(2)}) copy-start(s32[256,2]{0,1:T(2,128)} %param.18) | copy-start | bytes 6148
  24.6 15.8 %copy-start.8 = (f32[1280]{0:T(1024)S(1)}, f32[1280]{0:T(1024)}, u32[]{:S(2)}) copy-start(f32[1280]{0:T(1024)} %param.32) | copy-start | bytes 15364
  37.1 3.9 %collective-permute-start.1 = (bf16[2,256,1280]{2,1,0:T(8,128)(2,1)}, bf16[2,256,1280]{2,1,0:T(8,128)(2,1)S(1)}, u32[]{:S(2)}, u32[]{:S(2)}) collective-permute-start(bf16[2,256,1280]{2,1,0:T(8,128)(2,1)} %bitcast.31), channel_id=1, source_target_pairs={{0,1},{1,0},{2,3},{3,2},{4,5},{5,4},{6,7},{7,6},{8,9},{9,8},{10,11... | collective-permute-start | bytes 3932168 | tf_op jit(solution)/shard_map/ppermute | solution.py:187
  41.0 23.5 %copy-start.1 = (bf16[1,384,1280]{2,1,0:T(8,128)(2,1)S(1)}, bf16[1,384,1280]{2,1,0:T(8,128)(2,1)}, u32[]{:S(2)}) copy-start(bf16[1,384,1280]{2,1,0:T(8,128)(2,1)} %param.20) | copy-start | bytes 2949124
  41.0 1.1 copy-start.4
  51.4 8.3 %collective-permute-start.3 = (bf16[64,640]{1,0:T(8,128)(2,1)S(1)}, bf16[64,640]{1,0:T(8,128)(2,1)S(1)}, u32[]{:S(2)}, u32[]{:S(2)}) collective-permute-start(bf16[64,640]{1,0:T(8,128)(2,1)S(1)} %get-tuple-element.9), channel_id=1, source_target_pairs={{0,129},{1,128},{2,131},{3,130},{4,133},{5,132},{6,135},{7,134},{8... | collective-permute-start | bytes 245768 | tf_op jit(solution)/shard_map/ppermute | solution.py:247
  56.7 7.6 %collective-permute-start.2 = (bf16[64,640]{1,0:T(8,128)(2,1)S(1)}, bf16[64,640]{1,0:T(8,128)(2,1)S(1)}, u32[]{:S(2)}, u32[]{:S(2)}) collective-permute-start(bf16[64,640]{1,0:T(8,128)(2,1)S(1)} %get-tuple-element.9), channel_id=1, source_target_pairs={{0,128},{1,129},{2,130},{3,131},{4,132},{5,133},{6,134},{7,135},{8... | collective-permute-start | bytes 245768 | tf_op jit(solution)/shard_map/ppermute | solution.py:247
  57.5 6.8 %collective-permute-start.5 = (bf16[64,640]{1,0:T(8,128)(2,1)S(1)}, bf16[64,640]{1,0:T(8,128)(2,1)S(1)}, u32[]{:S(2)}, u32[]{:S(2)}) collective-permute-start(bf16[64,640]{1,0:T(8,128)(2,1)S(1)} %get-tuple-element.10), channel_id=1, source_target_pairs={{0,3},{1,2},{2,1},{3,0},{4,7},{5,6},{6,5},{7,4},{8,11},{9,10},{10,... | collective-permute-start | bytes 245768 | tf_op jit(solution)/shard_map/ppermute | solution.py:247
  58.9 5.5 %collective-permute-start.4 = (bf16[64,640]{1,0:T(8,128)(2,1)S(1)}, bf16[64,640]{1,0:T(8,128)(2,1)S(1)}, u32[]{:S(2)}, u32[]{:S(2)}) collective-permute-start(bf16[64,640]{1,0:T(8,128)(2,1)S(1)} %get-tuple-element.10), channel_id=1, source_target_pairs={{0,2},{1,3},{2,0},{3,1},{4,6},{5,7},{6,4},{7,5},{8,10},{9,11},{10,... | collective-permute-start | bytes 245768 | tf_op jit(solution)/shard_map/ppermute | solution.py:247
  78.2 6.6 %copy-start.2 = (bf16[1,512,1280]{2,1,0:T(8,128)(2,1)S(1)}, bf16[1,512,1280]{2,1,0:T(8,128)(2,1)}, u32[]{:S(2)}) copy-start(bf16[1,512,1280]{2,1,0:T(8,128)(2,1)} %shard_map.166) | copy-start | bytes 3932164
  78.2 4.2 %collective-permute-start.6 = (bf16[1,512,1280]{2,1,0:T(8,128)(2,1)}, bf16[1,512,1280]{2,1,0:T(8,128)(2,1)S(1)}, u32[]{:S(2)}, u32[]{:S(2)}) collective-permute-start(bf16[1,512,1280]{2,1,0:T(8,128)(2,1)} %shard_map.166), channel_id=1, source_target_pairs={{0,1},{1,0},{2,3},{3,2},{4,5},{5,4},{6,7},{7,6},{8,9},{9,8},{10,11... | collective-permute-start | bytes 3932168 | tf_op jit(solution)/shard_map/ppermute | solution.py:23
  82.4 3.2 %copy-start.3 = (bf16[1,512,1280]{2,1,0:T(8,128)(2,1)}, bf16[1,512,1280]{2,1,0:T(8,128)(2,1)S(1)}, u32[]{:S(2)}) copy-start(bf16[1,512,1280]{2,1,0:T(8,128)(2,1)S(1)} %collective-permute-done.6) | copy-start | bytes 3932164
  84.8 0.8 copy-start.7
  100.0 3.2 %collective-permute-start.7 = (bf16[1,512,1280]{2,1,0:T(8,128)(2,1)}, bf16[1,512,1280]{2,1,0:T(8,128)(2,1)S(1)}, u32[]{:S(2)}, u32[]{:S(2)}) collective-permute-start(bf16[1,512,1280]{2,1,0:T(8,128)(2,1)} %bitcast.34), channel_id=1, source_target_pairs={{0,1},{1,0},{2,3},{3,2},{4,5},{5,4},{6,7},{7,6},{8,9},{9,8},{10,11... | collective-permute-start | bytes 3932168 | tf_op jit(solution)/shard_map/ppermute | solution.py:187

commit v6 on v5

--- a/solution.py
+++ b/solution.py
@@ -44,7 +44,7 @@
         o_ref[...] = acc_ref[...].astype(o_ref.dtype)
 
 
-def feed_forward(x, expand, contract, hidden_step=512, rows_per_step=256):
+def feed_forward(x, expand, contract, hidden_step=512, rows_per_step=512):
     length, width = x.shape
     hidden = expand.shape[1]
     return pl.pallas_call(
@@ -235,20 +235,25 @@
     )
     merged = merge(residual, mine, other, merge_weight)
 
-    arrived = []
-    for j in range(images_here):
-        halves = []
-        for flip in (0, 1):
-            perm = [
-                (r * 2 + t, (r ^ REQ_XOR[j]) * 2 + (t ^ flip))
-                for r in range(req_count)
-                for t in range(2)
-            ]
-            halves.append(lax.ppermute(merged[j], ("req", "tensor"), perm))
-        same, other = halves
-        low = jnp.where(core == 0, same, other)
-        high = jnp.where(core == 0, other, same)
-        arrived.append(jnp.concatenate([low, high], axis=-1))
+    swap_pair = [(0, 1), (1, 0)]
+    given = lax.ppermute(jnp.where(core == 0, merged[1], merged[0]), "tensor", swap_pair)
+    own_image = jnp.where(
+        core == 0,
+        jnp.concatenate([merged[0], given], axis=-1),
+        jnp.concatenate([given, merged[1]], axis=-1),
+    )
+    sent = []
+    for flip in (0, 1):
+        perm = [
+            (r * 2 + t, (r ^ REQ_XOR[t]) * 2 + (t ^ flip))
+            for r in range(req_count)
+            for t in range(2)
+        ]
+        sent.append(lax.ppermute(own_image, ("req", "tensor"), perm))
+    arrived = [
+        jnp.where(core == 0, sent[0], sent[1]),
+        jnp.where(core == 0, sent[1], sent[0]),
+    ]
     sources = [(device ^ REQ_XOR[j]) * images_here + j for j in range(images_here)]
     first_slot = place[sources[0]] % 2
     swap = first_slot != 0

time: 108 us -> 105 us (0.972)
  waiting for transfers between devices: 13.5 us -> 10.7 us
  Pallas kernels: 57.7 us -> 56.6 us
    ppermute x4 -> x3, waiting for transfers between devices: 4.82 us -> 1.91 us  [the longest x2 1.91 us: on_device(): sent.append(lax.ppermute(own_image, ('req', 'tensor'), perm))]
    pallas_call x2, Pallas kernels: 25 us -> 23.9 us  [feed_forward(): pl.pallas_call(functools.partial(_feed_forward_kernel, rows_per_step), ou...]
    ppermute x4 -> x3, starting transfers between devices: 7.49 us -> 7.42 us  [the longest x2 6.96 us: on_device(): sent.append(lax.ppermute(own_image, ('req', 'tensor'), perm))]
  transfers between devices with their start and end apart: 8 -> 7, of which waited for: 5 -> 5; matrix products, arithmetic and copies ran while one was open for 2% -> 3% of each run, Pallas kernels for 0% -> 0%
where the time goes in v6:
time: 105 us; the launch traced here: 103 us
  Pallas kernels  56.6 us (54%)
  other arithmetic  16.3 us (16%)
  starting transfers between devices  11.9 us (11%)
  waiting for transfers between devices  10.7 us (10%)
  local copies, waits for them, and re-layouts  5.72 us (5%)
  between operations  2.11 us (2%)
    pallas_call x2, Pallas kernels, attend(): pl.pallas_call(functools.partial(_attention_kernel, causal), out_shape=ja...  24.3 us
    pallas_call x2, Pallas kernels, feed_forward(): pl.pallas_call(functools.partial(_feed_forward_kernel, rows_per_step), ou...  23.9 us
    pallas_call x1, Pallas kernels, merge(): pl.pallas_call(_merge_kernel, out_shape=jax.ShapeDtypeStruct((images, hal...  8.44 us
    ppermute x2, starting transfers between devices, on_device(): sent.append(lax.ppermute(own_image, ('req', 'tensor'), perm))  6.96 us
    ppermute x2, waiting for transfers between devices, tensor_sum(): other = lax.ppermute(mine, 'tensor', [(0, 1), (1, 0)])  5.74 us
    reduce_sum x2, other arithmetic, normalize(): center = values - jnp.mean(values, axis=-1, keepdims=True)  4.31 us
    select_n x1, other arithmetic, on_device(): jnp.where(prompt_valid[None, :, None], decoded, jnp.zeros_like(decoded))  3.82 us
    ppermute x2, starting transfers between devices, tensor_sum(): other = lax.ppermute(mine, 'tensor', [(0, 1), (1, 0)])  3.74 us
  transfers between devices with their start and end apart: 7, of which 5 were waited for; matrix products, arithmetic and copies ran while one was open for 3% of the time, Pallas kernels for 0%

profile of v6, /device:TPU:1, one launch (start us, length us, event | category | flops | bytes accessed | tf_op | source)
XLA Modules:
  0.0 103.3 jit_solution(17469151237416920878)
XLA Ops:
  0.0 0.7 constant_dynamic-slice_fusion
  0.8 1.3 %reshape.275.gain_ref = f32[1,1280]{1,0:T(1,128)} reshape(f32[1280]{0:T(1024)} %param.25) | data formatting | bytes 10240 | tf_op jit(solution)/shard_map/reshape | solution.py:171
  2.1 0.7 and_convert_fusion.valid_ref
  2.7 0.0 copy-start.5
  2.7 11.6 %shard_map.163 = bf16[2,256,1280]{2,1,0:T(8,128)(2,1)} custom-call(bf16[2,256,1280]{2,1,0:T(8,128)(2,1)} %x_ref.1, f32[1,1280]{1,0:T(1,128)} %reshape.275.gain_ref, bf16[3,1280,640]{2,1,0:T(8,128)(2,1)} %bitcast.40, s32[2,1,256]{2,1,0:T(1,128)} %and_convert_fusion.valid_ref, bf16[640,1280]{1,0:T(8,128)(2,1)} %wo_ref.2), custom_call_target="tpu_custom_call" | custom-call | flops 4429185024 | bytes 9175040 | tf_op jit(solution)/shard_map/pallas_call | solution.py:150
  14.3 3.2 %collective-permute-start = (bf16[2,256,1280]{2,1,0:T(8,128)(2,1)}, bf16[2,256,1280]{2,1,0:T(8,128)(2,1)S(1)}, u32[]{:S(2)}, u32[]{:S(2)}) collective-permute-start(bf16[2,256,1280]{2,1,0:T(8,128)(2,1)} %shard_map.163), channel_id=1, source_target_pairs={{0,1},{1,0},{2,3},{3,2},{4,5},{5,4},{6,7},{7,6},{8,9},{9,8},{10,11... | collective-permute-start | bytes 3932168 | tf_op jit(solution)/shard_map/ppermute | solution.py:23
  17.5 2.9 %collective-permute-done = bf16[2,256,1280]{2,1,0:T(8,128)(2,1)S(1)} collective-permute-done((bf16[2,256,1280]{2,1,0:T(8,128)(2,1)}, bf16[2,256,1280]{2,1,0:T(8,128)(2,1)S(1)}, u32[]{:S(2)}, u32[]{:S(2)}) %collective-permute-start) | collective-permute-done | bytes 1310752 | tf_op jit(solution)/shard_map/ppermute | solution.py:23
  20.4 0.0 copy-done.5
  20.4 1.9 %fusion.7 = (f32[2,256]{1,0:T(2,128)S(1)}, f32[2,256,1280]{2,1,0:T(8,128)S(1)}) fusion(bf16[2,256,1280]{2,1,0:T(8,128)(2,1)S(1)} %collective-permute-done, bf16[2,256,1280]{2,1,0:T(8,128)(2,1)} %shard_map.163, bf16[2,256,1280]{2,1,0:T(8,128)(2,1)S(1)} %copy-done.5), kind=kLoop, calls=%fused_computation.47 | loop fusion | flops 3931648 | bytes 6555648 | tf_op jit(solution)/shard_map/reduce_sum | solution.py:16
  22.3 0.0 copy-start
  22.3 0.0 copy-start.6
  22.4 0.4 multiply_reduce_fusion.1
  22.8 0.3 copy-done.6
  23.1 1.5 %multiply_convert_fusion.1 = bf16[2,256,1280]{2,1,0:T(8,128)(2,1)} fusion(f32[2,256,1280]{2,1,0:T(8,128)S(1)} %get-tuple-element.6.res_ref, f32[1280]{0:T(1024)S(1)} %copy-done.6, f32[2,256]{1,0:T(2,128)S(1)} %add_rsqrt_fusion.1, f32[2,256]{1,0:T(2,128)S(1)} %broadcast_multiply_fusion.1), kind=kLoop, calls=%fused_computation.4 | loop fusion | flops 2621440 | bytes 3941376 | tf_op jit(solution)/shard_map/convert_element_type | solution.py:183
  24.5 0.0 copy-done
  24.5 0.0 copy-start.10
  24.5 0.0 copy-start.9
  24.5 11.9 %shard_map.164 = bf16[512,1280]{1,0:T(8,128)(2,1)} custom-call(bf16[512,1280]{1,0:T(8,128)(2,1)} %bitcast.37, bf16[1280,2560]{1,0:T(8,128)(2,1)} %w1_ref.2, bf16[2560,1280]{1,0:T(8,128)(2,1)} %w2_ref.2), custom_call_target="tpu_custom_call" | custom-call | flops 6710886400 | bytes 15728640 | tf_op jit(solution)/shard_map/pallas_call | solution.py:50
  36.5 0.4 collective-permute-start.1
  36.8 0.0 copy-done.10
  36.8 0.6 dynamic_slice.12
  39.4 0.0 copy-done.9
  39.4 0.1 constant_dynamic-slice_fusion.2
  39.5 0.1 add_select_fusion
  39.6 0.0 copy-start.8
  39.6 0.1 collective-permute-done.1.other_ref
  39.7 0.0 copy-start.4
  39.7 1.1 %copy-done.4 = bf16[2,256,1280]{2,1,0:T(8,128)(2,1)} copy-done((bf16[2,256,1280]{2,1,0:T(8,128)(2,1)}, bf16[2,256,1280]{2,1,0:T(8,128)(2,1)S(1)}, u32[]{:S(2)}) %copy-start.4) | copy-done | bytes 1310744
  40.8 8.4 %shard_map.165 = bf16[2,64,640]{2,1,0:T(8,128)(2,1)} custom-call(f32[2,256,1280]{2,1,0:T(8,128)} %copy-done, bf16[2,256,1280]{2,1,0:T(8,128)(2,1)} %bitcast.36, bf16[2,256,1280]{2,1,0:T(8,128)(2,1)} %copy-done.4, bf16[5120,640]{1,0:T(8,128)(2,1)} %w_ref.1), custom_call_target="tpu_custom_call" | custom-call | flops 922746880 | bytes 11796480 | tf_op jit(solution)/shard_map/pallas_call | solution.py:97
  49.2 0.0 copy-start.1
  49.2 1.0 broadcast_select_fusion.2
  50.2 0.5 collective-permute-start.2
  50.7 0.9 slice_bitcast_fusion
  51.6 0.0 collective-permute-done.2
  51.7 5.3 %collective-permute-start.4 = (bf16[64,1280]{1,0:T(8,128)(2,1)S(1)}, bf16[64,1280]{1,0:T(8,128)(2,1)S(1)}, u32[]{:S(2)}, u32[]{:S(2)}) collective-permute-start(bf16[64,1280]{1,0:T(8,128)(2,1)S(1)} %maximum_select_fusion.1), channel_id=1, source_target_pairs={{0,2},{1,129},{2,0},{3,131},{4,6},{5,133},{6,4},{7,135},{8,10},{9,... | collective-permute-start | bytes 491528 | tf_op jit(solution)/shard_map/ppermute | solution.py:252
  57.0 1.7 %collective-permute-start.3 = (bf16[64,1280]{1,0:T(8,128)(2,1)S(1)}, bf16[64,1280]{1,0:T(8,128)(2,1)S(1)}, u32[]{:S(2)}, u32[]{:S(2)}) collective-permute-start(bf16[64,1280]{1,0:T(8,128)(2,1)S(1)} %maximum_select_fusion.1), channel_id=1, source_target_pairs={{0,3},{1,128},{2,1},{3,130},{4,7},{5,132},{6,5},{7,134},{8,11},{9,... | collective-permute-start | bytes 491528 | tf_op jit(solution)/shard_map/ppermute | solution.py:252
  58.7 0.1 compare_and_fusion
  58.7 0.1 and.78
  58.8 0.0 copy-done.8
  58.8 0.6 reshape.278.gain_ref
  59.4 0.6 fusion.8
  60.0 0.0 collective-permute-done.4
  60.0 1.9 %collective-permute-done.3 = bf16[64,1280]{1,0:T(8,128)(2,1)S(1)} collective-permute-done((bf16[64,1280]{1,0:T(8,128)(2,1)S(1)}, bf16[64,1280]{1,0:T(8,128)(2,1)S(1)}, u32[]{:S(2)}, u32[]{:S(2)}) %collective-permute-start.3) | collective-permute-done | bytes 163872 | tf_op jit(solution)/shard_map/ppermute | solution.py:252
  61.9 0.1 maximum_select_fusion
  62.0 0.0 copy-done.1
  62.0 1.1 %maximum_bitcast_fusion.x_ref = bf16[1,512,1280]{2,1,0:T(8,128)(2,1)} fusion(bf16[384,1280]{1,0:T(8,128)(2,1)S(1)} %bitcast.30, bf16[128,1280]{1,0:T(8,128)(2,1)S(1)} %maximum_select_fusion), kind=kLoop, calls=%fused_computation.9 | loop fusion | flops 2621440 | bytes 2621440 | tf_op jit(solution)/shard_map/broadcast_in_dim | solution.py:272
  63.2 12.7 %shard_map.166 = bf16[1,512,1280]{2,1,0:T(8,128)(2,1)} custom-call(bf16[1,512,1280]{2,1,0:T(8,128)(2,1)} %maximum_bitcast_fusion.x_ref, f32[1,1280]{1,0:T(1,128)} %reshape.278.gain_ref, bf16[3,1280,640]{2,1,0:T(8,128)(2,1)} %bitcast.41, s32[1,1,512]{2,1,0:T(1,128)} %bitcast.39, bf16[640,1280]{1,0:T(8,128)(2,1)} %wo_ref.3), custom_call_target="tpu_custom_call" | custom-call | flops 5502926848 | bytes 9175040 | tf_op jit(solution)/shard_map/pallas_call | solution.py:150
  75.8 0.0 copy-start.2
  75.8 0.5 collective-permute-start.5
  76.3 2.9 %collective-permute-done.5 = bf16[1,512,1280]{2,1,0:T(8,128)(2,1)S(1)} collective-permute-done((bf16[1,512,1280]{2,1,0:T(8,128)(2,1)}, bf16[1,512,1280]{2,1,0:T(8,128)(2,1)S(1)}, u32[]{:S(2)}, u32[]{:S(2)}) %collective-permute-start.5) | collective-permute-done | bytes 1310752 | tf_op jit(solution)/shard_map/ppermute | solution.py:23
  79.2 0.0 copy-start.3
  79.2 2.4 %fusion.6 = f32[512]{0:T(512)S(1)} fusion(bf16[1,512,1280]{2,1,0:T(8,128)(2,1)S(1)} %collective-permute-done.5, bf16[1,512,1280]{2,1,0:T(8,128)(2,1)} %shard_map.166, bf16[1,384,1280]{2,1,0:T(8,128)(2,1)S(1)} %copy-done.1, bf16[1,128,1280]{2,1,0:T(8,128)(2,1)S(1)} %bitcast.31), kind=kLoop, calls=%fused_computation.46 | loop fusion | flops 5897728 | bytes 3934208 | tf_op jit(solution)/shard_map/reduce_sum | solution.py:16
  81.6 0.0 copy-start.7
  81.6 0.0 copy-done.2
  81.6 0.8 multiply_reduce_fusion
  82.4 0.0 copy-done.3
  82.4 0.0 copy-done.7
  82.4 1.8 %fusion.x_ref = bf16[512,1280]{1,0:T(8,128)(2,1)} fusion(f32[1280]{0:T(1024)S(1)} %copy-done.7, f32[512]{0:T(512)S(1)} %add_rsqrt_fusion, f32[512]{0:T(512)S(1)} %broadcast_multiply_fusion, bf16[1,512,1280]{2,1,0:T(8,128)(2,1)S(1)} %collective-permute-done.5, bf16[1,512,1280]{2,1,0:T(8,128)(2,1)S(1)} %copy-done.2, bf16[1,384,1280]{2,1,0:T(8,128)(2,1)S(1)} %copy-done.1, ...), kind=kLoop, calls=%fused_computation.7 | loop fusion | flops 7864320 | bytes 5252096 | tf_op jit(solution)/shard_map/reshape | solution.py:185
  84.3 11.9 %shard_map.167 = bf16[512,1280]{1,0:T(8,128)(2,1)} custom-call(bf16[512,1280]{1,0:T(8,128)(2,1)} %fusion.x_ref, bf16[1280,2560]{1,0:T(8,128)(2,1)} %w1_ref.3, bf16[2560,1280]{1,0:T(8,128)(2,1)} %w2_ref.3), custom_call_target="tpu_custom_call" | custom-call | flops 6710886400 | bytes 15728640 | tf_op jit(solution)/shard_map/pallas_call | solution.py:50
  96.2 0.4 collective-permute-start.6
  96.6 2.9 %collective-permute-done.6 = bf16[1,512,1280]{2,1,0:T(8,128)(2,1)S(1)} collective-permute-done((bf16[1,512,1280]{2,1,0:T(8,128)(2,1)}, bf16[1,512,1280]{2,1,0:T(8,128)(2,1)S(1)}, u32[]{:S(2)}, u32[]{:S(2)}) %collective-permute-start.6) | collective-permute-done | bytes 1310752 | tf_op jit(solution)/shard_map/ppermute | solution.py:187
  99.4 3.8 %fusion.1 = bf16[1,512,1280]{2,1,0:T(8,128)(2,1)} fusion(bf16[1,512,1280]{2,1,0:T(8,128)(2,1)S(1)} %collective-permute-done.6, pred[512]{0:T(512)(128)(4,1)S(1)} %get-tuple-element.17, bf16[512,1280]{1,0:T(8,128)(2,1)} %shard_map.167, bf16[1,512,1280]{2,1,0:T(8,128)(2,1)} %copy-done.3, bf16[1,512,1280]{2,1,0:T(8,128)(2,1)S(1)} %copy-done.2, ...), kind=kLoop, calls=%fused_computation.8 | loop fusion | flops 9175040 | bytes 7864832 | tf_op jit(solution)/shard_map/jit(_where)/select_n | solution.py:288
  (10 shorter events, 0.1 us)
Async XLA Ops:
  2.7 17.7 %copy-start.5 = (bf16[2,256,1280]{2,1,0:T(8,128)(2,1)S(1)}, bf16[2,256,1280]{2,1,0:T(8,128)(2,1)}, u32[]{:S(2)}) copy-start(bf16[2,256,1280]{2,1,0:T(8,128)(2,1)} %x_ref.1) | copy-start | bytes 3932164
  14.3 6.1 %collective-permute-start = (bf16[2,256,1280]{2,1,0:T(8,128)(2,1)}, bf16[2,256,1280]{2,1,0:T(8,128)(2,1)S(1)}, u32[]{:S(2)}, u32[]{:S(2)}) collective-permute-start(bf16[2,256,1280]{2,1,0:T(8,128)(2,1)} %shard_map.163), channel_id=1, source_target_pairs={{0,1},{1,0},{2,3},{3,2},{4,5},{5,4},{6,7},{7,6},{8,9},{9,8},{10,11... | collective-permute-start | bytes 3932168 | tf_op jit(solution)/shard_map/ppermute | solution.py:23
  22.3 2.2 %copy-start = (f32[2,256,1280]{2,1,0:T(8,128)}, f32[2,256,1280]{2,1,0:T(8,128)S(1)}, u32[]{:S(2)}) copy-start(f32[2,256,1280]{2,1,0:T(8,128)S(1)} %get-tuple-element.6.res_ref) | copy-start | bytes 7864324
  22.3 0.7 copy-start.6
  24.5 12.3 %copy-start.10 = (s32[256]{0:T(256)S(1)}, s32[256]{0:T(256)}, u32[]{:S(2)}) copy-start(s32[256]{0:T(256)} %param.19) | copy-start | bytes 3076
  24.5 14.9 %copy-start.9 = (s32[256,2]{0,1:T(2,128)S(1)}, s32[256,2]{0,1:T(2,128)}, u32[]{:S(2)}) copy-start(s32[256,2]{0,1:T(2,128)} %param.18) | copy-start | bytes 6148
  36.5 3.2 %collective-permute-start.1 = (bf16[2,256,1280]{2,1,0:T(8,128)(2,1)}, bf16[2,256,1280]{2,1,0:T(8,128)(2,1)S(1)}, u32[]{:S(2)}, u32[]{:S(2)}) collective-permute-start(bf16[2,256,1280]{2,1,0:T(8,128)(2,1)} %bitcast.35), channel_id=1, source_target_pairs={{0,1},{1,0},{2,3},{3,2},{4,5},{5,4},{6,7},{7,6},{8,9},{9,8},{10,11... | collective-permute-start | bytes 3932168 | tf_op jit(solution)/shard_map/ppermute | solution.py:187
  39.6 19.2 %copy-start.8 = (f32[1280]{0:T(1024)S(1)}, f32[1280]{0:T(1024)}, u32[]{:S(2)}) copy-start(f32[1280]{0:T(1024)} %param.32) | copy-start | bytes 15364
  39.7 1.1 %copy-start.4 = (bf16[2,256,1280]{2,1,0:T(8,128)(2,1)}, bf16[2,256,1280]{2,1,0:T(8,128)(2,1)S(1)}, u32[]{:S(2)}) copy-start(bf16[2,256,1280]{2,1,0:T(8,128)(2,1)S(1)} %collective-permute-done.1.other_ref) | copy-start | bytes 3932164
  49.2 12.8 %copy-start.1 = (bf16[1,384,1280]{2,1,0:T(8,128)(2,1)S(1)}, bf16[1,384,1280]{2,1,0:T(8,128)(2,1)}, u32[]{:S(2)}) copy-start(bf16[1,384,1280]{2,1,0:T(8,128)(2,1)} %param.20) | copy-start | bytes 2949124
  50.2 1.4 %collective-permute-start.2 = (bf16[64,640]{1,0:T(8,128)(2,1)S(1)}, bf16[64,640]{1,0:T(8,128)(2,1)S(1)}, u32[]{:S(2)}, u32[]{:S(2)}) collective-permute-start(bf16[64,640]{1,0:T(8,128)(2,1)S(1)} %broadcast_select_fusion.2), channel_id=1, source_target_pairs={{0,1},{1,0},{2,3},{3,2},{4,5},{5,4},{6,7},{7,6},{8,9},{9,8},{10,11... | collective-permute-start | bytes 245768 | tf_op jit(solution)/shard_map/ppermute | solution.py:239
  51.7 8.3 %collective-permute-start.4 = (bf16[64,1280]{1,0:T(8,128)(2,1)S(1)}, bf16[64,1280]{1,0:T(8,128)(2,1)S(1)}, u32[]{:S(2)}, u32[]{:S(2)}) collective-permute-start(bf16[64,1280]{1,0:T(8,128)(2,1)S(1)} %maximum_select_fusion.1), channel_id=1, source_target_pairs={{0,2},{1,129},{2,0},{3,131},{4,6},{5,133},{6,4},{7,135},{8,10},{9,... | collective-permute-start | bytes 491528 | tf_op jit(solution)/shard_map/ppermute | solution.py:252
  57.0 4.9 %collective-permute-start.3 = (bf16[64,1280]{1,0:T(8,128)(2,1)S(1)}, bf16[64,1280]{1,0:T(8,128)(2,1)S(1)}, u32[]{:S(2)}, u32[]{:S(2)}) collective-permute-start(bf16[64,1280]{1,0:T(8,128)(2,1)S(1)} %maximum_select_fusion.1), channel_id=1, source_target_pairs={{0,3},{1,128},{2,1},{3,130},{4,7},{5,132},{6,5},{7,134},{8,11},{9,... | collective-permute-start | bytes 491528 | tf_op jit(solution)/shard_map/ppermute | solution.py:252
  75.8 5.8 %copy-start.2 = (bf16[1,512,1280]{2,1,0:T(8,128)(2,1)S(1)}, bf16[1,512,1280]{2,1,0:T(8,128)(2,1)}, u32[]{:S(2)}) copy-start(bf16[1,512,1280]{2,1,0:T(8,128)(2,1)} %shard_map.166) | copy-start | bytes 3932164
  75.8 3.4 %collective-permute-start.5 = (bf16[1,512,1280]{2,1,0:T(8,128)(2,1)}, bf16[1,512,1280]{2,1,0:T(8,128)(2,1)S(1)}, u32[]{:S(2)}, u32[]{:S(2)}) collective-permute-start(bf16[1,512,1280]{2,1,0:T(8,128)(2,1)} %shard_map.166), channel_id=1, source_target_pairs={{0,1},{1,0},{2,3},{3,2},{4,5},{5,4},{6,7},{7,6},{8,9},{9,8},{10,11... | collective-permute-start | bytes 3932168 | tf_op jit(solution)/shard_map/ppermute | solution.py:23
  79.2 3.2 %copy-start.3 = (bf16[1,512,1280]{2,1,0:T(8,128)(2,1)}, bf16[1,512,1280]{2,1,0:T(8,128)(2,1)S(1)}, u32[]{:S(2)}) copy-start(bf16[1,512,1280]{2,1,0:T(8,128)(2,1)S(1)} %collective-permute-done.5) | copy-start | bytes 3932164
  81.6 0.8 copy-start.7
  96.2 3.2 %collective-permute-start.6 = (bf16[1,512,1280]{2,1,0:T(8,128)(2,1)}, bf16[1,512,1280]{2,1,0:T(8,128)(2,1)S(1)}, u32[]{:S(2)}, u32[]{:S(2)}) collective-permute-start(bf16[1,512,1280]{2,1,0:T(8,128)(2,1)} %bitcast.38), channel_id=1, source_target_pairs={{0,1},{1,0},{2,3},{3,2},{4,5},{5,4},{6,7},{7,6},{8,9},{9,8},{10,11... | collective-permute-start | bytes 3932168 | tf_op jit(solution)/shard_map/ppermute | solution.py:187

commit v7 on v6

--- a/solution.py
+++ b/solution.py
@@ -67,27 +67,36 @@
 
 
 def _merge_kernel(res_ref, mine_ref, other_ref, w_ref, o_ref):
-    cells, width = res_ref.shape[1], res_ref.shape[2]
+    images, cells, width = res_ref.shape
     half = GRID // 2
-    slot = lax.broadcasted_iota(jnp.int32, (half * half, cells), 0)
-    cell = lax.broadcasted_iota(jnp.int32, (half * half, cells), 1)
-    for i in range(res_ref.shape[0]):
-        encoded = (
-            res_ref[i] + (mine_ref[i].astype(jnp.float32) + other_ref[i].astype(jnp.float32))
-        ).astype(jnp.bfloat16)
-        total = None
-        for a in range(2):
-            for b in range(2):
-                wanted = (2 * (slot // half) + a) * GRID + 2 * (slot % half) + b
-                pick = jnp.where(cell == wanted, 1.0, 0.0).astype(jnp.bfloat16)
-                rows = jnp.dot(pick, encoded, preferred_element_type=jnp.float32).astype(jnp.bfloat16)
-                part = jnp.dot(
-                    rows,
-                    w_ref[pl.ds((2 * a + b) * width, width), :],
-                    preferred_element_type=jnp.float32,
-                )
-                total = part if total is None else total + part
-        o_ref[i] = total.astype(o_ref.dtype)
+    slots = half * half
+    encoded = jnp.concatenate(
+        [
+            (res_ref[i] + (mine_ref[i].astype(jnp.float32) + other_ref[i].astype(jnp.float32))).astype(
+                jnp.bfloat16
+            )
+            for i in range(images)
+        ],
+        axis=0,
+    )
+    slot = lax.broadcasted_iota(jnp.int32, (images * slots, images * cells), 0)
+    cell = lax.broadcasted_iota(jnp.int32, (images * slots, images * cells), 1)
+    image = slot // slots
+    block = slot % slots
+    total = None
+    for a in range(2):
+        for b in range(2):
+            wanted = image * cells + (2 * (block // half) + a) * GRID + 2 * (block % half) + b
+            pick = jnp.where(cell == wanted, 1.0, 0.0).astype(jnp.bfloat16)
+            rows = jnp.dot(pick, encoded, preferred_element_type=jnp.float32).astype(jnp.bfloat16)
+            part = jnp.dot(
+                rows,
+                w_ref[pl.ds((2 * a + b) * width, width), :],
+                preferred_element_type=jnp.float32,
+            )
+            total = part if total is None else total + part
+    for i in range(images):
+        o_ref[i] = total[i * slots : (i + 1) * slots].astype(o_ref.dtype)
 
 
 def merge(residual, mine, other, merge_weight):

time: 105 us -> 104 us (level)
  Pallas kernels: 56.6 us -> 55.4 us
    pallas_call x1, Pallas kernels: 8.44 us -> 7.27 us  [merge(): pl.pallas_call(_merge_kernel, out_shape=jax.ShapeDtypeStruct((images, hal...]
where the time goes in v7:
time: 104 us; the launch traced here: 102 us
  Pallas kernels  55.4 us (53%)
  other arithmetic  16.3 us (16%)
  starting transfers between devices  11.9 us (11%)
  waiting for transfers between devices  10.7 us (10%)
  local copies, waits for them, and re-layouts  5.72 us (6%)
  between operations  2.11 us (2%)
    pallas_call x2, Pallas kernels, attend(): pl.pallas_call(functools.partial(_attention_kernel, causal), out_shape=ja...  24.3 us
    pallas_call x2, Pallas kernels, feed_forward(): pl.pallas_call(functools.partial(_feed_forward_kernel, rows_per_step), ou...  23.9 us
    pallas_call x1, Pallas kernels, merge(): pl.pallas_call(_merge_kernel, out_shape=jax.ShapeDtypeStruct((images, hal...  7.27 us
    ppermute x2, starting transfers between devices, on_device(): sent.append(lax.ppermute(own_image, ('req', 'tensor'), perm))  6.96 us
    ppermute x2, waiting for transfers between devices, tensor_sum(): other = lax.ppermute(mine, 'tensor', [(0, 1), (1, 0)])  5.74 us
    reduce_sum x2, other arithmetic, normalize(): center = values - jnp.mean(values, axis=-1, keepdims=True)  4.31 us
    select_n x1, other arithmetic, on_device(): jnp.where(prompt_valid[None, :, None], decoded, jnp.zeros_like(decoded))  3.82 us
    ppermute x2, starting transfers between devices, tensor_sum(): other = lax.ppermute(mine, 'tensor', [(0, 1), (1, 0)])  3.74 us
  transfers between devices with their start and end apart: 7, of which 5 were waited for; matrix products, arithmetic and copies ran while one was open for 3% of the time, Pallas kernels for 0%

profile of v7, /device:TPU:1, one launch (start us, length us, event | category | flops | bytes accessed | tf_op | source)
XLA Modules:
  0.0 102.1 jit_solution(16278941387830230075)
XLA Ops:
  0.0 0.7 constant_dynamic-slice_fusion
  0.8 1.3 %reshape.275.gain_ref = f32[1,1280]{1,0:T(1,128)} reshape(f32[1280]{0:T(1024)} %param.25) | data formatting | bytes 10240 | tf_op jit(solution)/shard_map/reshape | solution.py:180
  2.1 0.7 and_convert_fusion.valid_ref
  2.7 0.0 copy-start.5
  2.7 11.6 %shard_map.163 = bf16[2,256,1280]{2,1,0:T(8,128)(2,1)} custom-call(bf16[2,256,1280]{2,1,0:T(8,128)(2,1)} %x_ref.1, f32[1,1280]{1,0:T(1,128)} %reshape.275.gain_ref, bf16[3,1280,640]{2,1,0:T(8,128)(2,1)} %bitcast.40, s32[2,1,256]{2,1,0:T(1,128)} %and_convert_fusion.valid_ref, bf16[640,1280]{1,0:T(8,128)(2,1)} %wo_ref.2), custom_call_target="tpu_custom_call" | custom-call | flops 4429185024 | bytes 9175040 | tf_op jit(solution)/shard_map/pallas_call | solution.py:159
  14.3 3.2 %collective-permute-start = (bf16[2,256,1280]{2,1,0:T(8,128)(2,1)}, bf16[2,256,1280]{2,1,0:T(8,128)(2,1)S(1)}, u32[]{:S(2)}, u32[]{:S(2)}) collective-permute-start(bf16[2,256,1280]{2,1,0:T(8,128)(2,1)} %shard_map.163), channel_id=1, source_target_pairs={{0,1},{1,0},{2,3},{3,2},{4,5},{5,4},{6,7},{7,6},{8,9},{9,8},{10,11... | collective-permute-start | bytes 3932168 | tf_op jit(solution)/shard_map/ppermute | solution.py:23
  17.5 2.9 %collective-permute-done = bf16[2,256,1280]{2,1,0:T(8,128)(2,1)S(1)} collective-permute-done((bf16[2,256,1280]{2,1,0:T(8,128)(2,1)}, bf16[2,256,1280]{2,1,0:T(8,128)(2,1)S(1)}, u32[]{:S(2)}, u32[]{:S(2)}) %collective-permute-start) | collective-permute-done | bytes 1310752 | tf_op jit(solution)/shard_map/ppermute | solution.py:23
  20.4 0.0 copy-done.5
  20.4 1.9 %fusion.7 = (f32[2,256]{1,0:T(2,128)S(1)}, f32[2,256,1280]{2,1,0:T(8,128)S(1)}) fusion(bf16[2,256,1280]{2,1,0:T(8,128)(2,1)S(1)} %collective-permute-done, bf16[2,256,1280]{2,1,0:T(8,128)(2,1)} %shard_map.163, bf16[2,256,1280]{2,1,0:T(8,128)(2,1)S(1)} %copy-done.5), kind=kLoop, calls=%fused_computation.47 | loop fusion | flops 3931648 | bytes 6555648 | tf_op jit(solution)/shard_map/reduce_sum | solution.py:16
  22.3 0.0 copy-start
  22.3 0.0 copy-start.6
  22.4 0.4 multiply_reduce_fusion.1
  22.8 0.3 copy-done.6
  23.1 1.5 %multiply_convert_fusion.1 = bf16[2,256,1280]{2,1,0:T(8,128)(2,1)} fusion(f32[2,256,1280]{2,1,0:T(8,128)S(1)} %get-tuple-element.6.res_ref, f32[1280]{0:T(1024)S(1)} %copy-done.6, f32[2,256]{1,0:T(2,128)S(1)} %add_rsqrt_fusion.1, f32[2,256]{1,0:T(2,128)S(1)} %broadcast_multiply_fusion.1), kind=kLoop, calls=%fused_computation.4 | loop fusion | flops 2621440 | bytes 3941376 | tf_op jit(solution)/shard_map/convert_element_type | solution.py:192
  24.5 0.0 copy-done
  24.5 0.0 copy-start.10
  24.5 0.0 copy-start.9
  24.5 11.9 %shard_map.164 = bf16[512,1280]{1,0:T(8,128)(2,1)} custom-call(bf16[512,1280]{1,0:T(8,128)(2,1)} %bitcast.37, bf16[1280,2560]{1,0:T(8,128)(2,1)} %w1_ref.2, bf16[2560,1280]{1,0:T(8,128)(2,1)} %w2_ref.2), custom_call_target="tpu_custom_call" | custom-call | flops 6710886400 | bytes 15728640 | tf_op jit(solution)/shard_map/pallas_call | solution.py:50
  36.5 0.4 collective-permute-start.1
  36.8 0.0 copy-done.10
  36.8 0.6 dynamic_slice.12
  39.4 0.0 copy-done.9
  39.4 0.1 constant_dynamic-slice_fusion.2
  39.5 0.1 add_select_fusion
  39.6 0.0 copy-start.8
  39.6 0.1 collective-permute-done.1.other_ref
  39.7 0.0 copy-start.4
  39.7 1.1 %copy-done.4 = bf16[2,256,1280]{2,1,0:T(8,128)(2,1)} copy-done((bf16[2,256,1280]{2,1,0:T(8,128)(2,1)}, bf16[2,256,1280]{2,1,0:T(8,128)(2,1)S(1)}, u32[]{:S(2)}) %copy-start.4) | copy-done | bytes 1310744
  40.8 7.3 %shard_map.165 = bf16[2,64,640]{2,1,0:T(8,128)(2,1)} custom-call(f32[2,256,1280]{2,1,0:T(8,128)} %copy-done, bf16[2,256,1280]{2,1,0:T(8,128)(2,1)} %bitcast.36, bf16[2,256,1280]{2,1,0:T(8,128)(2,1)} %copy-done.4, bf16[5120,640]{1,0:T(8,128)(2,1)} %w_ref.1), custom_call_target="tpu_custom_call" | custom-call | flops 922746880 | bytes 11796480 | tf_op jit(solution)/shard_map/pallas_call | solution.py:106
  48.0 0.0 copy-start.1
  48.0 1.0 %broadcast_select_fusion.2 = bf16[64,640]{1,0:T(8,128)(2,1)S(1)} fusion(pred[]{:T(512)S(6)} %eq.6, bf16[2,64,640]{2,1,0:T(8,128)(2,1)} %shard_map.165), kind=kLoop, calls=%fused_computation.16 | loop fusion | flops 40960 | bytes 245761 | tf_op jit(solution)/shard_map/jit(_where)/select_n | solution.py:248
  49.1 0.5 collective-permute-start.2
  49.5 0.9 slice_bitcast_fusion
  50.5 0.0 collective-permute-done.2
  50.5 5.3 %collective-permute-start.4 = (bf16[64,1280]{1,0:T(8,128)(2,1)S(1)}, bf16[64,1280]{1,0:T(8,128)(2,1)S(1)}, u32[]{:S(2)}, u32[]{:S(2)}) collective-permute-start(bf16[64,1280]{1,0:T(8,128)(2,1)S(1)} %maximum_select_fusion.1), channel_id=1, source_target_pairs={{0,2},{1,129},{2,0},{3,131},{4,6},{5,133},{6,4},{7,135},{8,10},{9,... | collective-permute-start | bytes 491528 | tf_op jit(solution)/shard_map/ppermute | solution.py:261
  55.8 1.7 %collective-permute-start.3 = (bf16[64,1280]{1,0:T(8,128)(2,1)S(1)}, bf16[64,1280]{1,0:T(8,128)(2,1)S(1)}, u32[]{:S(2)}, u32[]{:S(2)}) collective-permute-start(bf16[64,1280]{1,0:T(8,128)(2,1)S(1)} %maximum_select_fusion.1), channel_id=1, source_target_pairs={{0,3},{1,128},{2,1},{3,130},{4,7},{5,132},{6,5},{7,134},{8,11},{9,... | collective-permute-start | bytes 491528 | tf_op jit(solution)/shard_map/ppermute | solution.py:261
  57.5 0.1 compare_and_fusion
  57.6 0.1 and.78
  57.7 0.0 copy-done.8
  57.7 0.6 reshape.278.gain_ref
  58.2 0.6 fusion.8
  58.8 0.0 collective-permute-done.4
  58.8 1.9 %collective-permute-done.3 = bf16[64,1280]{1,0:T(8,128)(2,1)S(1)} collective-permute-done((bf16[64,1280]{1,0:T(8,128)(2,1)S(1)}, bf16[64,1280]{1,0:T(8,128)(2,1)S(1)}, u32[]{:S(2)}, u32[]{:S(2)}) %collective-permute-start.3) | collective-permute-done | bytes 163872 | tf_op jit(solution)/shard_map/ppermute | solution.py:261
  60.8 0.1 maximum_select_fusion
  60.8 0.0 copy-done.1
  60.8 1.1 %maximum_bitcast_fusion.x_ref = bf16[1,512,1280]{2,1,0:T(8,128)(2,1)} fusion(bf16[384,1280]{1,0:T(8,128)(2,1)S(1)} %bitcast.30, bf16[128,1280]{1,0:T(8,128)(2,1)S(1)} %maximum_select_fusion), kind=kLoop, calls=%fused_computation.9 | loop fusion | flops 2621440 | bytes 2621440 | tf_op jit(solution)/shard_map/broadcast_in_dim | solution.py:281
  62.0 12.7 %shard_map.166 = bf16[1,512,1280]{2,1,0:T(8,128)(2,1)} custom-call(bf16[1,512,1280]{2,1,0:T(8,128)(2,1)} %maximum_bitcast_fusion.x_ref, f32[1,1280]{1,0:T(1,128)} %reshape.278.gain_ref, bf16[3,1280,640]{2,1,0:T(8,128)(2,1)} %bitcast.41, s32[1,1,512]{2,1,0:T(1,128)} %bitcast.39, bf16[640,1280]{1,0:T(8,128)(2,1)} %wo_ref.3), custom_call_target="tpu_custom_call" | custom-call | flops 5502926848 | bytes 9175040 | tf_op jit(solution)/shard_map/pallas_call | solution.py:159
  74.7 0.0 copy-start.2
  74.7 0.5 collective-permute-start.5
  75.2 2.9 %collective-permute-done.5 = bf16[1,512,1280]{2,1,0:T(8,128)(2,1)S(1)} collective-permute-done((bf16[1,512,1280]{2,1,0:T(8,128)(2,1)}, bf16[1,512,1280]{2,1,0:T(8,128)(2,1)S(1)}, u32[]{:S(2)}, u32[]{:S(2)}) %collective-permute-start.5) | collective-permute-done | bytes 1310752 | tf_op jit(solution)/shard_map/ppermute | solution.py:23
  78.0 0.0 copy-start.3
  78.0 2.4 %fusion.6 = f32[512]{0:T(512)S(1)} fusion(bf16[1,512,1280]{2,1,0:T(8,128)(2,1)S(1)} %collective-permute-done.5, bf16[1,512,1280]{2,1,0:T(8,128)(2,1)} %shard_map.166, bf16[1,384,1280]{2,1,0:T(8,128)(2,1)S(1)} %copy-done.1, bf16[1,128,1280]{2,1,0:T(8,128)(2,1)S(1)} %bitcast.31), kind=kLoop, calls=%fused_computation.46 | loop fusion | flops 5897728 | bytes 3934208 | tf_op jit(solution)/shard_map/reduce_sum | solution.py:16
  80.4 0.0 copy-start.7
  80.5 0.0 copy-done.2
  80.5 0.8 multiply_reduce_fusion
  81.3 0.0 copy-done.3
  81.3 0.0 copy-done.7
  81.3 1.8 %fusion.x_ref = bf16[512,1280]{1,0:T(8,128)(2,1)} fusion(f32[1280]{0:T(1024)S(1)} %copy-done.7, f32[512]{0:T(512)S(1)} %add_rsqrt_fusion, f32[512]{0:T(512)S(1)} %broadcast_multiply_fusion, bf16[1,512,1280]{2,1,0:T(8,128)(2,1)S(1)} %collective-permute-done.5, bf16[1,512,1280]{2,1,0:T(8,128)(2,1)S(1)} %copy-done.2, bf16[1,384,1280]{2,1,0:T(8,128)(2,1)S(1)} %copy-done.1, ...), kind=kLoop, calls=%fused_computation.7 | loop fusion | flops 7864320 | bytes 5252096 | tf_op jit(solution)/shard_map/reshape | solution.py:194
  83.1 11.9 %shard_map.167 = bf16[512,1280]{1,0:T(8,128)(2,1)} custom-call(bf16[512,1280]{1,0:T(8,128)(2,1)} %fusion.x_ref, bf16[1280,2560]{1,0:T(8,128)(2,1)} %w1_ref.3, bf16[2560,1280]{1,0:T(8,128)(2,1)} %w2_ref.3), custom_call_target="tpu_custom_call" | custom-call | flops 6710886400 | bytes 15728640 | tf_op jit(solution)/shard_map/pallas_call | solution.py:50
  95.0 0.4 collective-permute-start.6
  95.4 2.9 %collective-permute-done.6 = bf16[1,512,1280]{2,1,0:T(8,128)(2,1)S(1)} collective-permute-done((bf16[1,512,1280]{2,1,0:T(8,128)(2,1)}, bf16[1,512,1280]{2,1,0:T(8,128)(2,1)S(1)}, u32[]{:S(2)}, u32[]{:S(2)}) %collective-permute-start.6) | collective-permute-done | bytes 1310752 | tf_op jit(solution)/shard_map/ppermute | solution.py:196
  98.3 3.8 %fusion.1 = bf16[1,512,1280]{2,1,0:T(8,128)(2,1)} fusion(bf16[1,512,1280]{2,1,0:T(8,128)(2,1)S(1)} %collective-permute-done.6, pred[512]{0:T(512)(128)(4,1)S(1)} %get-tuple-element.17, bf16[512,1280]{1,0:T(8,128)(2,1)} %shard_map.167, bf16[1,512,1280]{2,1,0:T(8,128)(2,1)} %copy-done.3, bf16[1,512,1280]{2,1,0:T(8,128)(2,1)S(1)} %copy-done.2, ...), kind=kLoop, calls=%fused_computation.8 | loop fusion | flops 9175040 | bytes 7864832 | tf_op jit(solution)/shard_map/jit(_where)/select_n | solution.py:297
  (10 shorter events, 0.1 us)
Async XLA Ops:
  2.7 17.7 %copy-start.5 = (bf16[2,256,1280]{2,1,0:T(8,128)(2,1)S(1)}, bf16[2,256,1280]{2,1,0:T(8,128)(2,1)}, u32[]{:S(2)}) copy-start(bf16[2,256,1280]{2,1,0:T(8,128)(2,1)} %x_ref.1) | copy-start | bytes 3932164
  14.3 6.1 %collective-permute-start = (bf16[2,256,1280]{2,1,0:T(8,128)(2,1)}, bf16[2,256,1280]{2,1,0:T(8,128)(2,1)S(1)}, u32[]{:S(2)}, u32[]{:S(2)}) collective-permute-start(bf16[2,256,1280]{2,1,0:T(8,128)(2,1)} %shard_map.163), channel_id=1, source_target_pairs={{0,1},{1,0},{2,3},{3,2},{4,5},{5,4},{6,7},{7,6},{8,9},{9,8},{10,11... | collective-permute-start | bytes 3932168 | tf_op jit(solution)/shard_map/ppermute | solution.py:23
  22.3 2.2 %copy-start = (f32[2,256,1280]{2,1,0:T(8,128)}, f32[2,256,1280]{2,1,0:T(8,128)S(1)}, u32[]{:S(2)}) copy-start(f32[2,256,1280]{2,1,0:T(8,128)S(1)} %get-tuple-element.6.res_ref) | copy-start | bytes 7864324
  22.3 0.7 copy-start.6
  24.5 12.3 %copy-start.10 = (s32[256]{0:T(256)S(1)}, s32[256]{0:T(256)}, u32[]{:S(2)}) copy-start(s32[256]{0:T(256)} %param.19) | copy-start | bytes 3076
  24.5 14.9 %copy-start.9 = (s32[256,2]{0,1:T(2,128)S(1)}, s32[256,2]{0,1:T(2,128)}, u32[]{:S(2)}) copy-start(s32[256,2]{0,1:T(2,128)} %param.18) | copy-start | bytes 6148
  36.5 3.2 %collective-permute-start.1 = (bf16[2,256,1280]{2,1,0:T(8,128)(2,1)}, bf16[2,256,1280]{2,1,0:T(8,128)(2,1)S(1)}, u32[]{:S(2)}, u32[]{:S(2)}) collective-permute-start(bf16[2,256,1280]{2,1,0:T(8,128)(2,1)} %bitcast.35), channel_id=1, source_target_pairs={{0,1},{1,0},{2,3},{3,2},{4,5},{5,4},{6,7},{7,6},{8,9},{9,8},{10,11... | collective-permute-start | bytes 3932168 | tf_op jit(solution)/shard_map/ppermute | solution.py:196
  39.6 18.1 %copy-start.8 = (f32[1280]{0:T(1024)S(1)}, f32[1280]{0:T(1024)}, u32[]{:S(2)}) copy-start(f32[1280]{0:T(1024)} %param.32) | copy-start | bytes 15364
  39.7 1.1 %copy-start.4 = (bf16[2,256,1280]{2,1,0:T(8,128)(2,1)}, bf16[2,256,1280]{2,1,0:T(8,128)(2,1)S(1)}, u32[]{:S(2)}) copy-start(bf16[2,256,1280]{2,1,0:T(8,128)(2,1)S(1)} %collective-permute-done.1.other_ref) | copy-start | bytes 3932164
  48.0 12.8 %copy-start.1 = (bf16[1,384,1280]{2,1,0:T(8,128)(2,1)S(1)}, bf16[1,384,1280]{2,1,0:T(8,128)(2,1)}, u32[]{:S(2)}) copy-start(bf16[1,384,1280]{2,1,0:T(8,128)(2,1)} %param.20) | copy-start | bytes 2949124
  49.1 1.4 %collective-permute-start.2 = (bf16[64,640]{1,0:T(8,128)(2,1)S(1)}, bf16[64,640]{1,0:T(8,128)(2,1)S(1)}, u32[]{:S(2)}, u32[]{:S(2)}) collective-permute-start(bf16[64,640]{1,0:T(8,128)(2,1)S(1)} %broadcast_select_fusion.2), channel_id=1, source_target_pairs={{0,1},{1,0},{2,3},{3,2},{4,5},{5,4},{6,7},{7,6},{8,9},{9,8},{10,11... | collective-permute-start | bytes 245768 | tf_op jit(solution)/shard_map/ppermute | solution.py:248
  50.5 8.3 %collective-permute-start.4 = (bf16[64,1280]{1,0:T(8,128)(2,1)S(1)}, bf16[64,1280]{1,0:T(8,128)(2,1)S(1)}, u32[]{:S(2)}, u32[]{:S(2)}) collective-permute-start(bf16[64,1280]{1,0:T(8,128)(2,1)S(1)} %maximum_select_fusion.1), channel_id=1, source_target_pairs={{0,2},{1,129},{2,0},{3,131},{4,6},{5,133},{6,4},{7,135},{8,10},{9,... | collective-permute-start | bytes 491528 | tf_op jit(solution)/shard_map/ppermute | solution.py:261
  55.8 4.9 %collective-permute-start.3 = (bf16[64,1280]{1,0:T(8,128)(2,1)S(1)}, bf16[64,1280]{1,0:T(8,128)(2,1)S(1)}, u32[]{:S(2)}, u32[]{:S(2)}) collective-permute-start(bf16[64,1280]{1,0:T(8,128)(2,1)S(1)} %maximum_select_fusion.1), channel_id=1, source_target_pairs={{0,3},{1,128},{2,1},{3,130},{4,7},{5,132},{6,5},{7,134},{8,11},{9,... | collective-permute-start | bytes 491528 | tf_op jit(solution)/shard_map/ppermute | solution.py:261
  74.7 5.8 %copy-start.2 = (bf16[1,512,1280]{2,1,0:T(8,128)(2,1)S(1)}, bf16[1,512,1280]{2,1,0:T(8,128)(2,1)}, u32[]{:S(2)}) copy-start(bf16[1,512,1280]{2,1,0:T(8,128)(2,1)} %shard_map.166) | copy-start | bytes 3932164
  74.7 3.4 %collective-permute-start.5 = (bf16[1,512,1280]{2,1,0:T(8,128)(2,1)}, bf16[1,512,1280]{2,1,0:T(8,128)(2,1)S(1)}, u32[]{:S(2)}, u32[]{:S(2)}) collective-permute-start(bf16[1,512,1280]{2,1,0:T(8,128)(2,1)} %shard_map.166), channel_id=1, source_target_pairs={{0,1},{1,0},{2,3},{3,2},{4,5},{5,4},{6,7},{7,6},{8,9},{9,8},{10,11... | collective-permute-start | bytes 3932168 | tf_op jit(solution)/shard_map/ppermute | solution.py:23
  78.0 3.2 %copy-start.3 = (bf16[1,512,1280]{2,1,0:T(8,128)(2,1)}, bf16[1,512,1280]{2,1,0:T(8,128)(2,1)S(1)}, u32[]{:S(2)}) copy-start(bf16[1,512,1280]{2,1,0:T(8,128)(2,1)S(1)} %collective-permute-done.5) | copy-start | bytes 3932164
  80.4 0.8 copy-start.7
  95.0 3.2 %collective-permute-start.6 = (bf16[1,512,1280]{2,1,0:T(8,128)(2,1)}, bf16[1,512,1280]{2,1,0:T(8,128)(2,1)S(1)}, u32[]{:S(2)}, u32[]{:S(2)}) collective-permute-start(bf16[1,512,1280]{2,1,0:T(8,128)(2,1)} %bitcast.38), channel_id=1, source_target_pairs={{0,1},{1,0},{2,3},{3,2},{4,5},{5,4},{6,7},{7,6},{8,9},{9,8},{10,11... | collective-permute-start | bytes 3932168 | tf_op jit(solution)/shard_map/ppermute | solution.py:196

commit v8 on v7

--- a/solution.py
+++ b/solution.py
@@ -124,12 +124,17 @@
     for j, ref in enumerate((q_ref, k_ref, v_ref)):
         ref[...] = jnp.dot(first, w_ref[j], preferred_element_type=jnp.float32).astype(ref.dtype)
     keys = valid_ref[0] > 0
-    if causal:
-        row = lax.broadcasted_iota(jnp.int32, (length, length), 0)
-        col = lax.broadcasted_iota(jnp.int32, (length, length), 1)
-        allowed = keys & (col <= row)
-    else:
-        allowed = jnp.broadcast_to(keys, (length, length))
+    blocks = 2 if causal else 1
+    block = length // blocks
+    allowed = []
+    for qi in range(blocks):
+        seen = (qi + 1) * block if causal else length
+        if causal:
+            row = lax.broadcasted_iota(jnp.int32, (block, seen), 0) + qi * block
+            col = lax.broadcasted_iota(jnp.int32, (block, seen), 1)
+            allowed.append(keys[:, :seen] & (col <= row))
+        else:
+            allowed.append(jnp.broadcast_to(keys, (block, seen)))
     acc_ref[...] = jnp.zeros_like(acc_ref)
     for h in range(width // HEAD_DIM):
         start = min((h * HEAD_DIM) // 128 * 128, width - window)
@@ -137,17 +142,20 @@
         lane = lax.broadcasted_iota(jnp.int32, (1, window), 1) + start
         mine = (lane >= h * HEAD_DIM) & (lane < (h + 1) * HEAD_DIM)
         zero = jnp.zeros((), q_ref.dtype)
-        queries = jnp.where(mine, q_ref[:, lanes], zero)
-        scores = lax.dot_general(
-            queries, k_ref[:, lanes], (((1,), (1,)), ((), ())),
-            preferred_element_type=jnp.float32,
-        ) * HEAD_DIM ** (-0.5)
-        scores = jnp.where(allowed, scores, jnp.float32(-1e30))
-        top = jnp.max(scores, axis=-1, keepdims=True)
-        raised = jnp.exp(scores - top)
-        probs = (raised / jnp.sum(raised, axis=-1, keepdims=True)).astype(jnp.bfloat16)
-        values_h = jnp.where(mine, v_ref[:, lanes], zero)
-        acc_ref[:, lanes] += jnp.dot(probs, values_h, preferred_element_type=jnp.float32)
+        for qi in range(blocks):
+            seen = (qi + 1) * block if causal else length
+            rows = pl.ds(qi * block, block)
+            queries = jnp.where(mine, q_ref[rows, lanes], zero)
+            scores = lax.dot_general(
+                queries, k_ref[pl.ds(0, seen), lanes], (((1,), (1,)), ((), ())),
+                preferred_element_type=jnp.float32,
+            ) * HEAD_DIM ** (-0.5)
+            scores = jnp.where(allowed[qi], scores, jnp.float32(-1e30))
+            top = jnp.max(scores, axis=-1, keepdims=True)
+            raised = jnp.exp(scores - top)
+            probs = (raised / jnp.sum(raised, axis=-1, keepdims=True)).astype(jnp.bfloat16)
+            values_h = jnp.where(mine, v_ref[pl.ds(0, seen), lanes], zero)
+            acc_ref[rows, lanes] += jnp.dot(probs, values_h, preferred_element_type=jnp.float32)
     mixed = acc_ref[...].astype(jnp.bfloat16)
     o_ref[0] = jnp.dot(mixed, wo_ref[...], preferred_element_type=jnp.float32).astype(o_ref.dtype)
 

time: 104 us -> 105 us (level)
  Pallas kernels: 55.4 us -> 56.5 us
    pallas_call x2, Pallas kernels: 24.3 us -> 25.3 us  [attend(): pl.pallas_call(functools.partial(_attention_kernel, causal), out_shape=ja...]
where the time goes in v8:
time: 105 us; the launch traced here: 103 us
  Pallas kernels  56.5 us (54%)
  other arithmetic  16.3 us (16%)
  starting transfers between devices  11.9 us (11%)
  waiting for transfers between devices  10.7 us (10%)
  local copies, waits for them, and re-layouts  5.72 us (5%)
  between operations  2.11 us (2%)
    pallas_call x2, Pallas kernels, attend(): pl.pallas_call(functools.partial(_attention_kernel, causal), out_shape=ja...  25.3 us
    pallas_call x2, Pallas kernels, feed_forward(): pl.pallas_call(functools.partial(_feed_forward_kernel, rows_per_step), ou...  23.9 us
    pallas_call x1, Pallas kernels, merge(): pl.pallas_call(_merge_kernel, out_shape=jax.ShapeDtypeStruct((images, hal...  7.27 us
    ppermute x2, starting transfers between devices, on_device(): sent.append(lax.ppermute(own_image, ('req', 'tensor'), perm))  6.96 us
    ppermute x2, waiting for transfers between devices, tensor_sum(): other = lax.ppermute(mine, 'tensor', [(0, 1), (1, 0)])  5.74 us
    reduce_sum x2, other arithmetic, normalize(): center = values - jnp.mean(values, axis=-1, keepdims=True)  4.31 us
    select_n x1, other arithmetic, on_device(): jnp.where(prompt_valid[None, :, None], decoded, jnp.zeros_like(decoded))  3.82 us
    ppermute x2, starting transfers between devices, tensor_sum(): other = lax.ppermute(mine, 'tensor', [(0, 1), (1, 0)])  3.73 us
  transfers between devices with their start and end apart: 7, of which 5 were waited for; matrix products, arithmetic and copies ran while one was open for 3% of the time, Pallas kernels for 0%

profile of v8, /device:TPU:1, one launch (start us, length us, event | category | flops | bytes accessed | tf_op | source)
XLA Modules:
  0.0 103.2 jit_solution(10615646445460823446)
XLA Ops:
  0.0 0.7 constant_dynamic-slice_fusion
  0.8 1.3 %reshape.275.gain_ref = f32[1,1280]{1,0:T(1,128)} reshape(f32[1280]{0:T(1024)} %param.25) | data formatting | bytes 10240 | tf_op jit(solution)/shard_map/reshape | solution.py:188
  2.1 0.7 and_convert_fusion.valid_ref
  2.7 0.0 copy-start.5
  2.7 11.6 %shard_map.163 = bf16[2,256,1280]{2,1,0:T(8,128)(2,1)} custom-call(bf16[2,256,1280]{2,1,0:T(8,128)(2,1)} %x_ref.1, f32[1,1280]{1,0:T(1,128)} %reshape.275.gain_ref, bf16[3,1280,640]{2,1,0:T(8,128)(2,1)} %bitcast.40, s32[2,1,256]{2,1,0:T(1,128)} %and_convert_fusion.valid_ref, bf16[640,1280]{1,0:T(8,128)(2,1)} %wo_ref.2), custom_call_target="tpu_custom_call" | custom-call | flops 4429185024 | bytes 9175040 | tf_op jit(solution)/shard_map/pallas_call | solution.py:167
  14.3 3.2 %collective-permute-start = (bf16[2,256,1280]{2,1,0:T(8,128)(2,1)}, bf16[2,256,1280]{2,1,0:T(8,128)(2,1)S(1)}, u32[]{:S(2)}, u32[]{:S(2)}) collective-permute-start(bf16[2,256,1280]{2,1,0:T(8,128)(2,1)} %shard_map.163), channel_id=1, source_target_pairs={{0,1},{1,0},{2,3},{3,2},{4,5},{5,4},{6,7},{7,6},{8,9},{9,8},{10,11... | collective-permute-start | bytes 3932168 | tf_op jit(solution)/shard_map/ppermute | solution.py:23
  17.5 2.9 %collective-permute-done = bf16[2,256,1280]{2,1,0:T(8,128)(2,1)S(1)} collective-permute-done((bf16[2,256,1280]{2,1,0:T(8,128)(2,1)}, bf16[2,256,1280]{2,1,0:T(8,128)(2,1)S(1)}, u32[]{:S(2)}, u32[]{:S(2)}) %collective-permute-start) | collective-permute-done | bytes 1310752 | tf_op jit(solution)/shard_map/ppermute | solution.py:23
  20.4 0.0 copy-done.5
  20.4 1.9 %fusion.7 = (f32[2,256]{1,0:T(2,128)S(1)}, f32[2,256,1280]{2,1,0:T(8,128)S(1)}) fusion(bf16[2,256,1280]{2,1,0:T(8,128)(2,1)S(1)} %collective-permute-done, bf16[2,256,1280]{2,1,0:T(8,128)(2,1)} %shard_map.163, bf16[2,256,1280]{2,1,0:T(8,128)(2,1)S(1)} %copy-done.5), kind=kLoop, calls=%fused_computation.47 | loop fusion | flops 3931648 | bytes 6555648 | tf_op jit(solution)/shard_map/reduce_sum | solution.py:16
  22.3 0.0 copy-start
  22.3 0.0 copy-start.6
  22.4 0.4 multiply_reduce_fusion.1
  22.8 0.3 copy-done.6
  23.1 1.5 %multiply_convert_fusion.1 = bf16[2,256,1280]{2,1,0:T(8,128)(2,1)} fusion(f32[2,256,1280]{2,1,0:T(8,128)S(1)} %get-tuple-element.6.res_ref, f32[1280]{0:T(1024)S(1)} %copy-done.6, f32[2,256]{1,0:T(2,128)S(1)} %add_rsqrt_fusion.1, f32[2,256]{1,0:T(2,128)S(1)} %broadcast_multiply_fusion.1), kind=kLoop, calls=%fused_computation.4 | loop fusion | flops 2621440 | bytes 3941376 | tf_op jit(solution)/shard_map/convert_element_type | solution.py:200
  24.5 0.0 copy-done
  24.5 0.0 copy-start.10
  24.5 0.0 copy-start.9
  24.5 11.9 %shard_map.164 = bf16[512,1280]{1,0:T(8,128)(2,1)} custom-call(bf16[512,1280]{1,0:T(8,128)(2,1)} %bitcast.37, bf16[1280,2560]{1,0:T(8,128)(2,1)} %w1_ref.2, bf16[2560,1280]{1,0:T(8,128)(2,1)} %w2_ref.2), custom_call_target="tpu_custom_call" | custom-call | flops 6710886400 | bytes 15728640 | tf_op jit(solution)/shard_map/pallas_call | solution.py:50
  36.5 0.4 collective-permute-start.1
  36.8 0.0 copy-done.10
  36.8 0.6 dynamic_slice.12
  39.4 0.0 copy-done.9
  39.4 0.1 constant_dynamic-slice_fusion.2
  39.5 0.1 add_select_fusion
  39.6 0.0 copy-start.8
  39.6 0.1 collective-permute-done.1.other_ref
  39.7 0.0 copy-start.4
  39.7 1.1 %copy-done.4 = bf16[2,256,1280]{2,1,0:T(8,128)(2,1)} copy-done((bf16[2,256,1280]{2,1,0:T(8,128)(2,1)}, bf16[2,256,1280]{2,1,0:T(8,128)(2,1)S(1)}, u32[]{:S(2)}) %copy-start.4) | copy-done | bytes 1310744
  40.8 7.3 %shard_map.165 = bf16[2,64,640]{2,1,0:T(8,128)(2,1)} custom-call(f32[2,256,1280]{2,1,0:T(8,128)} %copy-done, bf16[2,256,1280]{2,1,0:T(8,128)(2,1)} %bitcast.36, bf16[2,256,1280]{2,1,0:T(8,128)(2,1)} %copy-done.4, bf16[5120,640]{1,0:T(8,128)(2,1)} %w_ref.1), custom_call_target="tpu_custom_call" | custom-call | flops 922746880 | bytes 11796480 | tf_op jit(solution)/shard_map/pallas_call | solution.py:106
  48.0 0.0 copy-start.1
  48.0 1.0 broadcast_select_fusion.2
  49.1 0.5 collective-permute-start.2
  49.5 0.9 slice_bitcast_fusion
  50.5 0.0 collective-permute-done.2
  50.5 5.3 %collective-permute-start.4 = (bf16[64,1280]{1,0:T(8,128)(2,1)S(1)}, bf16[64,1280]{1,0:T(8,128)(2,1)S(1)}, u32[]{:S(2)}, u32[]{:S(2)}) collective-permute-start(bf16[64,1280]{1,0:T(8,128)(2,1)S(1)} %maximum_select_fusion.1), channel_id=1, source_target_pairs={{0,2},{1,129},{2,0},{3,131},{4,6},{5,133},{6,4},{7,135},{8,10},{9,... | collective-permute-start | bytes 491528 | tf_op jit(solution)/shard_map/ppermute | solution.py:269
  55.8 1.7 %collective-permute-start.3 = (bf16[64,1280]{1,0:T(8,128)(2,1)S(1)}, bf16[64,1280]{1,0:T(8,128)(2,1)S(1)}, u32[]{:S(2)}, u32[]{:S(2)}) collective-permute-start(bf16[64,1280]{1,0:T(8,128)(2,1)S(1)} %maximum_select_fusion.1), channel_id=1, source_target_pairs={{0,3},{1,128},{2,1},{3,130},{4,7},{5,132},{6,5},{7,134},{8,11},{9,... | collective-permute-start | bytes 491528 | tf_op jit(solution)/shard_map/ppermute | solution.py:269
  57.5 0.1 compare_and_fusion
  57.6 0.1 and.78
  57.7 0.0 copy-done.8
  57.7 0.6 reshape.278.gain_ref
  58.2 0.6 fusion.8
  58.8 0.0 collective-permute-done.4
  58.8 1.9 %collective-permute-done.3 = bf16[64,1280]{1,0:T(8,128)(2,1)S(1)} collective-permute-done((bf16[64,1280]{1,0:T(8,128)(2,1)S(1)}, bf16[64,1280]{1,0:T(8,128)(2,1)S(1)}, u32[]{:S(2)}, u32[]{:S(2)}) %collective-permute-start.3) | collective-permute-done | bytes 163872 | tf_op jit(solution)/shard_map/ppermute | solution.py:269
  60.8 0.1 maximum_select_fusion
  60.8 0.0 copy-done.1
  60.8 1.1 %maximum_bitcast_fusion.x_ref = bf16[1,512,1280]{2,1,0:T(8,128)(2,1)} fusion(bf16[384,1280]{1,0:T(8,128)(2,1)S(1)} %bitcast.30, bf16[128,1280]{1,0:T(8,128)(2,1)S(1)} %maximum_select_fusion), kind=kLoop, calls=%fused_computation.9 | loop fusion | flops 2621440 | bytes 2621440 | tf_op jit(solution)/shard_map/broadcast_in_dim | solution.py:289
  62.0 13.7 %shard_map.166 = bf16[1,512,1280]{2,1,0:T(8,128)(2,1)} custom-call(bf16[1,512,1280]{2,1,0:T(8,128)(2,1)} %maximum_bitcast_fusion.x_ref, f32[1,1280]{1,0:T(1,128)} %reshape.278.gain_ref, bf16[3,1280,640]{2,1,0:T(8,128)(2,1)} %bitcast.41, s32[1,1,512]{2,1,0:T(1,128)} %bitcast.39, bf16[640,1280]{1,0:T(8,128)(2,1)} %wo_ref.3), custom_call_target="tpu_custom_call" | custom-call | flops 5502926848 | bytes 9175040 | tf_op jit(solution)/shard_map/pallas_call | solution.py:167
  75.7 0.0 copy-start.2
  75.7 0.5 collective-permute-start.5
  76.2 2.9 %collective-permute-done.5 = bf16[1,512,1280]{2,1,0:T(8,128)(2,1)S(1)} collective-permute-done((bf16[1,512,1280]{2,1,0:T(8,128)(2,1)}, bf16[1,512,1280]{2,1,0:T(8,128)(2,1)S(1)}, u32[]{:S(2)}, u32[]{:S(2)}) %collective-permute-start.5) | collective-permute-done | bytes 1310752 | tf_op jit(solution)/shard_map/ppermute | solution.py:23
  79.1 0.0 copy-start.3
  79.1 2.4 %fusion.6 = f32[512]{0:T(512)S(1)} fusion(bf16[1,512,1280]{2,1,0:T(8,128)(2,1)S(1)} %collective-permute-done.5, bf16[1,512,1280]{2,1,0:T(8,128)(2,1)} %shard_map.166, bf16[1,384,1280]{2,1,0:T(8,128)(2,1)S(1)} %copy-done.1, bf16[1,128,1280]{2,1,0:T(8,128)(2,1)S(1)} %bitcast.31), kind=kLoop, calls=%fused_computation.46 | loop fusion | flops 5897728 | bytes 3934208 | tf_op jit(solution)/shard_map/reduce_sum | solution.py:16
  81.5 0.0 copy-start.7
  81.5 0.0 copy-done.2
  81.5 0.8 multiply_reduce_fusion
  82.3 0.0 copy-done.3
  82.3 0.0 copy-done.7
  82.3 1.8 %fusion.x_ref = bf16[512,1280]{1,0:T(8,128)(2,1)} fusion(f32[1280]{0:T(1024)S(1)} %copy-done.7, f32[512]{0:T(512)S(1)} %add_rsqrt_fusion, f32[512]{0:T(512)S(1)} %broadcast_multiply_fusion, bf16[1,512,1280]{2,1,0:T(8,128)(2,1)S(1)} %collective-permute-done.5, bf16[1,512,1280]{2,1,0:T(8,128)(2,1)S(1)} %copy-done.2, bf16[1,384,1280]{2,1,0:T(8,128)(2,1)S(1)} %copy-done.1, ...), kind=kLoop, calls=%fused_computation.7 | loop fusion | flops 7864320 | bytes 5252096 | tf_op jit(solution)/shard_map/reshape | solution.py:202
  84.2 11.9 %shard_map.167 = bf16[512,1280]{1,0:T(8,128)(2,1)} custom-call(bf16[512,1280]{1,0:T(8,128)(2,1)} %fusion.x_ref, bf16[1280,2560]{1,0:T(8,128)(2,1)} %w1_ref.3, bf16[2560,1280]{1,0:T(8,128)(2,1)} %w2_ref.3), custom_call_target="tpu_custom_call" | custom-call | flops 6710886400 | bytes 15728640 | tf_op jit(solution)/shard_map/pallas_call | solution.py:50
  96.1 0.4 collective-permute-start.6
  96.5 2.9 %collective-permute-done.6 = bf16[1,512,1280]{2,1,0:T(8,128)(2,1)S(1)} collective-permute-done((bf16[1,512,1280]{2,1,0:T(8,128)(2,1)}, bf16[1,512,1280]{2,1,0:T(8,128)(2,1)S(1)}, u32[]{:S(2)}, u32[]{:S(2)}) %collective-permute-start.6) | collective-permute-done | bytes 1310752 | tf_op jit(solution)/shard_map/ppermute | solution.py:204
  99.4 3.8 %fusion.1 = bf16[1,512,1280]{2,1,0:T(8,128)(2,1)} fusion(bf16[1,512,1280]{2,1,0:T(8,128)(2,1)S(1)} %collective-permute-done.6, pred[512]{0:T(512)(128)(4,1)S(1)} %get-tuple-element.17, bf16[512,1280]{1,0:T(8,128)(2,1)} %shard_map.167, bf16[1,512,1280]{2,1,0:T(8,128)(2,1)} %copy-done.3, bf16[1,512,1280]{2,1,0:T(8,128)(2,1)S(1)} %copy-done.2, ...), kind=kLoop, calls=%fused_computation.8 | loop fusion | flops 9175040 | bytes 7864832 | tf_op jit(solution)/shard_map/jit(_where)/select_n | solution.py:305
  (10 shorter events, 0.1 us)
Async XLA Ops:
  2.7 17.7 %copy-start.5 = (bf16[2,256,1280]{2,1,0:T(8,128)(2,1)S(1)}, bf16[2,256,1280]{2,1,0:T(8,128)(2,1)}, u32[]{:S(2)}) copy-start(bf16[2,256,1280]{2,1,0:T(8,128)(2,1)} %x_ref.1) | copy-start | bytes 3932164
  14.3 6.1 %collective-permute-start = (bf16[2,256,1280]{2,1,0:T(8,128)(2,1)}, bf16[2,256,1280]{2,1,0:T(8,128)(2,1)S(1)}, u32[]{:S(2)}, u32[]{:S(2)}) collective-permute-start(bf16[2,256,1280]{2,1,0:T(8,128)(2,1)} %shard_map.163), channel_id=1, source_target_pairs={{0,1},{1,0},{2,3},{3,2},{4,5},{5,4},{6,7},{7,6},{8,9},{9,8},{10,11... | collective-permute-start | bytes 3932168 | tf_op jit(solution)/shard_map/ppermute | solution.py:23
  22.3 2.2 %copy-start = (f32[2,256,1280]{2,1,0:T(8,128)}, f32[2,256,1280]{2,1,0:T(8,128)S(1)}, u32[]{:S(2)}) copy-start(f32[2,256,1280]{2,1,0:T(8,128)S(1)} %get-tuple-element.6.res_ref) | copy-start | bytes 7864324
  22.3 0.7 copy-start.6
  24.5 12.3 %copy-start.10 = (s32[256]{0:T(256)S(1)}, s32[256]{0:T(256)}, u32[]{:S(2)}) copy-start(s32[256]{0:T(256)} %param.19) | copy-start | bytes 3076
  24.5 14.9 %copy-start.9 = (s32[256,2]{0,1:T(2,128)S(1)}, s32[256,2]{0,1:T(2,128)}, u32[]{:S(2)}) copy-start(s32[256,2]{0,1:T(2,128)} %param.18) | copy-start | bytes 6148
  36.5 3.2 %collective-permute-start.1 = (bf16[2,256,1280]{2,1,0:T(8,128)(2,1)}, bf16[2,256,1280]{2,1,0:T(8,128)(2,1)S(1)}, u32[]{:S(2)}, u32[]{:S(2)}) collective-permute-start(bf16[2,256,1280]{2,1,0:T(8,128)(2,1)} %bitcast.35), channel_id=1, source_target_pairs={{0,1},{1,0},{2,3},{3,2},{4,5},{5,4},{6,7},{7,6},{8,9},{9,8},{10,11... | collective-permute-start | bytes 3932168 | tf_op jit(solution)/shard_map/ppermute | solution.py:204
  39.6 18.1 %copy-start.8 = (f32[1280]{0:T(1024)S(1)}, f32[1280]{0:T(1024)}, u32[]{:S(2)}) copy-start(f32[1280]{0:T(1024)} %param.32) | copy-start | bytes 15364
  39.7 1.1 %copy-start.4 = (bf16[2,256,1280]{2,1,0:T(8,128)(2,1)}, bf16[2,256,1280]{2,1,0:T(8,128)(2,1)S(1)}, u32[]{:S(2)}) copy-start(bf16[2,256,1280]{2,1,0:T(8,128)(2,1)S(1)} %collective-permute-done.1.other_ref) | copy-start | bytes 3932164
  48.0 12.8 %copy-start.1 = (bf16[1,384,1280]{2,1,0:T(8,128)(2,1)S(1)}, bf16[1,384,1280]{2,1,0:T(8,128)(2,1)}, u32[]{:S(2)}) copy-start(bf16[1,384,1280]{2,1,0:T(8,128)(2,1)} %param.20) | copy-start | bytes 2949124
  49.1 1.4 %collective-permute-start.2 = (bf16[64,640]{1,0:T(8,128)(2,1)S(1)}, bf16[64,640]{1,0:T(8,128)(2,1)S(1)}, u32[]{:S(2)}, u32[]{:S(2)}) collective-permute-start(bf16[64,640]{1,0:T(8,128)(2,1)S(1)} %broadcast_select_fusion.2), channel_id=1, source_target_pairs={{0,1},{1,0},{2,3},{3,2},{4,5},{5,4},{6,7},{7,6},{8,9},{9,8},{10,11... | collective-permute-start | bytes 245768 | tf_op jit(solution)/shard_map/ppermute | solution.py:256
  50.5 8.3 %collective-permute-start.4 = (bf16[64,1280]{1,0:T(8,128)(2,1)S(1)}, bf16[64,1280]{1,0:T(8,128)(2,1)S(1)}, u32[]{:S(2)}, u32[]{:S(2)}) collective-permute-start(bf16[64,1280]{1,0:T(8,128)(2,1)S(1)} %maximum_select_fusion.1), channel_id=1, source_target_pairs={{0,2},{1,129},{2,0},{3,131},{4,6},{5,133},{6,4},{7,135},{8,10},{9,... | collective-permute-start | bytes 491528 | tf_op jit(solution)/shard_map/ppermute | solution.py:269
  55.8 4.9 %collective-permute-start.3 = (bf16[64,1280]{1,0:T(8,128)(2,1)S(1)}, bf16[64,1280]{1,0:T(8,128)(2,1)S(1)}, u32[]{:S(2)}, u32[]{:S(2)}) collective-permute-start(bf16[64,1280]{1,0:T(8,128)(2,1)S(1)} %maximum_select_fusion.1), channel_id=1, source_target_pairs={{0,3},{1,128},{2,1},{3,130},{4,7},{5,132},{6,5},{7,134},{8,11},{9,... | collective-permute-start | bytes 491528 | tf_op jit(solution)/shard_map/ppermute | solution.py:269
  75.7 5.8 %copy-start.2 = (bf16[1,512,1280]{2,1,0:T(8,128)(2,1)S(1)}, bf16[1,512,1280]{2,1,0:T(8,128)(2,1)}, u32[]{:S(2)}) copy-start(bf16[1,512,1280]{2,1,0:T(8,128)(2,1)} %shard_map.166) | copy-start | bytes 3932164
  75.7 3.4 %collective-permute-start.5 = (bf16[1,512,1280]{2,1,0:T(8,128)(2,1)}, bf16[1,512,1280]{2,1,0:T(8,128)(2,1)S(1)}, u32[]{:S(2)}, u32[]{:S(2)}) collective-permute-start(bf16[1,512,1280]{2,1,0:T(8,128)(2,1)} %shard_map.166), channel_id=1, source_target_pairs={{0,1},{1,0},{2,3},{3,2},{4,5},{5,4},{6,7},{7,6},{8,9},{9,8},{10,11... | collective-permute-start | bytes 3932168 | tf_op jit(solution)/shard_map/ppermute | solution.py:23
  79.1 3.2 %copy-start.3 = (bf16[1,512,1280]{2,1,0:T(8,128)(2,1)}, bf16[1,512,1280]{2,1,0:T(8,128)(2,1)S(1)}, u32[]{:S(2)}) copy-start(bf16[1,512,1280]{2,1,0:T(8,128)(2,1)S(1)} %collective-permute-done.5) | copy-start | bytes 3932164
  81.5 0.8 copy-start.7
  96.1 3.2 %collective-permute-start.6 = (bf16[1,512,1280]{2,1,0:T(8,128)(2,1)}, bf16[1,512,1280]{2,1,0:T(8,128)(2,1)S(1)}, u32[]{:S(2)}, u32[]{:S(2)}) collective-permute-start(bf16[1,512,1280]{2,1,0:T(8,128)(2,1)} %bitcast.38), channel_id=1, source_target_pairs={{0,1},{1,0},{2,3},{3,2},{4,5},{5,4},{6,7},{7,6},{8,9},{9,8},{10,11... | collective-permute-start | bytes 3932168 | tf_op jit(solution)/shard_map/ppermute | solution.py:204

commit v9 on v7

--- a/solution.py
+++ b/solution.py
@@ -120,7 +120,7 @@
     values = x_ref[0].astype(jnp.float32)
     center = values - jnp.mean(values, axis=-1, keepdims=True)
     spread = jnp.mean(center * center, axis=-1, keepdims=True)
-    first = (center * lax.rsqrt(spread + 1e-06) * gain_ref[...]).astype(jnp.bfloat16)
+    first = (center * lax.rsqrt(spread + 1e-06) * gain_ref[...][None, :]).astype(jnp.bfloat16)
     for j, ref in enumerate((q_ref, k_ref, v_ref)):
         ref[...] = jnp.dot(first, w_ref[j], preferred_element_type=jnp.float32).astype(ref.dtype)
     keys = valid_ref[0] > 0
@@ -162,7 +162,7 @@
         grid=(batch,),
         in_specs=[
             pl.BlockSpec((1, length, model_width), lambda b: (b, 0, 0)),
-            pl.BlockSpec((1, model_width), lambda b: (0, 0)),
+            pl.BlockSpec((model_width,), lambda b: (0,)),
             pl.BlockSpec((3, model_width, width), lambda b: (0, 0, 0)),
             pl.BlockSpec((1, 1, length), lambda b: (b, 0, 0)),
             pl.BlockSpec((width, model_width), lambda b: (0, 0)),
@@ -177,7 +177,7 @@
         ),
     )(
         inputs,
-        gain_first.reshape(1, model_width),
+        gain_first,
         weight,
         key_valid.astype(jnp.int32).reshape(batch, 1, length),
         attend_out,

time: 104 us -> 103 us (level)
  local copies, waits for them, and re-layouts: 5.72 us -> 3.84 us
    reshape x2 -> x0, local copies, waits for them, and re-layouts: 1.88 us -> none  [attend(): gain_first.reshape(1, model_width)]
  transfers between devices with their start and end apart: 7 -> 7, of which waited for: 5 -> 6; matrix products, arithmetic and copies ran while one was open for 3% -> 2% of each run, Pallas kernels for 0% -> 0%
where the time goes in v9:
time: 103 us; the launch traced here: 101 us
  Pallas kernels  55.4 us (54%)
  other arithmetic  16.3 us (16%)
  starting transfers between devices  11.9 us (12%)
  waiting for transfers between devices  11.2 us (11%)
  local copies, waits for them, and re-layouts  3.84 us (4%)
  between operations  2.11 us (2%)
    pallas_call x2, Pallas kernels, attend(): pl.pallas_call(functools.partial(_attention_kernel, causal), out_shape=ja...  24.3 us
    pallas_call x2, Pallas kernels, feed_forward(): pl.pallas_call(functools.partial(_feed_forward_kernel, rows_per_step), ou...  23.9 us
    pallas_call x1, Pallas kernels, merge(): pl.pallas_call(_merge_kernel, out_shape=jax.ShapeDtypeStruct((images, hal...  7.28 us
    ppermute x2, starting transfers between devices, on_device(): sent.append(lax.ppermute(own_image, ('req', 'tensor'), perm))  6.95 us
    ppermute x2, waiting for transfers between devices, tensor_sum(): other = lax.ppermute(mine, 'tensor', [(0, 1), (1, 0)])  5.74 us
    reduce_sum x2, other arithmetic, normalize(): center = values - jnp.mean(values, axis=-1, keepdims=True)  4.31 us
    select_n x1, other arithmetic, on_device(): jnp.where(prompt_valid[None, :, None], decoded, jnp.zeros_like(decoded))  3.82 us
    ppermute x2, starting transfers between devices, tensor_sum(): other = lax.ppermute(mine, 'tensor', [(0, 1), (1, 0)])  3.74 us
  transfers between devices with their start and end apart: 7, of which 6 were waited for; matrix products, arithmetic and copies ran while one was open for 2% of the time, Pallas kernels for 0%

profile of v9, /device:TPU:1, one launch (start us, length us, event | category | flops | bytes accessed | tf_op | source)
XLA Modules:
  0.0 100.8 jit_solution(3973140999602912139)
XLA Ops:
  0.0 0.7 constant_dynamic-slice_fusion
  0.8 0.7 and_convert_fusion.valid_ref
  1.4 0.0 copy-start.5
  1.4 11.6 %shard_map.163 = bf16[2,256,1280]{2,1,0:T(8,128)(2,1)} custom-call(bf16[2,256,1280]{2,1,0:T(8,128)(2,1)} %x_ref.1, f32[1280]{0:T(1024)} %gain_ref.2, bf16[3,1280,640]{2,1,0:T(8,128)(2,1)} %bitcast.40, s32[2,1,256]{2,1,0:T(1,128)} %and_convert_fusion.valid_ref, bf16[640,1280]{1,0:T(8,128)(2,1)} %wo_ref.2), custom_call_target="tpu_custom_call" | custom-call | flops 4429185024 | bytes 9175040 | tf_op jit(solution)/shard_map/pallas_call | solution.py:159
  13.0 3.2 %collective-permute-start = (bf16[2,256,1280]{2,1,0:T(8,128)(2,1)}, bf16[2,256,1280]{2,1,0:T(8,128)(2,1)S(1)}, u32[]{:S(2)}, u32[]{:S(2)}) collective-permute-start(bf16[2,256,1280]{2,1,0:T(8,128)(2,1)} %shard_map.163), channel_id=1, source_target_pairs={{0,1},{1,0},{2,3},{3,2},{4,5},{5,4},{6,7},{7,6},{8,9},{9,8},{10,11... | collective-permute-start | bytes 3932168 | tf_op jit(solution)/shard_map/ppermute | solution.py:23
  16.3 2.9 %collective-permute-done = bf16[2,256,1280]{2,1,0:T(8,128)(2,1)S(1)} collective-permute-done((bf16[2,256,1280]{2,1,0:T(8,128)(2,1)}, bf16[2,256,1280]{2,1,0:T(8,128)(2,1)S(1)}, u32[]{:S(2)}, u32[]{:S(2)}) %collective-permute-start) | collective-permute-done | bytes 1310752 | tf_op jit(solution)/shard_map/ppermute | solution.py:23
  19.1 0.0 copy-done.5
  19.1 1.9 %fusion.7 = (f32[2,256]{1,0:T(2,128)S(1)}, f32[2,256,1280]{2,1,0:T(8,128)S(1)}) fusion(bf16[2,256,1280]{2,1,0:T(8,128)(2,1)S(1)} %collective-permute-done, bf16[2,256,1280]{2,1,0:T(8,128)(2,1)} %shard_map.163, bf16[2,256,1280]{2,1,0:T(8,128)(2,1)S(1)} %copy-done.5), kind=kLoop, calls=%fused_computation.47 | loop fusion | flops 3931648 | bytes 6555648 | tf_op jit(solution)/shard_map/reduce_sum | solution.py:16
  21.0 0.0 copy-start
  21.0 0.0 copy-start.6
  21.1 0.4 multiply_reduce_fusion.1
  21.5 0.3 copy-done.6
  21.8 1.5 %multiply_convert_fusion.1 = bf16[2,256,1280]{2,1,0:T(8,128)(2,1)} fusion(f32[2,256,1280]{2,1,0:T(8,128)S(1)} %get-tuple-element.6.res_ref, f32[1280]{0:T(1024)S(1)} %copy-done.6, f32[2,256]{1,0:T(2,128)S(1)} %add_rsqrt_fusion.1, f32[2,256]{1,0:T(2,128)S(1)} %broadcast_multiply_fusion.1), kind=kLoop, calls=%fused_computation.4 | loop fusion | flops 2621440 | bytes 3941376 | tf_op jit(solution)/shard_map/convert_element_type | solution.py:192
  23.2 0.0 copy-done
  23.2 0.0 copy-start.9
  23.2 0.0 copy-start.8
  23.2 11.9 %shard_map.164 = bf16[512,1280]{1,0:T(8,128)(2,1)} custom-call(bf16[512,1280]{1,0:T(8,128)(2,1)} %bitcast.37, bf16[1280,2560]{1,0:T(8,128)(2,1)} %w1_ref.2, bf16[2560,1280]{1,0:T(8,128)(2,1)} %w2_ref.2), custom_call_target="tpu_custom_call" | custom-call | flops 6710886400 | bytes 15728640 | tf_op jit(solution)/shard_map/pallas_call | solution.py:50
  35.2 0.4 collective-permute-start.1
  35.5 0.0 copy-done.9
  35.5 0.6 dynamic_slice.12
  38.1 0.0 copy-done.8
  38.1 0.1 constant_dynamic-slice_fusion.2
  38.2 0.1 add_select_fusion
  38.3 0.1 collective-permute-done.1.other_ref
  38.4 0.0 copy-start.4
  38.4 1.1 %copy-done.4 = bf16[2,256,1280]{2,1,0:T(8,128)(2,1)} copy-done((bf16[2,256,1280]{2,1,0:T(8,128)(2,1)}, bf16[2,256,1280]{2,1,0:T(8,128)(2,1)S(1)}, u32[]{:S(2)}) %copy-start.4) | copy-done | bytes 1310744
  39.5 7.3 %shard_map.165 = bf16[2,64,640]{2,1,0:T(8,128)(2,1)} custom-call(f32[2,256,1280]{2,1,0:T(8,128)} %copy-done, bf16[2,256,1280]{2,1,0:T(8,128)(2,1)} %bitcast.36, bf16[2,256,1280]{2,1,0:T(8,128)(2,1)} %copy-done.4, bf16[5120,640]{1,0:T(8,128)(2,1)} %w_ref.1), custom_call_target="tpu_custom_call" | custom-call | flops 922746880 | bytes 11796480 | tf_op jit(solution)/shard_map/pallas_call | solution.py:106
  46.8 0.0 copy-start.1
  46.8 1.0 %broadcast_select_fusion.2 = bf16[64,640]{1,0:T(8,128)(2,1)S(1)} fusion(pred[]{:T(512)S(6)} %eq.6, bf16[2,64,640]{2,1,0:T(8,128)(2,1)} %shard_map.165), kind=kLoop, calls=%fused_computation.16 | loop fusion | flops 40960 | bytes 245761 | tf_op jit(solution)/shard_map/jit(_where)/select_n | solution.py:248
  47.8 0.5 collective-permute-start.2
  48.2 0.9 slice_bitcast_fusion
  49.2 0.0 collective-permute-done.2
  49.2 5.3 %collective-permute-start.4 = (bf16[64,1280]{1,0:T(8,128)(2,1)S(1)}, bf16[64,1280]{1,0:T(8,128)(2,1)S(1)}, u32[]{:S(2)}, u32[]{:S(2)}) collective-permute-start(bf16[64,1280]{1,0:T(8,128)(2,1)S(1)} %maximum_select_fusion.1), channel_id=1, source_target_pairs={{0,2},{1,129},{2,0},{3,131},{4,6},{5,133},{6,4},{7,135},{8,10},{9,... | collective-permute-start | bytes 491528 | tf_op jit(solution)/shard_map/ppermute | solution.py:261
  54.5 1.7 %collective-permute-start.3 = (bf16[64,1280]{1,0:T(8,128)(2,1)S(1)}, bf16[64,1280]{1,0:T(8,128)(2,1)S(1)}, u32[]{:S(2)}, u32[]{:S(2)}) collective-permute-start(bf16[64,1280]{1,0:T(8,128)(2,1)S(1)} %maximum_select_fusion.1), channel_id=1, source_target_pairs={{0,3},{1,128},{2,1},{3,130},{4,7},{5,132},{6,5},{7,134},{8,11},{9,... | collective-permute-start | bytes 491528 | tf_op jit(solution)/shard_map/ppermute | solution.py:261
  56.2 0.1 compare_and_fusion
  56.3 0.1 and.78
  56.4 0.6 fusion.8
  57.0 0.5 collective-permute-done.4
  57.5 1.9 %collective-permute-done.3 = bf16[64,1280]{1,0:T(8,128)(2,1)S(1)} collective-permute-done((bf16[64,1280]{1,0:T(8,128)(2,1)S(1)}, bf16[64,1280]{1,0:T(8,128)(2,1)S(1)}, u32[]{:S(2)}, u32[]{:S(2)}) %collective-permute-start.3) | collective-permute-done | bytes 163872 | tf_op jit(solution)/shard_map/ppermute | solution.py:261
  59.5 0.1 maximum_select_fusion
  59.6 0.0 copy-done.1
  59.6 1.1 %maximum_bitcast_fusion.x_ref = bf16[1,512,1280]{2,1,0:T(8,128)(2,1)} fusion(bf16[384,1280]{1,0:T(8,128)(2,1)S(1)} %bitcast.30, bf16[128,1280]{1,0:T(8,128)(2,1)S(1)} %maximum_select_fusion), kind=kLoop, calls=%fused_computation.9 | loop fusion | flops 2621440 | bytes 2621440 | tf_op jit(solution)/shard_map/broadcast_in_dim | solution.py:281
  60.7 12.7 %shard_map.166 = bf16[1,512,1280]{2,1,0:T(8,128)(2,1)} custom-call(bf16[1,512,1280]{2,1,0:T(8,128)(2,1)} %maximum_bitcast_fusion.x_ref, f32[1280]{0:T(1024)} %gain_ref.3, bf16[3,1280,640]{2,1,0:T(8,128)(2,1)} %bitcast.41, s32[1,1,512]{2,1,0:T(1,128)} %bitcast.39, bf16[640,1280]{1,0:T(8,128)(2,1)} %wo_ref.3), custom_call_target="tpu_custom_call" | custom-call | flops 5502926848 | bytes 9175040 | tf_op jit(solution)/shard_map/pallas_call | solution.py:159
  73.4 0.0 copy-start.2
  73.4 0.5 collective-permute-start.5
  73.9 2.9 %collective-permute-done.5 = bf16[1,512,1280]{2,1,0:T(8,128)(2,1)S(1)} collective-permute-done((bf16[1,512,1280]{2,1,0:T(8,128)(2,1)}, bf16[1,512,1280]{2,1,0:T(8,128)(2,1)S(1)}, u32[]{:S(2)}, u32[]{:S(2)}) %collective-permute-start.5) | collective-permute-done | bytes 1310752 | tf_op jit(solution)/shard_map/ppermute | solution.py:23
  76.8 0.0 copy-start.3
  76.8 2.4 %fusion.6 = f32[512]{0:T(512)S(1)} fusion(bf16[1,512,1280]{2,1,0:T(8,128)(2,1)S(1)} %collective-permute-done.5, bf16[1,512,1280]{2,1,0:T(8,128)(2,1)} %shard_map.166, bf16[1,384,1280]{2,1,0:T(8,128)(2,1)S(1)} %copy-done.1, bf16[1,128,1280]{2,1,0:T(8,128)(2,1)S(1)} %bitcast.31), kind=kLoop, calls=%fused_computation.46 | loop fusion | flops 5897728 | bytes 3934208 | tf_op jit(solution)/shard_map/reduce_sum | solution.py:16
  79.2 0.0 copy-start.7
  79.2 0.0 copy-done.2
  79.2 0.8 multiply_reduce_fusion
  80.0 0.0 copy-done.3
  80.0 0.0 copy-done.7
  80.0 1.8 %fusion.x_ref = bf16[512,1280]{1,0:T(8,128)(2,1)} fusion(f32[1280]{0:T(1024)S(1)} %copy-done.7, f32[512]{0:T(512)S(1)} %add_rsqrt_fusion, f32[512]{0:T(512)S(1)} %broadcast_multiply_fusion, bf16[1,512,1280]{2,1,0:T(8,128)(2,1)S(1)} %collective-permute-done.5, bf16[1,512,1280]{2,1,0:T(8,128)(2,1)S(1)} %copy-done.2, bf16[1,384,1280]{2,1,0:T(8,128)(2,1)S(1)} %copy-done.1, ...), kind=kLoop, calls=%fused_computation.7 | loop fusion | flops 7864320 | bytes 5252096 | tf_op jit(solution)/shard_map/reshape | solution.py:194
  81.8 11.9 %shard_map.167 = bf16[512,1280]{1,0:T(8,128)(2,1)} custom-call(bf16[512,1280]{1,0:T(8,128)(2,1)} %fusion.x_ref, bf16[1280,2560]{1,0:T(8,128)(2,1)} %w1_ref.3, bf16[2560,1280]{1,0:T(8,128)(2,1)} %w2_ref.3), custom_call_target="tpu_custom_call" | custom-call | flops 6710886400 | bytes 15728640 | tf_op jit(solution)/shard_map/pallas_call | solution.py:50
  93.8 0.4 collective-permute-start.6
  94.1 2.9 %collective-permute-done.6 = bf16[1,512,1280]{2,1,0:T(8,128)(2,1)S(1)} collective-permute-done((bf16[1,512,1280]{2,1,0:T(8,128)(2,1)}, bf16[1,512,1280]{2,1,0:T(8,128)(2,1)S(1)}, u32[]{:S(2)}, u32[]{:S(2)}) %collective-permute-start.6) | collective-permute-done | bytes 1310752 | tf_op jit(solution)/shard_map/ppermute | solution.py:196
  97.0 3.8 %fusion.1 = bf16[1,512,1280]{2,1,0:T(8,128)(2,1)} fusion(bf16[1,512,1280]{2,1,0:T(8,128)(2,1)S(1)} %collective-permute-done.6, pred[512]{0:T(512)(128)(4,1)S(1)} %get-tuple-element.17, bf16[512,1280]{1,0:T(8,128)(2,1)} %shard_map.167, bf16[1,512,1280]{2,1,0:T(8,128)(2,1)} %copy-done.3, bf16[1,512,1280]{2,1,0:T(8,128)(2,1)S(1)} %copy-done.2, ...), kind=kLoop, calls=%fused_computation.8 | loop fusion | flops 9175040 | bytes 7864832 | tf_op jit(solution)/shard_map/jit(_where)/select_n | solution.py:297
  (10 shorter events, 0.1 us)
Async XLA Ops:
  1.4 17.7 %copy-start.5 = (bf16[2,256,1280]{2,1,0:T(8,128)(2,1)S(1)}, bf16[2,256,1280]{2,1,0:T(8,128)(2,1)}, u32[]{:S(2)}) copy-start(bf16[2,256,1280]{2,1,0:T(8,128)(2,1)} %x_ref.1) | copy-start | bytes 3932164
  13.0 6.1 %collective-permute-start = (bf16[2,256,1280]{2,1,0:T(8,128)(2,1)}, bf16[2,256,1280]{2,1,0:T(8,128)(2,1)S(1)}, u32[]{:S(2)}, u32[]{:S(2)}) collective-permute-start(bf16[2,256,1280]{2,1,0:T(8,128)(2,1)} %shard_map.163), channel_id=1, source_target_pairs={{0,1},{1,0},{2,3},{3,2},{4,5},{5,4},{6,7},{7,6},{8,9},{9,8},{10,11... | collective-permute-start | bytes 3932168 | tf_op jit(solution)/shard_map/ppermute | solution.py:23
  21.0 2.2 %copy-start = (f32[2,256,1280]{2,1,0:T(8,128)}, f32[2,256,1280]{2,1,0:T(8,128)S(1)}, u32[]{:S(2)}) copy-start(f32[2,256,1280]{2,1,0:T(8,128)S(1)} %get-tuple-element.6.res_ref) | copy-start | bytes 7864324
  21.0 0.7 copy-start.6
  23.2 12.3 %copy-start.9 = (s32[256]{0:T(256)S(1)}, s32[256]{0:T(256)}, u32[]{:S(2)}) copy-start(s32[256]{0:T(256)} %param.19) | copy-start | bytes 3076
  23.2 14.9 %copy-start.8 = (s32[256,2]{0,1:T(2,128)S(1)}, s32[256,2]{0,1:T(2,128)}, u32[]{:S(2)}) copy-start(s32[256,2]{0,1:T(2,128)} %param.18) | copy-start | bytes 6148
  35.2 3.2 %collective-permute-start.1 = (bf16[2,256,1280]{2,1,0:T(8,128)(2,1)}, bf16[2,256,1280]{2,1,0:T(8,128)(2,1)S(1)}, u32[]{:S(2)}, u32[]{:S(2)}) collective-permute-start(bf16[2,256,1280]{2,1,0:T(8,128)(2,1)} %bitcast.35), channel_id=1, source_target_pairs={{0,1},{1,0},{2,3},{3,2},{4,5},{5,4},{6,7},{7,6},{8,9},{9,8},{10,11... | collective-permute-start | bytes 3932168 | tf_op jit(solution)/shard_map/ppermute | solution.py:196
  38.4 1.1 %copy-start.4 = (bf16[2,256,1280]{2,1,0:T(8,128)(2,1)}, bf16[2,256,1280]{2,1,0:T(8,128)(2,1)S(1)}, u32[]{:S(2)}) copy-start(bf16[2,256,1280]{2,1,0:T(8,128)(2,1)S(1)} %collective-permute-done.1.other_ref) | copy-start | bytes 3932164
  46.8 12.8 %copy-start.1 = (bf16[1,384,1280]{2,1,0:T(8,128)(2,1)S(1)}, bf16[1,384,1280]{2,1,0:T(8,128)(2,1)}, u32[]{:S(2)}) copy-start(bf16[1,384,1280]{2,1,0:T(8,128)(2,1)} %param.20) | copy-start | bytes 2949124
  47.8 1.4 %collective-permute-start.2 = (bf16[64,640]{1,0:T(8,128)(2,1)S(1)}, bf16[64,640]{1,0:T(8,128)(2,1)S(1)}, u32[]{:S(2)}, u32[]{:S(2)}) collective-permute-start(bf16[64,640]{1,0:T(8,128)(2,1)S(1)} %broadcast_select_fusion.2), channel_id=1, source_target_pairs={{0,1},{1,0},{2,3},{3,2},{4,5},{5,4},{6,7},{7,6},{8,9},{9,8},{10,11... | collective-permute-start | bytes 245768 | tf_op jit(solution)/shard_map/ppermute | solution.py:248
  49.2 8.3 %collective-permute-start.4 = (bf16[64,1280]{1,0:T(8,128)(2,1)S(1)}, bf16[64,1280]{1,0:T(8,128)(2,1)S(1)}, u32[]{:S(2)}, u32[]{:S(2)}) collective-permute-start(bf16[64,1280]{1,0:T(8,128)(2,1)S(1)} %maximum_select_fusion.1), channel_id=1, source_target_pairs={{0,2},{1,129},{2,0},{3,131},{4,6},{5,133},{6,4},{7,135},{8,10},{9,... | collective-permute-start | bytes 491528 | tf_op jit(solution)/shard_map/ppermute | solution.py:261
  54.5 5.0 %collective-permute-start.3 = (bf16[64,1280]{1,0:T(8,128)(2,1)S(1)}, bf16[64,1280]{1,0:T(8,128)(2,1)S(1)}, u32[]{:S(2)}, u32[]{:S(2)}) collective-permute-start(bf16[64,1280]{1,0:T(8,128)(2,1)S(1)} %maximum_select_fusion.1), channel_id=1, source_target_pairs={{0,3},{1,128},{2,1},{3,130},{4,7},{5,132},{6,5},{7,134},{8,11},{9,... | collective-permute-start | bytes 491528 | tf_op jit(solution)/shard_map/ppermute | solution.py:261
  73.4 5.8 %copy-start.2 = (bf16[1,512,1280]{2,1,0:T(8,128)(2,1)S(1)}, bf16[1,512,1280]{2,1,0:T(8,128)(2,1)}, u32[]{:S(2)}) copy-start(bf16[1,512,1280]{2,1,0:T(8,128)(2,1)} %shard_map.166) | copy-start | bytes 3932164
  73.4 3.4 %collective-permute-start.5 = (bf16[1,512,1280]{2,1,0:T(8,128)(2,1)}, bf16[1,512,1280]{2,1,0:T(8,128)(2,1)S(1)}, u32[]{:S(2)}, u32[]{:S(2)}) collective-permute-start(bf16[1,512,1280]{2,1,0:T(8,128)(2,1)} %shard_map.166), channel_id=1, source_target_pairs={{0,1},{1,0},{2,3},{3,2},{4,5},{5,4},{6,7},{7,6},{8,9},{9,8},{10,11... | collective-permute-start | bytes 3932168 | tf_op jit(solution)/shard_map/ppermute | solution.py:23
  76.8 3.2 %copy-start.3 = (bf16[1,512,1280]{2,1,0:T(8,128)(2,1)}, bf16[1,512,1280]{2,1,0:T(8,128)(2,1)S(1)}, u32[]{:S(2)}) copy-start(bf16[1,512,1280]{2,1,0:T(8,128)(2,1)S(1)} %collective-permute-done.5) | copy-start | bytes 3932164
  79.2 0.8 copy-start.7
  93.8 3.2 %collective-permute-start.6 = (bf16[1,512,1280]{2,1,0:T(8,128)(2,1)}, bf16[1,512,1280]{2,1,0:T(8,128)(2,1)S(1)}, u32[]{:S(2)}, u32[]{:S(2)}) collective-permute-start(bf16[1,512,1280]{2,1,0:T(8,128)(2,1)} %bitcast.38), channel_id=1, source_target_pairs={{0,1},{1,0},{2,3},{3,2},{4,5},{5,4},{6,7},{7,6},{8,9},{9,8},{10,11... | collective-permute-start | bytes 3932168 | tf_op jit(solution)/shard_map/ppermute | solution.py:196

commit v10 on v9

--- a/solution.py
+++ b/solution.py
@@ -44,7 +44,7 @@
         o_ref[...] = acc_ref[...].astype(o_ref.dtype)
 
 
-def feed_forward(x, expand, contract, hidden_step=512, rows_per_step=512):
+def feed_forward(x, expand, contract, hidden_step=640, rows_per_step=512):
     length, width = x.shape
     hidden = expand.shape[1]
     return pl.pallas_call(

time: 103 us -> 105 us (1.019)
  Pallas kernels: 55.4 us -> 57.8 us
    pallas_call x2, Pallas kernels: 23.9 us -> 26.2 us  [feed_forward(): pl.pallas_call(functools.partial(_feed_forward_kernel, rows_per_step), ou...]
where the time goes in v10:
time: 105 us; the launch traced here: 103 us
  Pallas kernels  57.8 us (55%)
  other arithmetic  16.3 us (16%)
  starting transfers between devices  11.9 us (11%)
  waiting for transfers between devices  11.2 us (11%)
  local copies, waits for them, and re-layouts  3.84 us (4%)
  between operations  2.11 us (2%)
    pallas_call x2, Pallas kernels, feed_forward(): pl.pallas_call(functools.partial(_feed_forward_kernel, rows_per_step), ou...  26.2 us
    pallas_call x2, Pallas kernels, attend(): pl.pallas_call(functools.partial(_attention_kernel, causal), out_shape=ja...  24.3 us
    pallas_call x1, Pallas kernels, merge(): pl.pallas_call(_merge_kernel, out_shape=jax.ShapeDtypeStruct((images, hal...  7.27 us
    ppermute x2, starting transfers between devices, on_device(): sent.append(lax.ppermute(own_image, ('req', 'tensor'), perm))  6.95 us
    ppermute x2, waiting for transfers between devices, tensor_sum(): other = lax.ppermute(mine, 'tensor', [(0, 1), (1, 0)])  5.74 us
    reduce_sum x2, other arithmetic, normalize(): center = values - jnp.mean(values, axis=-1, keepdims=True)  4.31 us
    select_n x1, other arithmetic, on_device(): jnp.where(prompt_valid[None, :, None], decoded, jnp.zeros_like(decoded))  3.82 us
    ppermute x2, starting transfers between devices, tensor_sum(): other = lax.ppermute(mine, 'tensor', [(0, 1), (1, 0)])  3.74 us
  transfers between devices with their start and end apart: 7, of which 6 were waited for; matrix products, arithmetic and copies ran while one was open for 2% of the time, Pallas kernels for 0%

profile of v10, /device:TPU:1, one launch (start us, length us, event | category | flops | bytes accessed | tf_op | source)
XLA Modules:
  0.0 103.2 jit_solution(13371222021455592496)
XLA Ops:
  0.0 0.7 constant_dynamic-slice_fusion
  0.8 0.7 and_convert_fusion.valid_ref
  1.4 0.0 copy-start.5
  1.4 11.6 %shard_map.163 = bf16[2,256,1280]{2,1,0:T(8,128)(2,1)} custom-call(bf16[2,256,1280]{2,1,0:T(8,128)(2,1)} %x_ref.1, f32[1280]{0:T(1024)} %gain_ref.2, bf16[3,1280,640]{2,1,0:T(8,128)(2,1)} %bitcast.40, s32[2,1,256]{2,1,0:T(1,128)} %and_convert_fusion.valid_ref, bf16[640,1280]{1,0:T(8,128)(2,1)} %wo_ref.2), custom_call_target="tpu_custom_call" | custom-call | flops 4429185024 | bytes 9175040 | tf_op jit(solution)/shard_map/pallas_call | solution.py:159
  13.0 3.2 %collective-permute-start = (bf16[2,256,1280]{2,1,0:T(8,128)(2,1)}, bf16[2,256,1280]{2,1,0:T(8,128)(2,1)S(1)}, u32[]{:S(2)}, u32[]{:S(2)}) collective-permute-start(bf16[2,256,1280]{2,1,0:T(8,128)(2,1)} %shard_map.163), channel_id=1, source_target_pairs={{0,1},{1,0},{2,3},{3,2},{4,5},{5,4},{6,7},{7,6},{8,9},{9,8},{10,11... | collective-permute-start | bytes 3932168 | tf_op jit(solution)/shard_map/ppermute | solution.py:23
  16.3 2.9 %collective-permute-done = bf16[2,256,1280]{2,1,0:T(8,128)(2,1)S(1)} collective-permute-done((bf16[2,256,1280]{2,1,0:T(8,128)(2,1)}, bf16[2,256,1280]{2,1,0:T(8,128)(2,1)S(1)}, u32[]{:S(2)}, u32[]{:S(2)}) %collective-permute-start) | collective-permute-done | bytes 1310752 | tf_op jit(solution)/shard_map/ppermute | solution.py:23
  19.1 0.0 copy-done.5
  19.1 1.9 %fusion.7 = (f32[2,256]{1,0:T(2,128)S(1)}, f32[2,256,1280]{2,1,0:T(8,128)S(1)}) fusion(bf16[2,256,1280]{2,1,0:T(8,128)(2,1)S(1)} %collective-permute-done, bf16[2,256,1280]{2,1,0:T(8,128)(2,1)} %shard_map.163, bf16[2,256,1280]{2,1,0:T(8,128)(2,1)S(1)} %copy-done.5), kind=kLoop, calls=%fused_computation.47 | loop fusion | flops 3931648 | bytes 6555648 | tf_op jit(solution)/shard_map/reduce_sum | solution.py:16
  21.0 0.0 copy-start
  21.0 0.0 copy-start.6
  21.1 0.4 multiply_reduce_fusion.1
  21.5 0.3 copy-done.6
  21.8 1.5 %multiply_convert_fusion.1 = bf16[2,256,1280]{2,1,0:T(8,128)(2,1)} fusion(f32[2,256,1280]{2,1,0:T(8,128)S(1)} %get-tuple-element.6.res_ref, f32[1280]{0:T(1024)S(1)} %copy-done.6, f32[2,256]{1,0:T(2,128)S(1)} %add_rsqrt_fusion.1, f32[2,256]{1,0:T(2,128)S(1)} %broadcast_multiply_fusion.1), kind=kLoop, calls=%fused_computation.4 | loop fusion | flops 2621440 | bytes 3941376 | tf_op jit(solution)/shard_map/convert_element_type | solution.py:192
  23.2 0.0 copy-done
  23.2 0.0 copy-start.9
  23.2 0.0 copy-start.8
  23.2 13.1 %shard_map.164 = bf16[512,1280]{1,0:T(8,128)(2,1)} custom-call(bf16[512,1280]{1,0:T(8,128)(2,1)} %bitcast.37, bf16[1280,2560]{1,0:T(8,128)(2,1)} %w1_ref.2, bf16[2560,1280]{1,0:T(8,128)(2,1)} %w2_ref.2), custom_call_target="tpu_custom_call" | custom-call | flops 6710886400 | bytes 15728640 | tf_op jit(solution)/shard_map/pallas_call | solution.py:50
  36.4 0.4 collective-permute-start.1
  36.7 0.0 copy-done.9
  36.7 0.6 dynamic_slice.12
  39.3 0.0 copy-done.8
  39.3 0.1 constant_dynamic-slice_fusion.2
  39.4 0.1 add_select_fusion
  39.5 0.1 collective-permute-done.1.other_ref
  39.6 0.0 copy-start.4
  39.6 1.1 %copy-done.4 = bf16[2,256,1280]{2,1,0:T(8,128)(2,1)} copy-done((bf16[2,256,1280]{2,1,0:T(8,128)(2,1)}, bf16[2,256,1280]{2,1,0:T(8,128)(2,1)S(1)}, u32[]{:S(2)}) %copy-start.4) | copy-done | bytes 1310744
  40.7 7.3 %shard_map.165 = bf16[2,64,640]{2,1,0:T(8,128)(2,1)} custom-call(f32[2,256,1280]{2,1,0:T(8,128)} %copy-done, bf16[2,256,1280]{2,1,0:T(8,128)(2,1)} %bitcast.36, bf16[2,256,1280]{2,1,0:T(8,128)(2,1)} %copy-done.4, bf16[5120,640]{1,0:T(8,128)(2,1)} %w_ref.1), custom_call_target="tpu_custom_call" | custom-call | flops 922746880 | bytes 11796480 | tf_op jit(solution)/shard_map/pallas_call | solution.py:106
  47.9 0.0 copy-start.1
  47.9 1.0 broadcast_select_fusion.2
  49.0 0.5 collective-permute-start.2
  49.4 0.9 slice_bitcast_fusion
  50.4 0.0 collective-permute-done.2
  50.4 5.3 %collective-permute-start.4 = (bf16[64,1280]{1,0:T(8,128)(2,1)S(1)}, bf16[64,1280]{1,0:T(8,128)(2,1)S(1)}, u32[]{:S(2)}, u32[]{:S(2)}) collective-permute-start(bf16[64,1280]{1,0:T(8,128)(2,1)S(1)} %maximum_select_fusion.1), channel_id=1, source_target_pairs={{0,2},{1,129},{2,0},{3,131},{4,6},{5,133},{6,4},{7,135},{8,10},{9,... | collective-permute-start | bytes 491528 | tf_op jit(solution)/shard_map/ppermute | solution.py:261
  55.7 1.7 %collective-permute-start.3 = (bf16[64,1280]{1,0:T(8,128)(2,1)S(1)}, bf16[64,1280]{1,0:T(8,128)(2,1)S(1)}, u32[]{:S(2)}, u32[]{:S(2)}) collective-permute-start(bf16[64,1280]{1,0:T(8,128)(2,1)S(1)} %maximum_select_fusion.1), channel_id=1, source_target_pairs={{0,3},{1,128},{2,1},{3,130},{4,7},{5,132},{6,5},{7,134},{8,11},{9,... | collective-permute-start | bytes 491528 | tf_op jit(solution)/shard_map/ppermute | solution.py:261
  57.4 0.1 compare_and_fusion
  57.5 0.1 and.78
  57.5 0.6 fusion.8
  58.1 0.6 collective-permute-done.4
  58.7 1.9 %collective-permute-done.3 = bf16[64,1280]{1,0:T(8,128)(2,1)S(1)} collective-permute-done((bf16[64,1280]{1,0:T(8,128)(2,1)S(1)}, bf16[64,1280]{1,0:T(8,128)(2,1)S(1)}, u32[]{:S(2)}, u32[]{:S(2)}) %collective-permute-start.3) | collective-permute-done | bytes 163872 | tf_op jit(solution)/shard_map/ppermute | solution.py:261
  60.7 0.1 maximum_select_fusion
  60.7 0.0 copy-done.1
  60.8 1.1 %maximum_bitcast_fusion.x_ref = bf16[1,512,1280]{2,1,0:T(8,128)(2,1)} fusion(bf16[384,1280]{1,0:T(8,128)(2,1)S(1)} %bitcast.30, bf16[128,1280]{1,0:T(8,128)(2,1)S(1)} %maximum_select_fusion), kind=kLoop, calls=%fused_computation.9 | loop fusion | flops 2621440 | bytes 2621440 | tf_op jit(solution)/shard_map/broadcast_in_dim | solution.py:281
  61.9 12.7 %shard_map.166 = bf16[1,512,1280]{2,1,0:T(8,128)(2,1)} custom-call(bf16[1,512,1280]{2,1,0:T(8,128)(2,1)} %maximum_bitcast_fusion.x_ref, f32[1280]{0:T(1024)} %gain_ref.3, bf16[3,1280,640]{2,1,0:T(8,128)(2,1)} %bitcast.41, s32[1,1,512]{2,1,0:T(1,128)} %bitcast.39, bf16[640,1280]{1,0:T(8,128)(2,1)} %wo_ref.3), custom_call_target="tpu_custom_call" | custom-call | flops 5502926848 | bytes 9175040 | tf_op jit(solution)/shard_map/pallas_call | solution.py:159
  74.6 0.0 copy-start.2
  74.6 0.5 collective-permute-start.5
  75.1 2.9 %collective-permute-done.5 = bf16[1,512,1280]{2,1,0:T(8,128)(2,1)S(1)} collective-permute-done((bf16[1,512,1280]{2,1,0:T(8,128)(2,1)}, bf16[1,512,1280]{2,1,0:T(8,128)(2,1)S(1)}, u32[]{:S(2)}, u32[]{:S(2)}) %collective-permute-start.5) | collective-permute-done | bytes 1310752 | tf_op jit(solution)/shard_map/ppermute | solution.py:23
  77.9 0.0 copy-start.3
  77.9 2.4 %fusion.6 = f32[512]{0:T(512)S(1)} fusion(bf16[1,512,1280]{2,1,0:T(8,128)(2,1)S(1)} %collective-permute-done.5, bf16[1,512,1280]{2,1,0:T(8,128)(2,1)} %shard_map.166, bf16[1,384,1280]{2,1,0:T(8,128)(2,1)S(1)} %copy-done.1, bf16[1,128,1280]{2,1,0:T(8,128)(2,1)S(1)} %bitcast.31), kind=kLoop, calls=%fused_computation.46 | loop fusion | flops 5897728 | bytes 3934208 | tf_op jit(solution)/shard_map/reduce_sum | solution.py:16
  80.3 0.0 copy-start.7
  80.4 0.0 copy-done.2
  80.4 0.8 multiply_reduce_fusion
  81.2 0.0 copy-done.3
  81.2 0.0 copy-done.7
  81.2 1.8 %fusion.x_ref = bf16[512,1280]{1,0:T(8,128)(2,1)} fusion(f32[1280]{0:T(1024)S(1)} %copy-done.7, f32[512]{0:T(512)S(1)} %add_rsqrt_fusion, f32[512]{0:T(512)S(1)} %broadcast_multiply_fusion, bf16[1,512,1280]{2,1,0:T(8,128)(2,1)S(1)} %collective-permute-done.5, bf16[1,512,1280]{2,1,0:T(8,128)(2,1)S(1)} %copy-done.2, bf16[1,384,1280]{2,1,0:T(8,128)(2,1)S(1)} %copy-done.1, ...), kind=kLoop, calls=%fused_computation.7 | loop fusion | flops 7864320 | bytes 5252096 | tf_op jit(solution)/shard_map/reshape | solution.py:194
  83.0 13.1 %shard_map.167 = bf16[512,1280]{1,0:T(8,128)(2,1)} custom-call(bf16[512,1280]{1,0:T(8,128)(2,1)} %fusion.x_ref, bf16[1280,2560]{1,0:T(8,128)(2,1)} %w1_ref.3, bf16[2560,1280]{1,0:T(8,128)(2,1)} %w2_ref.3), custom_call_target="tpu_custom_call" | custom-call | flops 6710886400 | bytes 15728640 | tf_op jit(solution)/shard_map/pallas_call | solution.py:50
  96.1 0.4 collective-permute-start.6
  96.5 2.9 %collective-permute-done.6 = bf16[1,512,1280]{2,1,0:T(8,128)(2,1)S(1)} collective-permute-done((bf16[1,512,1280]{2,1,0:T(8,128)(2,1)}, bf16[1,512,1280]{2,1,0:T(8,128)(2,1)S(1)}, u32[]{:S(2)}, u32[]{:S(2)}) %collective-permute-start.6) | collective-permute-done | bytes 1310752 | tf_op jit(solution)/shard_map/ppermute | solution.py:196
  99.4 3.8 %fusion.1 = bf16[1,512,1280]{2,1,0:T(8,128)(2,1)} fusion(bf16[1,512,1280]{2,1,0:T(8,128)(2,1)S(1)} %collective-permute-done.6, pred[512]{0:T(512)(128)(4,1)S(1)} %get-tuple-element.17, bf16[512,1280]{1,0:T(8,128)(2,1)} %shard_map.167, bf16[1,512,1280]{2,1,0:T(8,128)(2,1)} %copy-done.3, bf16[1,512,1280]{2,1,0:T(8,128)(2,1)S(1)} %copy-done.2, ...), kind=kLoop, calls=%fused_computation.8 | loop fusion | flops 9175040 | bytes 7864832 | tf_op jit(solution)/shard_map/jit(_where)/select_n | solution.py:297
  (10 shorter events, 0.1 us)
Async XLA Ops:
  1.4 17.7 %copy-start.5 = (bf16[2,256,1280]{2,1,0:T(8,128)(2,1)S(1)}, bf16[2,256,1280]{2,1,0:T(8,128)(2,1)}, u32[]{:S(2)}) copy-start(bf16[2,256,1280]{2,1,0:T(8,128)(2,1)} %x_ref.1) | copy-start | bytes 3932164
  13.0 6.1 %collective-permute-start = (bf16[2,256,1280]{2,1,0:T(8,128)(2,1)}, bf16[2,256,1280]{2,1,0:T(8,128)(2,1)S(1)}, u32[]{:S(2)}, u32[]{:S(2)}) collective-permute-start(bf16[2,256,1280]{2,1,0:T(8,128)(2,1)} %shard_map.163), channel_id=1, source_target_pairs={{0,1},{1,0},{2,3},{3,2},{4,5},{5,4},{6,7},{7,6},{8,9},{9,8},{10,11... | collective-permute-start | bytes 3932168 | tf_op jit(solution)/shard_map/ppermute | solution.py:23
  21.0 2.2 %copy-start = (f32[2,256,1280]{2,1,0:T(8,128)}, f32[2,256,1280]{2,1,0:T(8,128)S(1)}, u32[]{:S(2)}) copy-start(f32[2,256,1280]{2,1,0:T(8,128)S(1)} %get-tuple-element.6.res_ref) | copy-start | bytes 7864324
  21.0 0.7 copy-start.6
  23.2 13.5 %copy-start.9 = (s32[256]{0:T(256)S(1)}, s32[256]{0:T(256)}, u32[]{:S(2)}) copy-start(s32[256]{0:T(256)} %param.19) | copy-start | bytes 3076
  23.2 16.1 %copy-start.8 = (s32[256,2]{0,1:T(2,128)S(1)}, s32[256,2]{0,1:T(2,128)}, u32[]{:S(2)}) copy-start(s32[256,2]{0,1:T(2,128)} %param.18) | copy-start | bytes 6148
  36.4 3.3 %collective-permute-start.1 = (bf16[2,256,1280]{2,1,0:T(8,128)(2,1)}, bf16[2,256,1280]{2,1,0:T(8,128)(2,1)S(1)}, u32[]{:S(2)}, u32[]{:S(2)}) collective-permute-start(bf16[2,256,1280]{2,1,0:T(8,128)(2,1)} %bitcast.35), channel_id=1, source_target_pairs={{0,1},{1,0},{2,3},{3,2},{4,5},{5,4},{6,7},{7,6},{8,9},{9,8},{10,11... | collective-permute-start | bytes 3932168 | tf_op jit(solution)/shard_map/ppermute | solution.py:196
  39.6 1.1 %copy-start.4 = (bf16[2,256,1280]{2,1,0:T(8,128)(2,1)}, bf16[2,256,1280]{2,1,0:T(8,128)(2,1)S(1)}, u32[]{:S(2)}) copy-start(bf16[2,256,1280]{2,1,0:T(8,128)(2,1)S(1)} %collective-permute-done.1.other_ref) | copy-start | bytes 3932164
  47.9 12.8 %copy-start.1 = (bf16[1,384,1280]{2,1,0:T(8,128)(2,1)S(1)}, bf16[1,384,1280]{2,1,0:T(8,128)(2,1)}, u32[]{:S(2)}) copy-start(bf16[1,384,1280]{2,1,0:T(8,128)(2,1)} %param.20) | copy-start | bytes 2949124
  49.0 1.4 %collective-permute-start.2 = (bf16[64,640]{1,0:T(8,128)(2,1)S(1)}, bf16[64,640]{1,0:T(8,128)(2,1)S(1)}, u32[]{:S(2)}, u32[]{:S(2)}) collective-permute-start(bf16[64,640]{1,0:T(8,128)(2,1)S(1)} %broadcast_select_fusion.2), channel_id=1, source_target_pairs={{0,1},{1,0},{2,3},{3,2},{4,5},{5,4},{6,7},{7,6},{8,9},{9,8},{10,11... | collective-permute-start | bytes 245768 | tf_op jit(solution)/shard_map/ppermute | solution.py:248
  50.4 8.3 %collective-permute-start.4 = (bf16[64,1280]{1,0:T(8,128)(2,1)S(1)}, bf16[64,1280]{1,0:T(8,128)(2,1)S(1)}, u32[]{:S(2)}, u32[]{:S(2)}) collective-permute-start(bf16[64,1280]{1,0:T(8,128)(2,1)S(1)} %maximum_select_fusion.1), channel_id=1, source_target_pairs={{0,2},{1,129},{2,0},{3,131},{4,6},{5,133},{6,4},{7,135},{8,10},{9,... | collective-permute-start | bytes 491528 | tf_op jit(solution)/shard_map/ppermute | solution.py:261
  55.7 5.0 %collective-permute-start.3 = (bf16[64,1280]{1,0:T(8,128)(2,1)S(1)}, bf16[64,1280]{1,0:T(8,128)(2,1)S(1)}, u32[]{:S(2)}, u32[]{:S(2)}) collective-permute-start(bf16[64,1280]{1,0:T(8,128)(2,1)S(1)} %maximum_select_fusion.1), channel_id=1, source_target_pairs={{0,3},{1,128},{2,1},{3,130},{4,7},{5,132},{6,5},{7,134},{8,11},{9,... | collective-permute-start | bytes 491528 | tf_op jit(solution)/shard_map/ppermute | solution.py:261
  74.6 5.8 %copy-start.2 = (bf16[1,512,1280]{2,1,0:T(8,128)(2,1)S(1)}, bf16[1,512,1280]{2,1,0:T(8,128)(2,1)}, u32[]{:S(2)}) copy-start(bf16[1,512,1280]{2,1,0:T(8,128)(2,1)} %shard_map.166) | copy-start | bytes 3932164
  74.6 3.4 %collective-permute-start.5 = (bf16[1,512,1280]{2,1,0:T(8,128)(2,1)}, bf16[1,512,1280]{2,1,0:T(8,128)(2,1)S(1)}, u32[]{:S(2)}, u32[]{:S(2)}) collective-permute-start(bf16[1,512,1280]{2,1,0:T(8,128)(2,1)} %shard_map.166), channel_id=1, source_target_pairs={{0,1},{1,0},{2,3},{3,2},{4,5},{5,4},{6,7},{7,6},{8,9},{9,8},{10,11... | collective-permute-start | bytes 3932168 | tf_op jit(solution)/shard_map/ppermute | solution.py:23
  77.9 3.2 %copy-start.3 = (bf16[1,512,1280]{2,1,0:T(8,128)(2,1)}, bf16[1,512,1280]{2,1,0:T(8,128)(2,1)S(1)}, u32[]{:S(2)}) copy-start(bf16[1,512,1280]{2,1,0:T(8,128)(2,1)S(1)} %collective-permute-done.5) | copy-start | bytes 3932164
  80.3 0.8 copy-start.7
  96.1 3.3 %collective-permute-start.6 = (bf16[1,512,1280]{2,1,0:T(8,128)(2,1)}, bf16[1,512,1280]{2,1,0:T(8,128)(2,1)S(1)}, u32[]{:S(2)}, u32[]{:S(2)}) collective-permute-start(bf16[1,512,1280]{2,1,0:T(8,128)(2,1)} %bitcast.38), channel_id=1, source_target_pairs={{0,1},{1,0},{2,3},{3,2},{4,5},{5,4},{6,7},{7,6},{8,9},{9,8},{10,11... | collective-permute-start | bytes 3932168 | tf_op jit(solution)/shard_map/ppermute | solution.py:196

commit v11 on v10

--- a/solution.py
+++ b/solution.py
@@ -44,7 +44,7 @@
         o_ref[...] = acc_ref[...].astype(o_ref.dtype)
 
 
-def feed_forward(x, expand, contract, hidden_step=640, rows_per_step=512):
+def feed_forward(x, expand, contract, hidden_step=256, rows_per_step=512):
     length, width = x.shape
     hidden = expand.shape[1]
     return pl.pallas_call(

time: 105 us -> 115 us (1.095)
  Pallas kernels: 57.8 us -> 68.1 us
    pallas_call x2, Pallas kernels: 26.2 us -> 36.6 us  [feed_forward(): pl.pallas_call(functools.partial(_feed_forward_kernel, rows_per_step), ou...]
where the time goes in v11:
time: 115 us; the launch traced here: 114 us
  Pallas kernels  68.1 us (59%)
  other arithmetic  16.3 us (14%)
  starting transfers between devices  11.9 us (10%)
  waiting for transfers between devices  11.2 us (10%)
  local copies, waits for them, and re-layouts  3.84 us (3%)
  between operations  2.11 us (2%)
    pallas_call x2, Pallas kernels, feed_forward(): pl.pallas_call(functools.partial(_feed_forward_kernel, rows_per_step), ou...  36.6 us
    pallas_call x2, Pallas kernels, attend(): pl.pallas_call(functools.partial(_attention_kernel, causal), out_shape=ja...  24.3 us
    pallas_call x1, Pallas kernels, merge(): pl.pallas_call(_merge_kernel, out_shape=jax.ShapeDtypeStruct((images, hal...  7.28 us
    ppermute x2, starting transfers between devices, on_device(): sent.append(lax.ppermute(own_image, ('req', 'tensor'), perm))  6.95 us
    ppermute x2, waiting for transfers between devices, tensor_sum(): other = lax.ppermute(mine, 'tensor', [(0, 1), (1, 0)])  5.74 us
    reduce_sum x2, other arithmetic, normalize(): center = values - jnp.mean(values, axis=-1, keepdims=True)  4.31 us
    select_n x1, other arithmetic, on_device(): jnp.where(prompt_valid[None, :, None], decoded, jnp.zeros_like(decoded))  3.82 us
    ppermute x2, starting transfers between devices, tensor_sum(): other = lax.ppermute(mine, 'tensor', [(0, 1), (1, 0)])  3.74 us
  transfers between devices with their start and end apart: 7, of which 6 were waited for; matrix products, arithmetic and copies ran while one was open for 2% of the time, Pallas kernels for 0%

profile of v11, /device:TPU:1, one launch (start us, length us, event | category | flops | bytes accessed | tf_op | source)
XLA Modules:
  0.0 113.6 jit_solution(3059072956669708937)
XLA Ops:
  0.0 0.7 constant_dynamic-slice_fusion
  0.8 0.7 and_convert_fusion.valid_ref
  1.4 0.0 copy-start.5
  1.4 11.6 %shard_map.163 = bf16[2,256,1280]{2,1,0:T(8,128)(2,1)} custom-call(bf16[2,256,1280]{2,1,0:T(8,128)(2,1)} %x_ref.1, f32[1280]{0:T(1024)} %gain_ref.2, bf16[3,1280,640]{2,1,0:T(8,128)(2,1)} %bitcast.40, s32[2,1,256]{2,1,0:T(1,128)} %and_convert_fusion.valid_ref, bf16[640,1280]{1,0:T(8,128)(2,1)} %wo_ref.2), custom_call_target="tpu_custom_call" | custom-call | flops 4429185024 | bytes 9175040 | tf_op jit(solution)/shard_map/pallas_call | solution.py:159
  13.0 3.2 %collective-permute-start = (bf16[2,256,1280]{2,1,0:T(8,128)(2,1)}, bf16[2,256,1280]{2,1,0:T(8,128)(2,1)S(1)}, u32[]{:S(2)}, u32[]{:S(2)}) collective-permute-start(bf16[2,256,1280]{2,1,0:T(8,128)(2,1)} %shard_map.163), channel_id=1, source_target_pairs={{0,1},{1,0},{2,3},{3,2},{4,5},{5,4},{6,7},{7,6},{8,9},{9,8},{10,11... | collective-permute-start | bytes 3932168 | tf_op jit(solution)/shard_map/ppermute | solution.py:23
  16.3 2.9 %collective-permute-done = bf16[2,256,1280]{2,1,0:T(8,128)(2,1)S(1)} collective-permute-done((bf16[2,256,1280]{2,1,0:T(8,128)(2,1)}, bf16[2,256,1280]{2,1,0:T(8,128)(2,1)S(1)}, u32[]{:S(2)}, u32[]{:S(2)}) %collective-permute-start) | collective-permute-done | bytes 1310752 | tf_op jit(solution)/shard_map/ppermute | solution.py:23
  19.1 0.0 copy-done.5
  19.1 1.9 %fusion.7 = (f32[2,256]{1,0:T(2,128)S(1)}, f32[2,256,1280]{2,1,0:T(8,128)S(1)}) fusion(bf16[2,256,1280]{2,1,0:T(8,128)(2,1)S(1)} %collective-permute-done, bf16[2,256,1280]{2,1,0:T(8,128)(2,1)} %shard_map.163, bf16[2,256,1280]{2,1,0:T(8,128)(2,1)S(1)} %copy-done.5), kind=kLoop, calls=%fused_computation.47 | loop fusion | flops 3931648 | bytes 6555648 | tf_op jit(solution)/shard_map/reduce_sum | solution.py:16
  21.0 0.0 copy-start
  21.0 0.0 copy-start.6
  21.1 0.4 multiply_reduce_fusion.1
  21.5 0.3 copy-done.6
  21.8 1.5 %multiply_convert_fusion.1 = bf16[2,256,1280]{2,1,0:T(8,128)(2,1)} fusion(f32[2,256,1280]{2,1,0:T(8,128)S(1)} %get-tuple-element.6.res_ref, f32[1280]{0:T(1024)S(1)} %copy-done.6, f32[2,256]{1,0:T(2,128)S(1)} %add_rsqrt_fusion.1, f32[2,256]{1,0:T(2,128)S(1)} %broadcast_multiply_fusion.1), kind=kLoop, calls=%fused_computation.4 | loop fusion | flops 2621440 | bytes 3941376 | tf_op jit(solution)/shard_map/convert_element_type | solution.py:192
  23.2 0.0 copy-done
  23.2 0.0 copy-start.9
  23.2 0.0 copy-start.8
  23.2 18.3 %shard_map.164 = bf16[512,1280]{1,0:T(8,128)(2,1)} custom-call(bf16[512,1280]{1,0:T(8,128)(2,1)} %bitcast.37, bf16[1280,2560]{1,0:T(8,128)(2,1)} %w1_ref.2, bf16[2560,1280]{1,0:T(8,128)(2,1)} %w2_ref.2), custom_call_target="tpu_custom_call" | custom-call | flops 6710886400 | bytes 15728640 | tf_op jit(solution)/shard_map/pallas_call | solution.py:50
  41.5 0.4 collective-permute-start.1
  41.9 0.0 copy-done.9
  41.9 0.6 dynamic_slice.12
  44.5 0.0 copy-done.8
  44.5 0.1 constant_dynamic-slice_fusion.2
  44.6 0.1 add_select_fusion
  44.7 0.1 collective-permute-done.1.other_ref
  44.8 0.0 copy-start.4
  44.8 1.1 copy-done.4
  45.8 7.3 %shard_map.165 = bf16[2,64,640]{2,1,0:T(8,128)(2,1)} custom-call(f32[2,256,1280]{2,1,0:T(8,128)} %copy-done, bf16[2,256,1280]{2,1,0:T(8,128)(2,1)} %bitcast.36, bf16[2,256,1280]{2,1,0:T(8,128)(2,1)} %copy-done.4, bf16[5120,640]{1,0:T(8,128)(2,1)} %w_ref.1), custom_call_target="tpu_custom_call" | custom-call | flops 922746880 | bytes 11796480 | tf_op jit(solution)/shard_map/pallas_call | solution.py:106
  53.1 0.0 copy-start.1
  53.1 1.0 broadcast_select_fusion.2
  54.1 0.5 collective-permute-start.2
  54.6 0.9 slice_bitcast_fusion
  55.6 0.0 collective-permute-done.2
  55.6 5.3 %collective-permute-start.4 = (bf16[64,1280]{1,0:T(8,128)(2,1)S(1)}, bf16[64,1280]{1,0:T(8,128)(2,1)S(1)}, u32[]{:S(2)}, u32[]{:S(2)}) collective-permute-start(bf16[64,1280]{1,0:T(8,128)(2,1)S(1)} %maximum_select_fusion.1), channel_id=1, source_target_pairs={{0,2},{1,129},{2,0},{3,131},{4,6},{5,133},{6,4},{7,135},{8,10},{9,... | collective-permute-start | bytes 491528 | tf_op jit(solution)/shard_map/ppermute | solution.py:261
  60.9 1.7 %collective-permute-start.3 = (bf16[64,1280]{1,0:T(8,128)(2,1)S(1)}, bf16[64,1280]{1,0:T(8,128)(2,1)S(1)}, u32[]{:S(2)}, u32[]{:S(2)}) collective-permute-start(bf16[64,1280]{1,0:T(8,128)(2,1)S(1)} %maximum_select_fusion.1), channel_id=1, source_target_pairs={{0,3},{1,128},{2,1},{3,130},{4,7},{5,132},{6,5},{7,134},{8,11},{9,... | collective-permute-start | bytes 491528 | tf_op jit(solution)/shard_map/ppermute | solution.py:261
  62.6 0.1 compare_and_fusion
  62.6 0.1 and.78
  62.7 0.6 fusion.8
  63.3 0.6 collective-permute-done.4
  63.9 1.9 %collective-permute-done.3 = bf16[64,1280]{1,0:T(8,128)(2,1)S(1)} collective-permute-done((bf16[64,1280]{1,0:T(8,128)(2,1)S(1)}, bf16[64,1280]{1,0:T(8,128)(2,1)S(1)}, u32[]{:S(2)}, u32[]{:S(2)}) %collective-permute-start.3) | collective-permute-done | bytes 163872 | tf_op jit(solution)/shard_map/ppermute | solution.py:261
  65.9 0.1 maximum_select_fusion
  65.9 0.0 copy-done.1
  65.9 1.1 %maximum_bitcast_fusion.x_ref = bf16[1,512,1280]{2,1,0:T(8,128)(2,1)} fusion(bf16[384,1280]{1,0:T(8,128)(2,1)S(1)} %bitcast.30, bf16[128,1280]{1,0:T(8,128)(2,1)S(1)} %maximum_select_fusion), kind=kLoop, calls=%fused_computation.9 | loop fusion | flops 2621440 | bytes 2621440 | tf_op jit(solution)/shard_map/broadcast_in_dim | solution.py:281
  67.1 12.7 %shard_map.166 = bf16[1,512,1280]{2,1,0:T(8,128)(2,1)} custom-call(bf16[1,512,1280]{2,1,0:T(8,128)(2,1)} %maximum_bitcast_fusion.x_ref, f32[1280]{0:T(1024)} %gain_ref.3, bf16[3,1280,640]{2,1,0:T(8,128)(2,1)} %bitcast.41, s32[1,1,512]{2,1,0:T(1,128)} %bitcast.39, bf16[640,1280]{1,0:T(8,128)(2,1)} %wo_ref.3), custom_call_target="tpu_custom_call" | custom-call | flops 5502926848 | bytes 9175040 | tf_op jit(solution)/shard_map/pallas_call | solution.py:159
  79.7 0.0 copy-start.2
  79.8 0.5 collective-permute-start.5
  80.3 2.9 %collective-permute-done.5 = bf16[1,512,1280]{2,1,0:T(8,128)(2,1)S(1)} collective-permute-done((bf16[1,512,1280]{2,1,0:T(8,128)(2,1)}, bf16[1,512,1280]{2,1,0:T(8,128)(2,1)S(1)}, u32[]{:S(2)}, u32[]{:S(2)}) %collective-permute-start.5) | collective-permute-done | bytes 1310752 | tf_op jit(solution)/shard_map/ppermute | solution.py:23
  83.1 0.0 copy-start.3
  83.1 2.4 %fusion.6 = f32[512]{0:T(512)S(1)} fusion(bf16[1,512,1280]{2,1,0:T(8,128)(2,1)S(1)} %collective-permute-done.5, bf16[1,512,1280]{2,1,0:T(8,128)(2,1)} %shard_map.166, bf16[1,384,1280]{2,1,0:T(8,128)(2,1)S(1)} %copy-done.1, bf16[1,128,1280]{2,1,0:T(8,128)(2,1)S(1)} %bitcast.31), kind=kLoop, calls=%fused_computation.46 | loop fusion | flops 5897728 | bytes 3934208 | tf_op jit(solution)/shard_map/reduce_sum | solution.py:16
  85.5 0.0 copy-start.7
  85.5 0.0 copy-done.2
  85.6 0.8 multiply_reduce_fusion
  86.3 0.0 copy-done.3
  86.4 0.0 copy-done.7
  86.4 1.8 %fusion.x_ref = bf16[512,1280]{1,0:T(8,128)(2,1)} fusion(f32[1280]{0:T(1024)S(1)} %copy-done.7, f32[512]{0:T(512)S(1)} %add_rsqrt_fusion, f32[512]{0:T(512)S(1)} %broadcast_multiply_fusion, bf16[1,512,1280]{2,1,0:T(8,128)(2,1)S(1)} %collective-permute-done.5, bf16[1,512,1280]{2,1,0:T(8,128)(2,1)S(1)} %copy-done.2, bf16[1,384,1280]{2,1,0:T(8,128)(2,1)S(1)} %copy-done.1, ...), kind=kLoop, calls=%fused_computation.7 | loop fusion | flops 7864320 | bytes 5252096 | tf_op jit(solution)/shard_map/reshape | solution.py:194
  88.2 18.3 %shard_map.167 = bf16[512,1280]{1,0:T(8,128)(2,1)} custom-call(bf16[512,1280]{1,0:T(8,128)(2,1)} %fusion.x_ref, bf16[1280,2560]{1,0:T(8,128)(2,1)} %w1_ref.3, bf16[2560,1280]{1,0:T(8,128)(2,1)} %w2_ref.3), custom_call_target="tpu_custom_call" | custom-call | flops 6710886400 | bytes 15728640 | tf_op jit(solution)/shard_map/pallas_call | solution.py:50
  106.5 0.4 collective-permute-start.6
  106.9 2.9 %collective-permute-done.6 = bf16[1,512,1280]{2,1,0:T(8,128)(2,1)S(1)} collective-permute-done((bf16[1,512,1280]{2,1,0:T(8,128)(2,1)}, bf16[1,512,1280]{2,1,0:T(8,128)(2,1)S(1)}, u32[]{:S(2)}, u32[]{:S(2)}) %collective-permute-start.6) | collective-permute-done | bytes 1310752 | tf_op jit(solution)/shard_map/ppermute | solution.py:196
  109.7 3.8 %fusion.1 = bf16[1,512,1280]{2,1,0:T(8,128)(2,1)} fusion(bf16[1,512,1280]{2,1,0:T(8,128)(2,1)S(1)} %collective-permute-done.6, pred[512]{0:T(512)(128)(4,1)S(1)} %get-tuple-element.17, bf16[512,1280]{1,0:T(8,128)(2,1)} %shard_map.167, bf16[1,512,1280]{2,1,0:T(8,128)(2,1)} %copy-done.3, bf16[1,512,1280]{2,1,0:T(8,128)(2,1)S(1)} %copy-done.2, ...), kind=kLoop, calls=%fused_computation.8 | loop fusion | flops 9175040 | bytes 7864832 | tf_op jit(solution)/shard_map/jit(_where)/select_n | solution.py:297
  (10 shorter events, 0.1 us)
Async XLA Ops:
  1.4 17.7 %copy-start.5 = (bf16[2,256,1280]{2,1,0:T(8,128)(2,1)S(1)}, bf16[2,256,1280]{2,1,0:T(8,128)(2,1)}, u32[]{:S(2)}) copy-start(bf16[2,256,1280]{2,1,0:T(8,128)(2,1)} %x_ref.1) | copy-start | bytes 3932164
  13.0 6.1 %collective-permute-start = (bf16[2,256,1280]{2,1,0:T(8,128)(2,1)}, bf16[2,256,1280]{2,1,0:T(8,128)(2,1)S(1)}, u32[]{:S(2)}, u32[]{:S(2)}) collective-permute-start(bf16[2,256,1280]{2,1,0:T(8,128)(2,1)} %shard_map.163), channel_id=1, source_target_pairs={{0,1},{1,0},{2,3},{3,2},{4,5},{5,4},{6,7},{7,6},{8,9},{9,8},{10,11... | collective-permute-start | bytes 3932168 | tf_op jit(solution)/shard_map/ppermute | solution.py:23
  21.0 2.2 %copy-start = (f32[2,256,1280]{2,1,0:T(8,128)}, f32[2,256,1280]{2,1,0:T(8,128)S(1)}, u32[]{:S(2)}) copy-start(f32[2,256,1280]{2,1,0:T(8,128)S(1)} %get-tuple-element.6.res_ref) | copy-start | bytes 7864324
  21.0 0.7 copy-start.6
  23.2 18.7 %copy-start.9 = (s32[256]{0:T(256)S(1)}, s32[256]{0:T(256)}, u32[]{:S(2)}) copy-start(s32[256]{0:T(256)} %param.19) | copy-start | bytes 3076
  23.2 21.2 %copy-start.8 = (s32[256,2]{0,1:T(2,128)S(1)}, s32[256,2]{0,1:T(2,128)}, u32[]{:S(2)}) copy-start(s32[256,2]{0,1:T(2,128)} %param.18) | copy-start | bytes 6148
  41.5 3.2 %collective-permute-start.1 = (bf16[2,256,1280]{2,1,0:T(8,128)(2,1)}, bf16[2,256,1280]{2,1,0:T(8,128)(2,1)S(1)}, u32[]{:S(2)}, u32[]{:S(2)}) collective-permute-start(bf16[2,256,1280]{2,1,0:T(8,128)(2,1)} %bitcast.35), channel_id=1, source_target_pairs={{0,1},{1,0},{2,3},{3,2},{4,5},{5,4},{6,7},{7,6},{8,9},{9,8},{10,11... | collective-permute-start | bytes 3932168 | tf_op jit(solution)/shard_map/ppermute | solution.py:196
  44.8 1.1 copy-start.4
  53.1 12.8 %copy-start.1 = (bf16[1,384,1280]{2,1,0:T(8,128)(2,1)S(1)}, bf16[1,384,1280]{2,1,0:T(8,128)(2,1)}, u32[]{:S(2)}) copy-start(bf16[1,384,1280]{2,1,0:T(8,128)(2,1)} %param.20) | copy-start | bytes 2949124
  54.1 1.4 %collective-permute-start.2 = (bf16[64,640]{1,0:T(8,128)(2,1)S(1)}, bf16[64,640]{1,0:T(8,128)(2,1)S(1)}, u32[]{:S(2)}, u32[]{:S(2)}) collective-permute-start(bf16[64,640]{1,0:T(8,128)(2,1)S(1)} %broadcast_select_fusion.2), channel_id=1, source_target_pairs={{0,1},{1,0},{2,3},{3,2},{4,5},{5,4},{6,7},{7,6},{8,9},{9,8},{10,11... | collective-permute-start | bytes 245768 | tf_op jit(solution)/shard_map/ppermute | solution.py:248
  55.6 8.3 %collective-permute-start.4 = (bf16[64,1280]{1,0:T(8,128)(2,1)S(1)}, bf16[64,1280]{1,0:T(8,128)(2,1)S(1)}, u32[]{:S(2)}, u32[]{:S(2)}) collective-permute-start(bf16[64,1280]{1,0:T(8,128)(2,1)S(1)} %maximum_select_fusion.1), channel_id=1, source_target_pairs={{0,2},{1,129},{2,0},{3,131},{4,6},{5,133},{6,4},{7,135},{8,10},{9,... | collective-permute-start | bytes 491528 | tf_op jit(solution)/shard_map/ppermute | solution.py:261
  60.9 5.0 %collective-permute-start.3 = (bf16[64,1280]{1,0:T(8,128)(2,1)S(1)}, bf16[64,1280]{1,0:T(8,128)(2,1)S(1)}, u32[]{:S(2)}, u32[]{:S(2)}) collective-permute-start(bf16[64,1280]{1,0:T(8,128)(2,1)S(1)} %maximum_select_fusion.1), channel_id=1, source_target_pairs={{0,3},{1,128},{2,1},{3,130},{4,7},{5,132},{6,5},{7,134},{8,11},{9,... | collective-permute-start | bytes 491528 | tf_op jit(solution)/shard_map/ppermute | solution.py:261
  79.7 5.8 %copy-start.2 = (bf16[1,512,1280]{2,1,0:T(8,128)(2,1)S(1)}, bf16[1,512,1280]{2,1,0:T(8,128)(2,1)}, u32[]{:S(2)}) copy-start(bf16[1,512,1280]{2,1,0:T(8,128)(2,1)} %shard_map.166) | copy-start | bytes 3932164
  79.8 3.4 %collective-permute-start.5 = (bf16[1,512,1280]{2,1,0:T(8,128)(2,1)}, bf16[1,512,1280]{2,1,0:T(8,128)(2,1)S(1)}, u32[]{:S(2)}, u32[]{:S(2)}) collective-permute-start(bf16[1,512,1280]{2,1,0:T(8,128)(2,1)} %shard_map.166), channel_id=1, source_target_pairs={{0,1},{1,0},{2,3},{3,2},{4,5},{5,4},{6,7},{7,6},{8,9},{9,8},{10,11... | collective-permute-start | bytes 3932168 | tf_op jit(solution)/shard_map/ppermute | solution.py:23
  83.1 3.2 %copy-start.3 = (bf16[1,512,1280]{2,1,0:T(8,128)(2,1)}, bf16[1,512,1280]{2,1,0:T(8,128)(2,1)S(1)}, u32[]{:S(2)}) copy-start(bf16[1,512,1280]{2,1,0:T(8,128)(2,1)S(1)} %collective-permute-done.5) | copy-start | bytes 3932164
  85.5 0.8 copy-start.7
  106.5 3.2 %collective-permute-start.6 = (bf16[1,512,1280]{2,1,0:T(8,128)(2,1)}, bf16[1,512,1280]{2,1,0:T(8,128)(2,1)S(1)}, u32[]{:S(2)}, u32[]{:S(2)}) collective-permute-start(bf16[1,512,1280]{2,1,0:T(8,128)(2,1)} %bitcast.38), channel_id=1, source_target_pairs={{0,1},{1,0},{2,3},{3,2},{4,5},{5,4},{6,7},{7,6},{8,9},{9,8},{10,11... | collective-permute-start | bytes 3932168 | tf_op jit(solution)/shard_map/ppermute | solution.py:196
